TPU v7x, 512 devices: a whole 4x4x16 slice. The times are simulated.
512 devices in a mesh: line: 32 (over z, core), scan: 16 (over x, y).
Axes of the slice: x: 4, y: 4, z: 16, core: 2. Of those that a mesh axis runs over, the one named last changes fastest.
Arguments:
- query_row: bfloat16 [32, 2048, 512], P('line', 'scan'), may hold values from -6 to 6
- key_row: bfloat16 [32, 2048, 512], P('line', 'scan'), may hold values from -6 to 6
- value_row: bfloat16 [32, 2048, 512], P('line', 'scan'), may hold values from -6 to 6
- decay_row: float32 [32, 2048, 4], P('line', 'scan'), may hold values from -2 to 0
- beta_row: float32 [32, 2048, 4], P('line', 'scan'), may hold values from 0.02 to 0.2
- gain_row: float32 [128], replicated, may hold values from 0.1 to 1.9
- query_col: bfloat16 [32, 16, 128, 512], P(None, 'scan', 'line'), may hold values from -6 to 6
- key_col: bfloat16 [32, 16, 128, 512], P(None, 'scan', 'line'), may hold values from -6 to 6
- decay_col: float32 [32, 16, 128, 4], P(None, 'scan', 'line'), may hold values from -2 to 0
- beta_col: float32 [32, 16, 128, 4], P(None, 'scan', 'line'), may hold values from 0.02 to 0.2
- gain_col: float32 [128], replicated, may hold values from 0.1 to 1.9
Outputs:
- mixed: bfloat16 [32, 2048, 512], P('line', 'scan')
All inputs are finite; a program needn't handle non-finite values.
Results may differ from a plain program's by a relative error of at most 0.0049.
Values may be sent and summed in bfloat16 or wider, within the bound.
No kernel may reach another device: no remote copies, remote signals or barrier semaphores. Data moves between devices by JAX's collectives and lax.ppermute only.
A program may use at most 64 MiB of HBM per device.

v0:
```python
import jax
import jax.numpy as jnp
from jax import lax
from jax.sharding import PartitionSpec as P

HIGHEST = lax.Precision.HIGHEST


def from_behind(block, axis, distance):
    devices = range(lax.axis_size(axis))
    route = [(i - distance, i) for i in devices if i - distance in devices]
    return lax.ppermute(block, axis, route)


def block_terms(query_block, key_block, value_block, log_decay, beta_block):
    key_unit = key_block / jnp.sqrt(jnp.sum(key_block * key_block, axis=-1, keepdims=True) + 1e-06)
    cumulative = jnp.cumsum(log_decay, axis=-1)
    sequence_length = key_block.shape[1]
    lower_mask = jnp.tril(jnp.ones((sequence_length, sequence_length), dtype=jnp.bool_))
    strict = jnp.tril(jnp.ones((sequence_length, sequence_length), dtype=jnp.bool_), -1)
    spread = cumulative[:, :, None] - cumulative[:, None, :]
    ratios = jnp.where(lower_mask, jnp.exp(jnp.where(lower_mask, spread, 0.0)), 0.0)
    key_inner = jnp.einsum("bik,bjk->bij", key_unit, key_unit, precision=HIGHEST)
    system = jnp.where(strict, beta_block[:, :, None] * ratios * key_inner, 0.0) + jnp.eye(
        sequence_length, dtype=jnp.float32
    )
    growth = jnp.exp(cumulative)
    right_side = jnp.concatenate(
        [beta_block[:, :, None] * value_block, (beta_block * growth)[:, :, None] * key_unit],
        axis=-1,
    )
    solved = jax.scipy.linalg.solve_triangular(system, right_side, lower=True)
    value_size = value_block.shape[-1]
    updates = solved[:, :, :value_size]
    weighted = solved[:, :, value_size:]
    attend = ratios * jnp.einsum("bik,bjk->bij", query_block, key_unit, precision=HIGHEST)
    local_out = jnp.einsum("bij,bjv->biv", attend, updates, precision=HIGHEST)
    state_query = growth[:, :, None] * query_block - jnp.einsum(
        "bij,bjk->bik", attend, weighted, precision=HIGHEST
    )
    key_tail = jnp.exp(cumulative[:, -1:] - cumulative)[:, :, None] * key_unit
    return (local_out, state_query, key_tail, weighted, updates, growth[:, -1])


def scan_blocks(queries, key_rows, values, log_decay, beta_rows, block_extent):
    batch_size, sequence_length, head_size = queries.shape
    number_of_blocks = sequence_length // block_extent

    def blocks(array):
        return array.reshape(
            (batch_size, number_of_blocks, block_extent) + array.shape[2:]
        ).swapaxes(0, 1)

    def scan_advance(carried, pieces):
        local_out, state_query, key_tail, weighted, updates, ending = block_terms(*pieces)
        output = local_out + jnp.einsum("bik,bkv->biv", state_query, carried, precision=HIGHEST)
        residue = updates - jnp.einsum("bjk,bkv->bjv", weighted, carried, precision=HIGHEST)
        carried = ending[:, None, None] * carried + jnp.einsum(
            "bjk,bjv->bkv", key_tail, residue, precision=HIGHEST
        )
        return (carried, output)

    initial = jnp.zeros((batch_size, head_size, head_size), dtype=jnp.float32)
    last_state, outputs = lax.scan(
        scan_advance,
        initial,
        (blocks(queries), blocks(key_rows), blocks(values), blocks(log_decay), blocks(beta_rows)),
    )
    return outputs.swapaxes(0, 1).reshape(batch_size, sequence_length, head_size)


def to_heads(array, leading_count, sequence_length, head_count, head_size):
    shaped = array.astype(jnp.float32).reshape(
        leading_count, sequence_length, head_count, head_size
    )
    return shaped.transpose(0, 2, 1, 3).reshape(
        leading_count * head_count, sequence_length, head_size
    )


def gates_to_heads(array, leading_count, sequence_length, head_count):
    return array.transpose(0, 2, 1).reshape(leading_count * head_count, sequence_length)


def from_heads(array, leading_count, sequence_length, head_count, head_size):
    return array.reshape(leading_count, head_count, sequence_length, head_size).transpose(
        0, 2, 1, 3
    )


def head_norm(array, gain):
    return array * lax.rsqrt(jnp.mean(array * array, axis=-1, keepdims=True) + 1e-05) * gain


def shards(
    query_row,
    key_row,
    value_row,
    decay_row,
    beta_row,
    gain_row,
    query_col,
    key_col,
    decay_col,
    beta_col,
    gain_col,
):
    row_count, segment, features = query_row.shape
    head_size = gain_row.shape[0]
    head_count = features // head_size
    line_count = lax.axis_size("line")
    local_out, state_query, key_tail, weighted, updates, ending = block_terms(
        to_heads(query_row, row_count, segment, head_count, head_size),
        to_heads(key_row, row_count, segment, head_count, head_size),
        to_heads(value_row, row_count, segment, head_count, head_size),
        gates_to_heads(decay_row, row_count, segment, head_count),
        gates_to_heads(beta_row, row_count, segment, head_count),
    )
    identity = jnp.broadcast_to(
        jnp.eye(head_size, dtype=jnp.float32), (row_count * head_count, head_size, head_size)
    )
    transfer = ending[:, None, None] * identity - jnp.einsum(
        "bjk,bjl->bkl", key_tail, weighted, precision=HIGHEST
    )
    offset = jnp.einsum("bjk,bjv->bkv", key_tail, updates, precision=HIGHEST)

    def body_advance(number, carried):
        arrived = from_behind(carried[1], "scan", 1)
        return (arrived, jnp.einsum("bij,bjv->biv", transfer, arrived, precision=HIGHEST) + offset)

    incoming, leaving = lax.fori_loop(
        0, lax.axis_size("scan") - 1, body_advance, (jnp.zeros_like(offset), offset)
    )
    row_out = local_out + jnp.einsum("bik,bkv->biv", state_query, incoming, precision=HIGHEST)
    row_scan = from_heads(row_out, row_count, segment, head_count, head_size)
    values_col = (
        head_norm(row_scan, gain_row).reshape(row_count, segment, features).astype(jnp.bfloat16)
    )
    arranged = values_col.reshape(row_count, line_count, segment // line_count, features)
    column_values = lax.all_to_all(arranged, "line", split_axis=1, concat_axis=0, tiled=True)
    total_rows = query_col.shape[0]
    column_count = query_col.shape[2]

    def columns(array):
        return array.reshape(total_rows, column_count, -1).transpose(1, 0, 2)

    block_extent = min(segment, total_rows)
    col_out = scan_blocks(
        to_heads(columns(query_col), column_count, total_rows, head_count, head_size),
        to_heads(columns(key_col), column_count, total_rows, head_count, head_size),
        to_heads(columns(column_values), column_count, total_rows, head_count, head_size),
        gates_to_heads(columns(decay_col), column_count, total_rows, head_count),
        gates_to_heads(columns(beta_col), column_count, total_rows, head_count),
        block_extent,
    )
    col_scan = from_heads(col_out, column_count, total_rows, head_count, head_size)
    normed = (
        head_norm(col_scan, gain_col)
        .transpose(1, 0, 2, 3)
        .reshape(total_rows, 1, column_count, features)
        .astype(jnp.bfloat16)
    )
    returned = lax.all_to_all(normed, "line", split_axis=0, concat_axis=1, tiled=True)
    return returned.reshape(row_count, segment, features)


def solution(mesh):
    placed = (
        P("line", "scan", None),
        P("line", "scan", None),
        P("line", "scan", None),
        P("line", "scan", None),
        P("line", "scan", None),
        P(),
        P(None, "scan", "line", None),
        P(None, "scan", "line", None),
        P(None, "scan", "line", None),
        P(None, "scan", "line", None),
        P(),
    )
    return jax.shard_map(
        shards, mesh=mesh, in_specs=placed, out_specs=P("line", "scan", None), check_vma=False
    )
```

profile of v0, /device:TPU:6, one launch (start us, length us, event | category | flops | bytes accessed | tf_op | source)
XLA Modules:
  0.0 320.1 jit_solution(1255475368791941096)
XLA Ops:
  0.0 0.9 fusion.47
  1.0 0.9 copy-done.2
  2.1 0.7 copy-done.3
  2.9 0.7 copy-done.9
  4.1 0.6 copy-done.7
  4.8 0.8 fusion.8
  5.6 39.3 %custom-call.10 = f32[4,1,128,128]{2,3,1,0:T(8,128)S(1)} custom-call(f32[4,1,128,128]{3,2,1,0:T(8,128)S(1)} %fusion.8), custom_call_target="InvertDiagBlocksLowerTriangular" | custom-call | tf_op jit(solution)/shard_map/jit(_solve_triangular)/vmap()/triangular_solve | solution.py:32
  45.4 0.6 fusion.9
  46.0 0.7 fusion.28
  46.8 0.7 convolution_subtract_fusion.1
  47.6 0.5 convolution_multiply_fusion.1
  48.0 0.6 fusion.30
  48.7 0.4 convolution_subtract_fusion.2
  49.1 176.1 %while.3 = (s32[]{:T(128)}, f32[4,128,128]{2,1,0:T(8,128)}, f32[4,128,128]{2,1,0:T(8,128)S(1)}, f32[4,128,128]{2,1,0:T(8,128)S(1)}, f32[4,128,128]{2,1,0:T(8,128)S(1)}) while((s32[]{:T(128)}, f32[4,128,128]{2,1,0:T(8,128)}, f32[4,128,128]{2,1,0:T(8,128)S(1)}, f32[4,128,128]{2,1,0:T(8,128)S(1)}, f32[4,128,128]{2,1,0:T(8,128)S(1)}) %tuple.54), condition=%wide.region_5.6_spmd.clone, body=%wide.region_4.5_spmd.sunk.clone | while | flops 100728832 | bytes 3145857 | solution.py:131
  49.1 3.5 %collective-permute-start = (f32[4,128,128]{2,1,0:T(8,128)S(1)}, f32[4,128,128]{2,1,0:T(8,128)S(1)}, u32[]{:S(2)}, u32[]{:S(2)}) collective-permute-start(f32[4,128,128]{2,1,0:T(8,128)S(1)} %get-tuple-element.160), channel_id=1, source_target_pairs={{0,1},{1,2},{2,3},{3,4},{4,5},{5,6},{6,7},{7,8},{8,9},{9,10},{10,1... | collective-permute-start | bytes 786440 | tf_op jit(solution)/shard_map/while/body/eval_jaxpr/ppermute | solution.py:12
  52.6 8.6 %collective-permute-done = f32[4,128,128]{2,1,0:T(8,128)S(1)} collective-permute-done((f32[4,128,128]{2,1,0:T(8,128)S(1)}, f32[4,128,128]{2,1,0:T(8,128)S(1)}, u32[]{:S(2)}, u32[]{:S(2)}) %collective-permute-start) | collective-permute-done | bytes 262176 | tf_op jit(solution)/shard_map/while/body/eval_jaxpr/ppermute | solution.py:12
  61.1 0.4 convolution_add_fusion.5
  61.8 1.9 collective-permute-start
  63.7 9.2 %collective-permute-done = f32[4,128,128]{2,1,0:T(8,128)S(1)} collective-permute-done((f32[4,128,128]{2,1,0:T(8,128)S(1)}, f32[4,128,128]{2,1,0:T(8,128)S(1)}, u32[]{:S(2)}, u32[]{:S(2)}) %collective-permute-start) | collective-permute-done | bytes 262176 | tf_op jit(solution)/shard_map/while/body/eval_jaxpr/ppermute | solution.py:12
  73.7 1.9 collective-permute-start
  75.6 8.4 %collective-permute-done = f32[4,128,128]{2,1,0:T(8,128)S(1)} collective-permute-done((f32[4,128,128]{2,1,0:T(8,128)S(1)}, f32[4,128,128]{2,1,0:T(8,128)S(1)}, u32[]{:S(2)}, u32[]{:S(2)}) %collective-permute-start) | collective-permute-done | bytes 262176 | tf_op jit(solution)/shard_map/while/body/eval_jaxpr/ppermute | solution.py:12
  84.7 1.9 collective-permute-start
  86.7 8.4 %collective-permute-done = f32[4,128,128]{2,1,0:T(8,128)S(1)} collective-permute-done((f32[4,128,128]{2,1,0:T(8,128)S(1)}, f32[4,128,128]{2,1,0:T(8,128)S(1)}, u32[]{:S(2)}, u32[]{:S(2)}) %collective-permute-start) | collective-permute-done | bytes 262176 | tf_op jit(solution)/shard_map/while/body/eval_jaxpr/ppermute | solution.py:12
  95.8 1.9 collective-permute-start
  97.7 8.4 %collective-permute-done = f32[4,128,128]{2,1,0:T(8,128)S(1)} collective-permute-done((f32[4,128,128]{2,1,0:T(8,128)S(1)}, f32[4,128,128]{2,1,0:T(8,128)S(1)}, u32[]{:S(2)}, u32[]{:S(2)}) %collective-permute-start) | collective-permute-done | bytes 262176 | tf_op jit(solution)/shard_map/while/body/eval_jaxpr/ppermute | solution.py:12
  106.2 0.4 convolution_add_fusion.5
  106.9 1.9 collective-permute-start
  108.8 8.4 %collective-permute-done = f32[4,128,128]{2,1,0:T(8,128)S(1)} collective-permute-done((f32[4,128,128]{2,1,0:T(8,128)S(1)}, f32[4,128,128]{2,1,0:T(8,128)S(1)}, u32[]{:S(2)}, u32[]{:S(2)}) %collective-permute-start) | collective-permute-done | bytes 262176 | tf_op jit(solution)/shard_map/while/body/eval_jaxpr/ppermute | solution.py:12
  117.2 0.4 convolution_add_fusion.5
  117.9 1.9 collective-permute-start
  119.8 8.8 %collective-permute-done = f32[4,128,128]{2,1,0:T(8,128)S(1)} collective-permute-done((f32[4,128,128]{2,1,0:T(8,128)S(1)}, f32[4,128,128]{2,1,0:T(8,128)S(1)}, u32[]{:S(2)}, u32[]{:S(2)}) %collective-permute-start) | collective-permute-done | bytes 262176 | tf_op jit(solution)/shard_map/while/body/eval_jaxpr/ppermute | solution.py:12
  129.3 1.9 collective-permute-start
  131.3 9.9 %collective-permute-done = f32[4,128,128]{2,1,0:T(8,128)S(1)} collective-permute-done((f32[4,128,128]{2,1,0:T(8,128)S(1)}, f32[4,128,128]{2,1,0:T(8,128)S(1)}, u32[]{:S(2)}, u32[]{:S(2)}) %collective-permute-start) | collective-permute-done | bytes 262176 | tf_op jit(solution)/shard_map/while/body/eval_jaxpr/ppermute | solution.py:12
  141.9 1.9 collective-permute-start
  143.8 11.1 %collective-permute-done = f32[4,128,128]{2,1,0:T(8,128)S(1)} collective-permute-done((f32[4,128,128]{2,1,0:T(8,128)S(1)}, f32[4,128,128]{2,1,0:T(8,128)S(1)}, u32[]{:S(2)}, u32[]{:S(2)}) %collective-permute-start) | collective-permute-done | bytes 262176 | tf_op jit(solution)/shard_map/while/body/eval_jaxpr/ppermute | solution.py:12
  154.8 0.4 convolution_add_fusion.5
  155.5 1.9 collective-permute-start
  157.4 10.4 %collective-permute-done = f32[4,128,128]{2,1,0:T(8,128)S(1)} collective-permute-done((f32[4,128,128]{2,1,0:T(8,128)S(1)}, f32[4,128,128]{2,1,0:T(8,128)S(1)}, u32[]{:S(2)}, u32[]{:S(2)}) %collective-permute-start) | collective-permute-done | bytes 262176 | tf_op jit(solution)/shard_map/while/body/eval_jaxpr/ppermute | solution.py:12
  167.8 0.4 convolution_add_fusion.5
  168.5 1.9 collective-permute-start
  170.5 9.6 %collective-permute-done = f32[4,128,128]{2,1,0:T(8,128)S(1)} collective-permute-done((f32[4,128,128]{2,1,0:T(8,128)S(1)}, f32[4,128,128]{2,1,0:T(8,128)S(1)}, u32[]{:S(2)}, u32[]{:S(2)}) %collective-permute-start) | collective-permute-done | bytes 262176 | tf_op jit(solution)/shard_map/while/body/eval_jaxpr/ppermute | solution.py:12
  180.0 0.4 convolution_add_fusion.5
  180.7 1.9 collective-permute-start
  182.6 8.6 %collective-permute-done = f32[4,128,128]{2,1,0:T(8,128)S(1)} collective-permute-done((f32[4,128,128]{2,1,0:T(8,128)S(1)}, f32[4,128,128]{2,1,0:T(8,128)S(1)}, u32[]{:S(2)}, u32[]{:S(2)}) %collective-permute-start) | collective-permute-done | bytes 262176 | tf_op jit(solution)/shard_map/while/body/eval_jaxpr/ppermute | solution.py:12
  191.3 0.4 convolution_add_fusion.5
  192.0 1.9 collective-permute-start
  193.9 8.4 %collective-permute-done = f32[4,128,128]{2,1,0:T(8,128)S(1)} collective-permute-done((f32[4,128,128]{2,1,0:T(8,128)S(1)}, f32[4,128,128]{2,1,0:T(8,128)S(1)}, u32[]{:S(2)}, u32[]{:S(2)}) %collective-permute-start) | collective-permute-done | bytes 262176 | tf_op jit(solution)/shard_map/while/body/eval_jaxpr/ppermute | solution.py:12
  203.0 1.9 collective-permute-start
  204.9 8.4 %collective-permute-done = f32[4,128,128]{2,1,0:T(8,128)S(1)} collective-permute-done((f32[4,128,128]{2,1,0:T(8,128)S(1)}, f32[4,128,128]{2,1,0:T(8,128)S(1)}, u32[]{:S(2)}, u32[]{:S(2)}) %collective-permute-start) | collective-permute-done | bytes 262176 | tf_op jit(solution)/shard_map/while/body/eval_jaxpr/ppermute | solution.py:12
  213.4 0.4 convolution_add_fusion.5
  214.1 1.9 collective-permute-start
  216.0 8.4 %collective-permute-done = f32[4,128,128]{2,1,0:T(8,128)S(1)} collective-permute-done((f32[4,128,128]{2,1,0:T(8,128)S(1)}, f32[4,128,128]{2,1,0:T(8,128)S(1)}, u32[]{:S(2)}, u32[]{:S(2)}) %collective-permute-start) | collective-permute-done | bytes 262176 | tf_op jit(solution)/shard_map/while/body/eval_jaxpr/ppermute | solution.py:12
  225.2 1.6 multiply_reduce_fusion.1
  226.7 0.6 copy-done.10
  227.6 0.7 convert_element_type.83
  228.3 15.8 %all-to-all-start = ((bf16[1,32,4,512]{3,2,0,1:T(4,128)(2,1)}), bf16[1,32,4,512]{3,2,0,1:T(4,128)(2,1)S(1)}, u32[]{:S(2)}, u32[]{:S(2)}) async-start(bf16[1,32,4,512]{3,2,0,1:T(4,128)(2,1)} %bitcast.34), calls=%async_computation | async-start | bytes 262144 | tf_op jit(solution)/shard_map/all_to_all | solution.py:140
  244.6 0.7 copy-done.8
  245.7 0.7 copy-done.6
  246.6 0.5 fusion.5
  247.1 39.4 %custom-call.9 = f32[16,1,32,32]{2,3,1,0:T(8,128)S(1)} custom-call(f32[16,1,32,32]{3,2,1,0:T(8,128)S(1)} %fusion.5), custom_call_target="InvertDiagBlocksLowerTriangular" | custom-call | tf_op jit(solution)/shard_map/while/body/eval_jaxpr/jit(_solve_triangular)/vmap()/triangular_solve | solution.py:32
  287.3 0.6 fusion.13
  289.4 0.5 copy-done.11
  290.3 29.0 %all_to_all.8 = bf16[32,1,4,512]{3,2,1,0:T(4,128)(2,1)S(1)} all-to-all(bf16[32,1,4,512]{3,2,1,0:T(4,128)(2,1)S(1)} %copy.53), channel_id=1, replica_groups=mesh['line'=32,'scan'=16] {'line'}, dimensions={0} | all-to-all | bytes 262144 | tf_op jit(solution)/shard_map/all_to_all | solution.py:163
  319.4 0.7 reshape.271
  (104 shorter events, 12.4 us)
Async XLA Ops:
  0.0 1.0 copy-start.1
  1.0 0.9 copy-start.2
  1.9 0.9 copy-start.3
  2.8 0.7 copy-start.9
  4.0 0.7 copy-start.7
  49.1 12.1 %collective-permute-start = (f32[4,128,128]{2,1,0:T(8,128)S(1)}, f32[4,128,128]{2,1,0:T(8,128)S(1)}, u32[]{:S(2)}, u32[]{:S(2)}) collective-permute-start(f32[4,128,128]{2,1,0:T(8,128)S(1)} %get-tuple-element.160), channel_id=1, source_target_pairs={{0,1},{1,2},{2,3},{3,4},{4,5},{5,6},{6,7},{7,8},{8,9},{9,10},{10,1... | collective-permute-start | bytes 786440 | tf_op jit(solution)/shard_map/while/body/eval_jaxpr/ppermute | solution.py:12
  61.1 0.7 copy-start
  61.8 11.2 %collective-permute-start = (f32[4,128,128]{2,1,0:T(8,128)S(1)}, f32[4,128,128]{2,1,0:T(8,128)S(1)}, u32[]{:S(2)}, u32[]{:S(2)}) collective-permute-start(f32[4,128,128]{2,1,0:T(8,128)S(1)} %get-tuple-element.160), channel_id=1, source_target_pairs={{0,1},{1,2},{2,3},{3,4},{4,5},{5,6},{6,7},{7,8},{8,9},{9,10},{10,1... | collective-permute-start | bytes 786440 | tf_op jit(solution)/shard_map/while/body/eval_jaxpr/ppermute | solution.py:12
  73.0 0.7 copy-start
  73.7 10.4 %collective-permute-start = (f32[4,128,128]{2,1,0:T(8,128)S(1)}, f32[4,128,128]{2,1,0:T(8,128)S(1)}, u32[]{:S(2)}, u32[]{:S(2)}) collective-permute-start(f32[4,128,128]{2,1,0:T(8,128)S(1)} %get-tuple-element.160), channel_id=1, source_target_pairs={{0,1},{1,2},{2,3},{3,4},{4,5},{5,6},{6,7},{7,8},{8,9},{9,10},{10,1... | collective-permute-start | bytes 786440 | tf_op jit(solution)/shard_map/while/body/eval_jaxpr/ppermute | solution.py:12
  84.1 0.7 copy-start
  84.7 10.4 %collective-permute-start = (f32[4,128,128]{2,1,0:T(8,128)S(1)}, f32[4,128,128]{2,1,0:T(8,128)S(1)}, u32[]{:S(2)}, u32[]{:S(2)}) collective-permute-start(f32[4,128,128]{2,1,0:T(8,128)S(1)} %get-tuple-element.160), channel_id=1, source_target_pairs={{0,1},{1,2},{2,3},{3,4},{4,5},{5,6},{6,7},{7,8},{8,9},{9,10},{10,1... | collective-permute-start | bytes 786440 | tf_op jit(solution)/shard_map/while/body/eval_jaxpr/ppermute | solution.py:12
  95.1 0.7 copy-start
  95.8 10.4 %collective-permute-start = (f32[4,128,128]{2,1,0:T(8,128)S(1)}, f32[4,128,128]{2,1,0:T(8,128)S(1)}, u32[]{:S(2)}, u32[]{:S(2)}) collective-permute-start(f32[4,128,128]{2,1,0:T(8,128)S(1)} %get-tuple-element.160), channel_id=1, source_target_pairs={{0,1},{1,2},{2,3},{3,4},{4,5},{5,6},{6,7},{7,8},{8,9},{9,10},{10,1... | collective-permute-start | bytes 786440 | tf_op jit(solution)/shard_map/while/body/eval_jaxpr/ppermute | solution.py:12
  106.2 0.7 copy-start
  106.9 10.4 %collective-permute-start = (f32[4,128,128]{2,1,0:T(8,128)S(1)}, f32[4,128,128]{2,1,0:T(8,128)S(1)}, u32[]{:S(2)}, u32[]{:S(2)}) collective-permute-start(f32[4,128,128]{2,1,0:T(8,128)S(1)} %get-tuple-element.160), channel_id=1, source_target_pairs={{0,1},{1,2},{2,3},{3,4},{4,5},{5,6},{6,7},{7,8},{8,9},{9,10},{10,1... | collective-permute-start | bytes 786440 | tf_op jit(solution)/shard_map/while/body/eval_jaxpr/ppermute | solution.py:12
  117.2 0.7 copy-start
  117.9 10.7 %collective-permute-start = (f32[4,128,128]{2,1,0:T(8,128)S(1)}, f32[4,128,128]{2,1,0:T(8,128)S(1)}, u32[]{:S(2)}, u32[]{:S(2)}) collective-permute-start(f32[4,128,128]{2,1,0:T(8,128)S(1)} %get-tuple-element.160), channel_id=1, source_target_pairs={{0,1},{1,2},{2,3},{3,4},{4,5},{5,6},{6,7},{7,8},{8,9},{9,10},{10,1... | collective-permute-start | bytes 786440 | tf_op jit(solution)/shard_map/while/body/eval_jaxpr/ppermute | solution.py:12
  128.6 0.7 copy-start
  129.3 11.8 %collective-permute-start = (f32[4,128,128]{2,1,0:T(8,128)S(1)}, f32[4,128,128]{2,1,0:T(8,128)S(1)}, u32[]{:S(2)}, u32[]{:S(2)}) collective-permute-start(f32[4,128,128]{2,1,0:T(8,128)S(1)} %get-tuple-element.160), channel_id=1, source_target_pairs={{0,1},{1,2},{2,3},{3,4},{4,5},{5,6},{6,7},{7,8},{8,9},{9,10},{10,1... | collective-permute-start | bytes 786440 | tf_op jit(solution)/shard_map/while/body/eval_jaxpr/ppermute | solution.py:12
  141.2 0.7 copy-start
  141.9 13.0 %collective-permute-start = (f32[4,128,128]{2,1,0:T(8,128)S(1)}, f32[4,128,128]{2,1,0:T(8,128)S(1)}, u32[]{:S(2)}, u32[]{:S(2)}) collective-permute-start(f32[4,128,128]{2,1,0:T(8,128)S(1)} %get-tuple-element.160), channel_id=1, source_target_pairs={{0,1},{1,2},{2,3},{3,4},{4,5},{5,6},{6,7},{7,8},{8,9},{9,10},{10,1... | collective-permute-start | bytes 786440 | tf_op jit(solution)/shard_map/while/body/eval_jaxpr/ppermute | solution.py:12
  154.8 0.7 copy-start
  155.5 12.3 %collective-permute-start = (f32[4,128,128]{2,1,0:T(8,128)S(1)}, f32[4,128,128]{2,1,0:T(8,128)S(1)}, u32[]{:S(2)}, u32[]{:S(2)}) collective-permute-start(f32[4,128,128]{2,1,0:T(8,128)S(1)} %get-tuple-element.160), channel_id=1, source_target_pairs={{0,1},{1,2},{2,3},{3,4},{4,5},{5,6},{6,7},{7,8},{8,9},{9,10},{10,1... | collective-permute-start | bytes 786440 | tf_op jit(solution)/shard_map/while/body/eval_jaxpr/ppermute | solution.py:12
  167.8 0.7 copy-start
  168.5 11.5 %collective-permute-start = (f32[4,128,128]{2,1,0:T(8,128)S(1)}, f32[4,128,128]{2,1,0:T(8,128)S(1)}, u32[]{:S(2)}, u32[]{:S(2)}) collective-permute-start(f32[4,128,128]{2,1,0:T(8,128)S(1)} %get-tuple-element.160), channel_id=1, source_target_pairs={{0,1},{1,2},{2,3},{3,4},{4,5},{5,6},{6,7},{7,8},{8,9},{9,10},{10,1... | collective-permute-start | bytes 786440 | tf_op jit(solution)/shard_map/while/body/eval_jaxpr/ppermute | solution.py:12
  180.0 0.7 copy-start
  180.7 10.6 %collective-permute-start = (f32[4,128,128]{2,1,0:T(8,128)S(1)}, f32[4,128,128]{2,1,0:T(8,128)S(1)}, u32[]{:S(2)}, u32[]{:S(2)}) collective-permute-start(f32[4,128,128]{2,1,0:T(8,128)S(1)} %get-tuple-element.160), channel_id=1, source_target_pairs={{0,1},{1,2},{2,3},{3,4},{4,5},{5,6},{6,7},{7,8},{8,9},{9,10},{10,1... | collective-permute-start | bytes 786440 | tf_op jit(solution)/shard_map/while/body/eval_jaxpr/ppermute | solution.py:12
  191.3 0.7 copy-start
  192.0 10.4 %collective-permute-start = (f32[4,128,128]{2,1,0:T(8,128)S(1)}, f32[4,128,128]{2,1,0:T(8,128)S(1)}, u32[]{:S(2)}, u32[]{:S(2)}) collective-permute-start(f32[4,128,128]{2,1,0:T(8,128)S(1)} %get-tuple-element.160), channel_id=1, source_target_pairs={{0,1},{1,2},{2,3},{3,4},{4,5},{5,6},{6,7},{7,8},{8,9},{9,10},{10,1... | collective-permute-start | bytes 786440 | tf_op jit(solution)/shard_map/while/body/eval_jaxpr/ppermute | solution.py:12
  202.3 0.7 copy-start
  203.0 10.4 %collective-permute-start = (f32[4,128,128]{2,1,0:T(8,128)S(1)}, f32[4,128,128]{2,1,0:T(8,128)S(1)}, u32[]{:S(2)}, u32[]{:S(2)}) collective-permute-start(f32[4,128,128]{2,1,0:T(8,128)S(1)} %get-tuple-element.160), channel_id=1, source_target_pairs={{0,1},{1,2},{2,3},{3,4},{4,5},{5,6},{6,7},{7,8},{8,9},{9,10},{10,1... | collective-permute-start | bytes 786440 | tf_op jit(solution)/shard_map/while/body/eval_jaxpr/ppermute | solution.py:12
  213.4 0.7 copy-start
  214.1 10.4 %collective-permute-start = (f32[4,128,128]{2,1,0:T(8,128)S(1)}, f32[4,128,128]{2,1,0:T(8,128)S(1)}, u32[]{:S(2)}, u32[]{:S(2)}) collective-permute-start(f32[4,128,128]{2,1,0:T(8,128)S(1)} %get-tuple-element.160), channel_id=1, source_target_pairs={{0,1},{1,2},{2,3},{3,4},{4,5},{5,6},{6,7},{7,8},{8,9},{9,10},{10,1... | collective-permute-start | bytes 786440 | tf_op jit(solution)/shard_map/while/body/eval_jaxpr/ppermute | solution.py:12
  224.5 0.7 copy-start
  226.7 0.7 copy-start.10
  228.3 15.8 %copy-start.4 = (bf16[32,1,4,512]{3,2,1,0:T(4,128)(2,1)S(1)}, bf16[32,1,4,512]{3,2,1,0:T(4,128)(2,1)}, u32[]{:S(2)}) copy-start(bf16[32,1,4,512]{3,2,1,0:T(4,128)(2,1)} %param.20) | copy-start | bytes 393220
  228.3 58.6 %all-to-all-start = ((bf16[1,32,4,512]{3,2,0,1:T(4,128)(2,1)}), bf16[1,32,4,512]{3,2,0,1:T(4,128)(2,1)S(1)}, u32[]{:S(2)}, u32[]{:S(2)}) async-start(bf16[1,32,4,512]{3,2,0,1:T(4,128)(2,1)} %bitcast.34), calls=%async_computation | async-start | bytes 262144 | tf_op jit(solution)/shard_map/all_to_all | solution.py:140
  244.4 1.2 copy-start.5
  244.6 0.7 copy-start.8
  245.7 0.7 copy-start.6
  289.3 0.7 copy-start.11
where the time goes:
time: 321 us; the launch traced here: 320 us
  waiting for transfers between devices  135 us (42%)
  other arithmetic  81.1 us (25%)
  starting transfers between devices  46 us (14%)
  blocking collectives  29 us (9%)
  matrix products  14.5 us (5%)
  local copies, waits for them, and re-layouts  13.4 us (4%)
    ppermute x15, waiting for transfers between devices, from_behind(): return lax.ppermute(block, axis, route)  135 us
    another operation x2, other arithmetic, block_terms(): solved = jax.scipy.linalg.solve_triangular(system, right_side, lower=True)  78.7 us
    ppermute x15, starting transfers between devices, from_behind(): return lax.ppermute(block, axis, route)  30.2 us
    all_to_all x1, blocking collectives, shards(): lax.all_to_all(normed, 'line', split_axis=0, concat_axis=1, tiled=True)  29 us
    all_to_all x1, starting transfers between devices, shards(): lax.all_to_all(arranged, 'line', split_axis=1, concat_axis=0, tiled=True)  15.8 us
  transfers between devices with their start and end apart: 16, of which 15 were waited for; matrix products, arithmetic and copies ran while one was open for 13% of the time, Pallas kernels for 0%

commit v1 on v0

v1 whole, which is shorter than its diff:
```python
import jax
import jax.numpy as jnp
from jax import lax
from jax.sharding import PartitionSpec as P

HIGHEST = lax.Precision.HIGHEST
BASE_BLOCK = 16


def from_behind(block, axis, distance):
    devices = range(lax.axis_size(axis))
    route = [(i - distance, i) for i in devices if i - distance in devices]
    return lax.ppermute(block, axis, route)


def matmul(spec, left, right):
    return jnp.einsum(spec, left, right, precision=HIGHEST)


def unit_lower_inverse(system):
    batch = system.shape[:-2]
    size = system.shape[-1]
    base = min(BASE_BLOCK, size)
    count = size // base
    assert count * base == size and count & (count - 1) == 0
    eye = jnp.eye(base, dtype=jnp.float32)
    grid = system.reshape(batch + (count, base, count, base))
    diagonal = jnp.moveaxis(jnp.diagonal(grid, axis1=-4, axis2=-2), -1, -3)
    lower = diagonal - eye
    inverse = eye - lower
    power = lower
    reach = 2
    while reach < base:
        power = matmul("...ij,...jk->...ik", power, power)
        inverse = inverse + matmul("...ij,...jk->...ik", inverse, power)
        reach *= 2
    width = base
    while width < size:
        pairs = size // (2 * width)
        grid = system.reshape(batch + (pairs, 2, width, pairs, 2, width))
        coupling = jnp.moveaxis(jnp.diagonal(grid, axis1=-6, axis2=-3), -1, -5)[..., 1, :, 0, :]
        halves = inverse.reshape(batch + (pairs, 2, width, width))
        upper_inverse = halves[..., 0, :, :]
        lower_inverse = halves[..., 1, :, :]
        mixed = -matmul(
            "...ij,...jk->...ik", matmul("...ij,...jk->...ik", lower_inverse, coupling), upper_inverse
        )
        top = jnp.concatenate([upper_inverse, jnp.zeros_like(upper_inverse)], axis=-1)
        bottom = jnp.concatenate([mixed, lower_inverse], axis=-1)
        inverse = jnp.concatenate([top, bottom], axis=-2)
        width *= 2
    return inverse.reshape(batch + (size, size))


def block_system(key_block, log_decay, beta_block):
    key_unit = key_block / jnp.sqrt(jnp.sum(key_block * key_block, axis=-1, keepdims=True) + 1e-06)
    cumulative = jnp.cumsum(log_decay, axis=-1)
    sequence_length = key_block.shape[1]
    lower_mask = jnp.tril(jnp.ones((sequence_length, sequence_length), dtype=jnp.bool_))
    strict = jnp.tril(jnp.ones((sequence_length, sequence_length), dtype=jnp.bool_), -1)
    spread = cumulative[:, :, None] - cumulative[:, None, :]
    ratios = jnp.where(lower_mask, jnp.exp(jnp.where(lower_mask, spread, 0.0)), 0.0)
    key_inner = matmul("bik,bjk->bij", key_unit, key_unit)
    system = jnp.where(strict, beta_block[:, :, None] * ratios * key_inner, 0.0) + jnp.eye(
        sequence_length, dtype=jnp.float32
    )
    return key_unit, cumulative, ratios, unit_lower_inverse(system)


def block_terms(query_block, key_block, value_block, log_decay, beta_block):
    key_unit, cumulative, ratios, system_inverse = block_system(key_block, log_decay, beta_block)
    growth = jnp.exp(cumulative)
    right_side = jnp.concatenate(
        [beta_block[:, :, None] * value_block, (beta_block * growth)[:, :, None] * key_unit],
        axis=-1,
    )
    solved = matmul("bij,bjv->biv", system_inverse, right_side)
    value_size = value_block.shape[-1]
    updates = solved[:, :, :value_size]
    weighted = solved[:, :, value_size:]
    attend = ratios * matmul("bik,bjk->bij", query_block, key_unit)
    local_out = matmul("bij,bjv->biv", attend, updates)
    state_query = growth[:, :, None] * query_block - matmul("bij,bjk->bik", attend, weighted)
    key_tail = jnp.exp(cumulative[:, -1:] - cumulative)[:, :, None] * key_unit
    return (local_out, state_query, key_tail, weighted, updates, growth[:, -1])


def column_operator(query_block, key_block, log_decay, beta_block):
    key_unit, cumulative, ratios, system_inverse = block_system(key_block, log_decay, beta_block)
    attend = ratios * matmul("bik,bjk->bij", query_block, key_unit)
    return matmul("bij,bjk->bik", attend, system_inverse) * beta_block[:, None, :]


def to_heads(array, leading_count, sequence_length, head_count, head_size):
    shaped = array.astype(jnp.float32).reshape(
        leading_count, sequence_length, head_count, head_size
    )
    return shaped.transpose(0, 2, 1, 3).reshape(
        leading_count * head_count, sequence_length, head_size
    )


def gates_to_heads(array, leading_count, sequence_length, head_count):
    return array.transpose(0, 2, 1).reshape(leading_count * head_count, sequence_length)


def from_heads(array, leading_count, sequence_length, head_count, head_size):
    return array.reshape(leading_count, head_count, sequence_length, head_size).transpose(
        0, 2, 1, 3
    )


def head_norm(array, gain):
    return array * lax.rsqrt(jnp.mean(array * array, axis=-1, keepdims=True) + 1e-05) * gain


def prefix_states(transfer, offset):
    scan_count = lax.axis_size("scan")
    head_size = offset.shape[-1]
    distance = 1
    while distance < scan_count:
        if 2 * distance < scan_count:
            arrived = from_behind(jnp.concatenate([transfer, offset], axis=-1), "scan", distance)
            composed = matmul("bij,bjv->biv", transfer, arrived)
            transfer = composed[:, :, :head_size]
            offset = composed[:, :, head_size:] + offset
        else:
            arrived = from_behind(offset, "scan", distance)
            offset = matmul("bij,bjv->biv", transfer, arrived) + offset
        distance *= 2
    return from_behind(offset, "scan", 1)


def shards(
    query_row,
    key_row,
    value_row,
    decay_row,
    beta_row,
    gain_row,
    query_col,
    key_col,
    decay_col,
    beta_col,
    gain_col,
):
    row_count, segment, features = query_row.shape
    head_size = gain_row.shape[0]
    head_count = features // head_size
    line_count = lax.axis_size("line")
    total_rows = query_col.shape[0]
    column_count = query_col.shape[2]

    def columns(array):
        return array.reshape(total_rows, column_count, -1).transpose(1, 0, 2)

    local_out, state_query, key_tail, weighted, updates, ending = block_terms(
        to_heads(query_row, row_count, segment, head_count, head_size),
        to_heads(key_row, row_count, segment, head_count, head_size),
        to_heads(value_row, row_count, segment, head_count, head_size),
        gates_to_heads(decay_row, row_count, segment, head_count),
        gates_to_heads(beta_row, row_count, segment, head_count),
    )
    identity = jnp.broadcast_to(
        jnp.eye(head_size, dtype=jnp.float32), (row_count * head_count, head_size, head_size)
    )
    transfer = ending[:, None, None] * identity - matmul("bjk,bjl->bkl", key_tail, weighted)
    offset = matmul("bjk,bjv->bkv", key_tail, updates)

    operator = column_operator(
        to_heads(columns(query_col), column_count, total_rows, head_count, head_size),
        to_heads(columns(key_col), column_count, total_rows, head_count, head_size),
        gates_to_heads(columns(decay_col), column_count, total_rows, head_count),
        gates_to_heads(columns(beta_col), column_count, total_rows, head_count),
    )

    incoming = prefix_states(transfer, offset)
    row_out = local_out + matmul("bik,bkv->biv", state_query, incoming)
    row_scan = from_heads(row_out, row_count, segment, head_count, head_size)
    values_col = (
        head_norm(row_scan, gain_row).reshape(row_count, segment, features).astype(jnp.bfloat16)
    )
    arranged = values_col.reshape(row_count, line_count, segment // line_count, features)
    column_values = lax.all_to_all(arranged, "line", split_axis=1, concat_axis=0, tiled=True)

    col_out = matmul(
        "bij,bjv->biv",
        operator,
        to_heads(columns(column_values), column_count, total_rows, head_count, head_size),
    )
    col_scan = from_heads(col_out, column_count, total_rows, head_count, head_size)
    normed = (
        head_norm(col_scan, gain_col)
        .transpose(1, 0, 2, 3)
        .reshape(total_rows, 1, column_count, features)
        .astype(jnp.bfloat16)
    )
    returned = lax.all_to_all(normed, "line", split_axis=0, concat_axis=1, tiled=True)
    return returned.reshape(row_count, segment, features)


def solution(mesh):
    placed = (
        P("line", "scan", None),
        P("line", "scan", None),
        P("line", "scan", None),
        P("line", "scan", None),
        P("line", "scan", None),
        P(),
        P(None, "scan", "line", None),
        P(None, "scan", "line", None),
        P(None, "scan", "line", None),
        P(None, "scan", "line", None),
        P(),
    )
    return jax.shard_map(
        shards, mesh=mesh, in_specs=placed, out_specs=P("line", "scan", None), check_vma=False
    )
```

time: 321 us -> 161 us (0.50)
  other arithmetic: 81.1 us -> 4.77 us
  waiting for transfers between devices: 135 us -> 65 us
  starting transfers between devices: 46 us -> 26.8 us
  local copies, waits for them, and re-layouts: 13.4 us -> 23.5 us
  blocking collectives: 29 us -> 20.2 us
  matrix products: 14.5 us -> 19.1 us
    ppermute x15 -> x5, waiting for transfers between devices: 135 us -> 48.8 us  [from_behind(): return lax.ppermute(block, axis, route)]
    another operation x10 -> x7, other arithmetic: 79.4 us -> 1.34 us  [the longest x2 1.17 us: block_system(): cumulative = jnp.cumsum(log_decay, axis=-1)]
    ppermute x15 -> x5, starting transfers between devices: 30.2 us -> 11.3 us  [from_behind(): return lax.ppermute(block, axis, route)]
    all_to_all x1, waiting for transfers between devices: 0.01 us -> 16.2 us  [shards(): lax.all_to_all(arranged, 'line', split_axis=1, concat_axis=0, tiled=True)]
    reshape x0 -> x8, local copies, waits for them, and re-layouts: none -> 9.05 us  [the longest x4 6.38 us: unit_lower_inverse(): grid = system.reshape(batch + (pairs, 2, width, pairs, 2, width))]
    all_to_all x1, blocking collectives: 29 us -> 20.2 us  [shards(): lax.all_to_all(normed, 'line', split_axis=0, concat_axis=1, tiled=True)]
    dot_general x27 -> x36, matrix products: 13.2 us -> 19.1 us  [matmul(): return jnp.einsum(spec, left, right, precision=HIGHEST)]
    gather x0 -> x6, local copies, waits for them, and re-layouts: none -> 5.56 us  [the longest x4 2.84 us: unit_lower_inverse(): jnp.diagonal(grid, axis1=-6, axis2=-3)]
  transfers between devices with their start and end apart: 16 -> 6, of which waited for: 15 -> 6; matrix products, arithmetic and copies ran while one was open for 13% -> 6% of each run, Pallas kernels for 0% -> 0%
where the time goes in v1:
time: 161 us; the launch traced here: 160 us
  waiting for transfers between devices  65 us (40%)
  starting transfers between devices  26.8 us (17%)
  local copies, waits for them, and re-layouts  23.5 us (15%)
  blocking collectives  20.2 us (13%)
  matrix products  19.1 us (12%)
  other arithmetic  4.77 us (3%)
    ppermute x5, waiting for transfers between devices, from_behind(): return lax.ppermute(block, axis, route)  48.8 us
    all_to_all x1, blocking collectives, shards(): lax.all_to_all(normed, 'line', split_axis=0, concat_axis=1, tiled=True)  20.2 us
    dot_general x36, matrix products, matmul(): return jnp.einsum(spec, left, right, precision=HIGHEST)  19.1 us
    all_to_all x1, waiting for transfers between devices, shards(): lax.all_to_all(arranged, 'line', split_axis=1, concat_axis=0, tiled=True)  16.2 us
    all_to_all x1, starting transfers between devices, shards(): lax.all_to_all(arranged, 'line', split_axis=1, concat_axis=0, tiled=True)  15.5 us
    ppermute x5, starting transfers between devices, from_behind(): return lax.ppermute(block, axis, route)  11.3 us
    reshape x4, local copies, waits for them, and re-layouts, unit_lower_inverse(): grid = system.reshape(batch + (pairs, 2, width, pairs, 2, width))  6.38 us
  transfers between devices with their start and end apart: 6, of which 6 were waited for; matrix products, arithmetic and copies ran while one was open for 6% of the time, Pallas kernels for 0%

profile of v1, /device:TPU:6, one launch (start us, length us, event | category | flops | bytes accessed | tf_op | source)
XLA Modules:
  0.0 160.5 jit_solution(16315347786779798503)
XLA Ops:
  0.0 0.8 fusion.86
  1.2 1.0 reduce_window_sum.23
  2.1 1.5 fusion.5
  3.6 0.6 reshape.334
  4.2 1.7 %copy.195 = f32[4,8,16,8,16]{4,2,3,1,0:T(8,128)} copy(f32[4,8,16,8,16]{4,3,2,1,0:T(8,128)S(1)} %reshape.334) | data formatting | bytes 524288 | tf_op jit(solution)/shard_map/reshape | solution.py:27
  5.9 2.2 %gather_fusion.1 = f32[8,4,16,16]{3,2,1,0:T(8,128)S(1)} fusion(f32[4,16,16,8,8]{2,1,4,3,0:T(8,128)} %bitcast.193, s32[8]{0:T(128)S(1)} %or_bitcast_fusion.1), kind=kCustom, calls=%fused_computation.1 | custom fusion | bytes 65600 | tf_op jit(solution)/shard_map/jit(diagonal)/gather | solution.py:28
  8.1 0.4 fusion.36
  8.5 0.4 convolution_add_fusion.2
  8.9 0.4 fusion.91
  9.3 2.7 %reshape.336 = f32[4,4,2,16,4,2,16]{6,5,4,3,2,1,0:T(2,128)S(1)} reshape(f32[4,128,128]{2,1,0:T(8,128)S(1)} %fusion.5) | data formatting | bytes 524288 | tf_op jit(solution)/shard_map/reshape | solution.py:40
  12.0 1.8 %reshape.338 = f32[4,2,2,32,2,2,32]{6,5,4,3,2,1,0:T(2,128)} reshape(f32[4,128,128]{2,1,0:T(8,128)S(1)} %fusion.5) | data formatting | bytes 524288 | tf_op jit(solution)/shard_map/reshape | solution.py:40
  13.8 1.1 transpose.144
  15.1 0.4 fusion.92
  15.5 0.4 convolution_add_fusion.1
  15.9 0.4 convolution_add_fusion
  16.3 1.7 %copy.194 = f32[4,4,2,16,4,2,16]{6,3,4,1,5,2,0:T(8,128)} copy(f32[4,4,2,16,4,2,16]{6,5,4,3,2,1,0:T(2,128)S(1)} %reshape.336) | data formatting | bytes 524288 | tf_op jit(solution)/shard_map/reshape | solution.py:40
  18.0 2.2 %gather_fusion.2 = f32[4,4,2,16,2,16]{5,3,4,2,1,0:T(8,128)S(1)} fusion(f32[4,2,16,2,16,4,4]{4,2,6,5,3,1,0:T(8,128)} %bitcast.192, s32[4]{0:T(128)S(1)} %or_bitcast_fusion), kind=kCustom, calls=%fused_computation.2 | custom fusion | bytes 131104 | tf_op jit(solution)/shard_map/jit(diagonal)/gather | solution.py:41
  20.8 0.6 copy-done
  21.6 0.6 gather_fusion.3
  22.9 1.0 slice.234
  24.7 0.3 broadcast_multiply_fusion
  25.0 0.6 fusion.8
  25.7 0.8 fusion.32
  26.8 0.7 convolution_subtract_fusion
  27.5 0.8 pad_maximum_fusion
  28.4 3.7 %collective-permute-start = (f32[4,128,256]{2,1,0:T(8,128)}, f32[4,128,256]{2,1,0:T(8,128)}, u32[]{:S(2)}, u32[]{:S(2)}) collective-permute-start(f32[4,128,256]{2,1,0:T(8,128)} %pad_maximum_fusion), channel_id=1, source_target_pairs={{0,1},{1,2},{2,3},{3,4},{4,5},{5,6},{6,7},{7,8},{8,9},{9,10},{10,1... | collective-permute-start | bytes 1572872 | tf_op jit(solution)/shard_map/ppermute | solution.py:13
  32.1 0.7 fusion.87
  33.3 0.7 fusion.4
  34.0 0.3 reshape.325
  34.4 0.6 gather_fusion
  35.0 0.4 fusion.39
  35.4 0.4 fusion.89
  35.8 0.4 fusion.90
  36.2 0.7 fusion.88
  36.9 0.4 convolution_add_fusion.5
  37.3 0.4 convolution_add_fusion.4
  37.7 8.6 %collective-permute-done = f32[4,128,256]{2,1,0:T(8,128)} collective-permute-done((f32[4,128,256]{2,1,0:T(8,128)}, f32[4,128,256]{2,1,0:T(8,128)}, u32[]{:S(2)}, u32[]{:S(2)}) %collective-permute-start) | collective-permute-done | bytes 524320 | tf_op jit(solution)/shard_map/ppermute | solution.py:13
  46.3 2.1 %fusion.93 = f32[4,128,256]{1,2,0:T(8,128)S(1)} fusion(f32[4,128,128]{2,1,0:T(8,128)S(1)} %convolution_subtract_fusion, f32[4,128,256]{2,1,0:T(8,128)} %collective-permute-done), kind=kOutput, calls=%fused_computation.184 | convolution fusion | flops 201326592 | bytes 1310720 | tf_op jit(solution)/shard_map/bij,bjv->biv/dot_general | solution.py:17
  48.5 3.0 %collective-permute-start.1 = (f32[4,128,256]{1,2,0:T(8,128)S(1)}, f32[4,128,256]{1,2,0:T(8,128)S(1)}, u32[]{:S(2)}, u32[]{:S(2)}) collective-permute-start(f32[4,128,256]{1,2,0:T(8,128)S(1)} %pad_maximum_fusion.1), channel_id=1, source_target_pairs={{0,2},{1,3},{2,4},{3,5},{4,6},{5,7},{6,8},{7,9},{8,10},{9,11},{10,... | collective-permute-start | bytes 1572872 | tf_op jit(solution)/shard_map/ppermute | solution.py:13
  51.5 0.4 fusion
  51.9 0.7 fusion.84
  52.6 13.0 %collective-permute-done.1 = f32[4,128,256]{1,2,0:T(8,128)S(1)} collective-permute-done((f32[4,128,256]{1,2,0:T(8,128)S(1)}, f32[4,128,256]{1,2,0:T(8,128)S(1)}, u32[]{:S(2)}, u32[]{:S(2)}) %collective-permute-start.1) | collective-permute-done | bytes 524320 | tf_op jit(solution)/shard_map/ppermute | solution.py:13
  65.6 0.6 fusion.77
  66.3 0.8 pad_maximum_fusion.2
  67.1 1.3 collective-permute-start.2
  68.4 0.3 transpose.135
  69.1 0.5 convolution_multiply_fusion.1
  69.6 11.5 %collective-permute-done.2 = f32[4,128,256]{1,2,0:T(8,128)} collective-permute-done((f32[4,128,256]{1,2,0:T(8,128)}, f32[4,128,256]{1,2,0:T(8,128)}, u32[]{:S(2)}, u32[]{:S(2)}) %collective-permute-start.2) | collective-permute-done | bytes 524320 | tf_op jit(solution)/shard_map/ppermute | solution.py:13
  81.2 1.7 %fusion.75 = f32[4,128,256]{2,1,0:T(8,128)S(1)} fusion(f32[4,128,256]{1,2,0:T(8,128)} %collective-permute-done.2, f32[4,128,256]{1,2,0:T(8,128)S(1)} %fusion.77), kind=kOutput, calls=%fused_computation.166 | convolution fusion | flops 201326592 | bytes 1310720 | tf_op jit(solution)/shard_map/bij,bjv->biv/dot_general | solution.py:17
  83.0 1.3 collective-permute-start.3
  84.6 0.6 fusion.34
  85.2 7.6 %collective-permute-done.3 = f32[4,128,128]{1,2,0:T(8,128)S(1)} collective-permute-done((f32[4,128,128]{1,2,0:T(8,128)S(1)}, f32[4,128,128]{1,2,0:T(8,128)S(1)}, u32[]{:S(2)}, u32[]{:S(2)}) %collective-permute-start.3) | collective-permute-done | bytes 262176 | tf_op jit(solution)/shard_map/ppermute | solution.py:13
  92.8 0.7 convolution_add_fusion.7
  93.6 2.1 %collective-permute-start.4 = (f32[4,128,128]{1,2,0:T(8,128)S(1)}, f32[4,128,128]{1,2,0:T(8,128)S(1)}, u32[]{:S(2)}, u32[]{:S(2)}) collective-permute-start(f32[4,128,128]{1,2,0:T(8,128)S(1)} %convolution_add_fusion.7), channel_id=1, source_target_pairs={{0,1},{1,2},{2,3},{3,4},{4,5},{5,6},{6,7},{7,8},{8,9},{9,10},{10,1... | collective-permute-start | bytes 786440 | tf_op jit(solution)/shard_map/ppermute | solution.py:13
  95.7 0.4 convolution_subtract_fusion.1
  96.1 8.0 %collective-permute-done.4 = f32[4,128,128]{1,2,0:T(8,128)S(1)} collective-permute-done((f32[4,128,128]{1,2,0:T(8,128)S(1)}, f32[4,128,128]{1,2,0:T(8,128)S(1)}, u32[]{:S(2)}, u32[]{:S(2)}) %collective-permute-start.4) | collective-permute-done | bytes 262176 | tf_op jit(solution)/shard_map/ppermute | solution.py:13
  104.1 0.7 multiply_reduce_fusion.1
  105.0 0.7 convert_element_type.90
  105.7 15.5 %all-to-all-start = ((bf16[1,32,4,512]{3,2,0,1:T(4,128)(2,1)}), bf16[1,32,4,512]{3,2,0,1:T(4,128)(2,1)S(1)}, u32[]{:S(2)}, u32[]{:S(2)}) async-start(bf16[1,32,4,512]{3,2,0,1:T(4,128)(2,1)} %bitcast.66), calls=%async_computation | async-start | bytes 262144 | tf_op jit(solution)/shard_map/all_to_all | solution.py:184
  121.4 0.4 convolution_multiply_fusion.4
  121.8 0.4 convolution_multiply_fusion.2
  122.2 16.2 %all-to-all-done = bf16[1,32,4,512]{3,2,0,1:T(4,128)(2,1)S(1)} async-done(((bf16[1,32,4,512]{3,2,0,1:T(4,128)(2,1)}), bf16[1,32,4,512]{3,2,0,1:T(4,128)(2,1)S(1)}, u32[]{:S(2)}, u32[]{:S(2)}) %all-to-all-start) | async-done | bytes 131104 | tf_op jit(solution)/shard_map/all_to_all | solution.py:184
  139.6 20.2 %all_to_all.8 = bf16[32,1,4,512]{3,2,1,0:T(4,128)(2,1)S(1)} all-to-all(bf16[32,1,4,512]{3,2,1,0:T(4,128)(2,1)S(1)} %copy.160), channel_id=1, replica_groups=mesh['line'=32,'scan'=16] {'line'}, dimensions={0} | all-to-all | bytes 262144 | tf_op jit(solution)/shard_map/all_to_all | solution.py:198
  159.8 0.7 reshape.350
  (131 shorter events, 6.0 us)
Async XLA Ops:
  1.0 25.8 %copy-start.20 = (f32[4,128]{1,0:T(4,128)}, f32[4,128]{1,0:T(4,128)S(1)}, u32[]{:S(2)}) copy-start(f32[4,128]{1,0:T(4,128)S(1)} %sqrt_bitcast_fusion) | copy-start | bytes 6148
  1.1 4.8 %copy-start.17 = (pred[128,128]{1,0:T(8,128)(4,1)}, pred[128,128]{1,0:T(8,128)(4,1)S(1)}, u32[]{:S(2)}) copy-start(pred[128,128]{1,0:T(8,128)(4,1)S(1)} %get-tuple-element.57) | copy-start | bytes 49156
  20.2 1.2 copy-start
  22.2 2.4 %copy-start.2 = (bf16[1,128,512]{2,1,0:T(8,128)(2,1)S(1)}, bf16[1,128,512]{2,1,0:T(8,128)(2,1)}, u32[]{:S(2)}) copy-start(bf16[1,128,512]{2,1,0:T(8,128)(2,1)} %param.13) | copy-start | bytes 393220
  22.3 2.3 %copy-start.22 = (f32[1,128,4]{1,2,0:T(4,128)S(1)}, f32[1,128,4]{1,2,0:T(4,128)}, u32[]{:S(2)}) copy-start(f32[1,128,4]{1,2,0:T(4,128)} %param.15) | copy-start | bytes 6148
  25.6 6.4 %copy-start.1 = (bf16[1,128,512]{2,1,0:T(8,128)(2,1)S(1)}, bf16[1,128,512]{2,1,0:T(8,128)(2,1)}, u32[]{:S(2)}) copy-start(bf16[1,128,512]{2,1,0:T(8,128)(2,1)} %param.11) | copy-start | bytes 393220
  25.7 7.1 %copy-start.7 = (bf16[32,1,4,512]{3,2,1,0:T(4,128)(2,1)S(1)}, bf16[32,1,4,512]{3,2,1,0:T(4,128)(2,1)}, u32[]{:S(2)}) copy-start(bf16[32,1,4,512]{3,2,1,0:T(4,128)(2,1)} %param.18) | copy-start | bytes 393220
  26.6 6.5 %copy-start.25 = (f32[32,1,4,4]{0,3,2,1:T(4,128)S(1)}, f32[32,1,4,4]{0,3,2,1:T(4,128)}, u32[]{:S(2)}) copy-start(f32[32,1,4,4]{0,3,2,1:T(4,128)} %param.19) | copy-start | bytes 6148
  26.6 6.7 %copy-start.19 = (f32[32,1,4,4]{0,3,2,1:T(4,128)S(1)}, f32[32,1,4,4]{0,3,2,1:T(4,128)}, u32[]{:S(2)}) copy-start(f32[32,1,4,4]{0,3,2,1:T(4,128)} %param.20) | copy-start | bytes 6148
  28.4 18.0 %collective-permute-start = (f32[4,128,256]{2,1,0:T(8,128)}, f32[4,128,256]{2,1,0:T(8,128)}, u32[]{:S(2)}, u32[]{:S(2)}) collective-permute-start(f32[4,128,256]{2,1,0:T(8,128)} %pad_maximum_fusion), channel_id=1, source_target_pairs={{0,1},{1,2},{2,3},{3,4},{4,5},{5,6},{6,7},{7,8},{8,9},{9,10},{10,1... | collective-permute-start | bytes 1572872 | tf_op jit(solution)/shard_map/ppermute | solution.py:13
  32.9 1.5 copy-start.3
  33.0 1.9 %copy-start.23 = (f32[16,32]{1,0:T(8,128)}, f32[16,32]{1,0:T(8,128)S(1)}, u32[]{:S(2)}) copy-start(f32[16,32]{1,0:T(8,128)S(1)} %sqrt.23) | copy-start | bytes 6148
  33.1 1.9 %copy-start.28 = (pred[32,32]{1,0:T(8,128)(4,1)}, pred[32,32]{1,0:T(8,128)(4,1)S(1)}, u32[]{:S(2)}) copy-start(pred[32,32]{1,0:T(8,128)(4,1)S(1)} %get-tuple-element.55) | copy-start | bytes 3076
  33.3 1.7 %copy-start.26 = (f32[16,32]{1,0:T(8,128)}, f32[16,32]{1,0:T(8,128)S(1)}, u32[]{:S(2)}) copy-start(f32[16,32]{1,0:T(8,128)S(1)} %reduce_window_sum.22) | copy-start | bytes 6148
  35.0 1.2 copy-start.8
  48.5 17.1 %collective-permute-start.1 = (f32[4,128,256]{1,2,0:T(8,128)S(1)}, f32[4,128,256]{1,2,0:T(8,128)S(1)}, u32[]{:S(2)}, u32[]{:S(2)}) collective-permute-start(f32[4,128,256]{1,2,0:T(8,128)S(1)} %pad_maximum_fusion.1), channel_id=1, source_target_pairs={{0,2},{1,3},{2,4},{3,5},{4,6},{5,7},{6,8},{7,9},{8,10},{9,11},{10,... | collective-permute-start | bytes 1572872 | tf_op jit(solution)/shard_map/ppermute | solution.py:13
  52.6 15.8 %copy-start.13 = (bf16[1,128,128]{2,1,0:T(8,128)(2,1)S(1)}, bf16[1,128,128]{2,1,0:T(8,128)(2,1)}, u32[]{:S(2)}) copy-start(bf16[1,128,128]{2,1,0:T(8,128)(2,1)} %get-tuple-element.41) | copy-start | bytes 98308
  52.6 15.8 %copy-start.14 = (bf16[1,128,128]{2,1,0:T(8,128)(2,1)S(1)}, bf16[1,128,128]{2,1,0:T(8,128)(2,1)}, u32[]{:S(2)}) copy-start(bf16[1,128,128]{2,1,0:T(8,128)(2,1)} %get-tuple-element.42) | copy-start | bytes 98308
  52.6 15.8 %copy-start.15 = (bf16[1,128,128]{2,1,0:T(8,128)(2,1)S(1)}, bf16[1,128,128]{2,1,0:T(8,128)(2,1)}, u32[]{:S(2)}) copy-start(bf16[1,128,128]{2,1,0:T(8,128)(2,1)} %get-tuple-element.43) | copy-start | bytes 98308
  52.6 15.8 %copy-start.16 = (bf16[1,128,128]{2,1,0:T(8,128)(2,1)S(1)}, bf16[1,128,128]{2,1,0:T(8,128)(2,1)}, u32[]{:S(2)}) copy-start(bf16[1,128,128]{2,1,0:T(8,128)(2,1)} %get-tuple-element.44) | copy-start | bytes 98308
  66.2 2.9 %copy-start.18 = (pred[128,128]{1,0:T(8,128)(4,1)S(1)}, pred[128,128]{1,0:T(8,128)(4,1)}, u32[]{:S(2)}) copy-start(pred[128,128]{1,0:T(8,128)(4,1)} %copy-done.17) | copy-start | bytes 49156
  66.2 2.9 %copy-start.21 = (f32[4,128]{1,0:T(4,128)S(1)}, f32[4,128]{1,0:T(4,128)}, u32[]{:S(2)}) copy-start(f32[4,128]{1,0:T(4,128)} %copy-done.20) | copy-start | bytes 6148
  67.1 14.1 %collective-permute-start.2 = (f32[4,128,256]{1,2,0:T(8,128)}, f32[4,128,256]{1,2,0:T(8,128)}, u32[]{:S(2)}, u32[]{:S(2)}) collective-permute-start(f32[4,128,256]{1,2,0:T(8,128)} %pad_maximum_fusion.2), channel_id=1, source_target_pairs={{0,4},{1,5},{2,6},{3,7},{4,8},{5,9},{6,10},{7,11},{8,12},{9,13},{1... | collective-permute-start | bytes 1572872 | tf_op jit(solution)/shard_map/ppermute | solution.py:13
  82.8 12.8 %copy-start.5 = (f32[1,128,128]{2,1,0:T(8,128)S(1)}, f32[1,128,128]{2,1,0:T(8,128)}, u32[]{:S(2)}) copy-start(f32[1,128,128]{2,1,0:T(8,128)} %get-tuple-element.31) | copy-start | bytes 196612
  82.8 12.8 %copy-start.6 = (f32[1,128,128]{2,1,0:T(8,128)S(1)}, f32[1,128,128]{2,1,0:T(8,128)}, u32[]{:S(2)}) copy-start(f32[1,128,128]{2,1,0:T(8,128)} %get-tuple-element.32) | copy-start | bytes 196612
  83.0 9.8 %collective-permute-start.3 = (f32[4,128,128]{1,2,0:T(8,128)S(1)}, f32[4,128,128]{1,2,0:T(8,128)S(1)}, u32[]{:S(2)}, u32[]{:S(2)}) collective-permute-start(f32[4,128,128]{1,2,0:T(8,128)S(1)} %add.162), channel_id=1, source_target_pairs={{0,8},{1,9},{2,10},{3,11},{4,12},{5,13},{6,14},{7,15},{16,24},{17,... | collective-permute-start | bytes 786440 | tf_op jit(solution)/shard_map/ppermute | solution.py:13
  84.6 20.2 %copy-start.30 = (f32[128]{0:T(128)S(1)}, f32[128]{0:T(128)}, u32[]{:S(2)}) copy-start(f32[128]{0:T(128)} %param.16) | copy-start | bytes 1540
  93.5 27.8 %copy-start.9 = (bf16[4,32,128]{2,1,0:T(8,128)(2,1)S(1)}, bf16[4,32,128]{2,1,0:T(8,128)(2,1)}, u32[]{:S(2)}) copy-start(bf16[4,32,128]{2,1,0:T(8,128)(2,1)} %get-tuple-element.45) | copy-start | bytes 98308
  93.5 27.8 %copy-start.10 = (bf16[4,32,128]{2,1,0:T(8,128)(2,1)S(1)}, bf16[4,32,128]{2,1,0:T(8,128)(2,1)}, u32[]{:S(2)}) copy-start(bf16[4,32,128]{2,1,0:T(8,128)(2,1)} %get-tuple-element.46) | copy-start | bytes 98308
  93.5 27.8 %copy-start.11 = (bf16[4,32,128]{2,1,0:T(8,128)(2,1)S(1)}, bf16[4,32,128]{2,1,0:T(8,128)(2,1)}, u32[]{:S(2)}) copy-start(bf16[4,32,128]{2,1,0:T(8,128)(2,1)} %get-tuple-element.47) | copy-start | bytes 98308
  93.5 27.8 %copy-start.12 = (bf16[4,32,128]{2,1,0:T(8,128)(2,1)S(1)}, bf16[4,32,128]{2,1,0:T(8,128)(2,1)}, u32[]{:S(2)}) copy-start(bf16[4,32,128]{2,1,0:T(8,128)(2,1)} %get-tuple-element.48) | copy-start | bytes 98308
  93.5 27.8 %copy-start.4 = (f32[4,128,128]{2,1,0:T(8,128)S(1)}, f32[4,128,128]{2,1,0:T(8,128)}, u32[]{:S(2)}) copy-start(f32[4,128,128]{2,1,0:T(8,128)} %copy-done.3) | copy-start | bytes 786436
  93.5 27.8 %copy-start.24 = (f32[16,32]{1,0:T(8,128)S(1)}, f32[16,32]{1,0:T(8,128)}, u32[]{:S(2)}) copy-start(f32[16,32]{1,0:T(8,128)} %copy-done.23) | copy-start | bytes 6148
  93.5 27.8 %copy-start.27 = (f32[16,32]{1,0:T(8,128)S(1)}, f32[16,32]{1,0:T(8,128)}, u32[]{:S(2)}) copy-start(f32[16,32]{1,0:T(8,128)} %copy-done.26) | copy-start | bytes 6148
  93.6 27.8 %copy-start.29 = (pred[32,32]{1,0:T(8,128)(4,1)S(1)}, pred[32,32]{1,0:T(8,128)(4,1)}, u32[]{:S(2)}) copy-start(pred[32,32]{1,0:T(8,128)(4,1)} %copy-done.28) | copy-start | bytes 3076
  93.6 10.5 %collective-permute-start.4 = (f32[4,128,128]{1,2,0:T(8,128)S(1)}, f32[4,128,128]{1,2,0:T(8,128)S(1)}, u32[]{:S(2)}, u32[]{:S(2)}) collective-permute-start(f32[4,128,128]{1,2,0:T(8,128)S(1)} %convolution_add_fusion.7), channel_id=1, source_target_pairs={{0,1},{1,2},{2,3},{3,4},{4,5},{5,6},{6,7},{7,8},{8,9},{9,10},{10,1... | collective-permute-start | bytes 786440 | tf_op jit(solution)/shard_map/ppermute | solution.py:13
  105.7 32.8 %all-to-all-start = ((bf16[1,32,4,512]{3,2,0,1:T(4,128)(2,1)}), bf16[1,32,4,512]{3,2,0,1:T(4,128)(2,1)S(1)}, u32[]{:S(2)}, u32[]{:S(2)}) async-start(bf16[1,32,4,512]{3,2,0,1:T(4,128)(2,1)} %bitcast.66), calls=%async_computation | async-start | bytes 262144 | tf_op jit(solution)/shard_map/all_to_all | solution.py:184
  121.4 17.8 %copy-start.31 = (f32[128]{0:T(128)S(1)}, f32[128]{0:T(128)}, u32[]{:S(2)}) copy-start(f32[128]{0:T(128)} %param.21) | copy-start | bytes 1540

commit v2 on v1

--- a/solution.py
+++ b/solution.py
@@ -18,17 +18,16 @@
 
 
 def unit_lower_inverse(system):
-    batch = system.shape[:-2]
     size = system.shape[-1]
     base = min(BASE_BLOCK, size)
-    count = size // base
-    assert count * base == size and count & (count - 1) == 0
-    eye = jnp.eye(base, dtype=jnp.float32)
-    grid = system.reshape(batch + (count, base, count, base))
-    diagonal = jnp.moveaxis(jnp.diagonal(grid, axis1=-4, axis2=-2), -1, -3)
-    lower = diagonal - eye
-    inverse = eye - lower
-    power = lower
+    assert size % base == 0
+    rows = lax.broadcasted_iota(jnp.int32, (size, size), 0)
+    cols = lax.broadcasted_iota(jnp.int32, (size, size), 1)
+    eye = jnp.eye(size, dtype=jnp.float32)
+    lower = system - eye
+    diagonal = jnp.where(rows // base == cols // base, lower, 0.0)
+    inverse = eye - diagonal
+    power = diagonal
     reach = 2
     while reach < base:
         power = matmul("...ij,...jk->...ik", power, power)
@@ -36,20 +35,13 @@
         reach *= 2
     width = base
     while width < size:
-        pairs = size // (2 * width)
-        grid = system.reshape(batch + (pairs, 2, width, pairs, 2, width))
-        coupling = jnp.moveaxis(jnp.diagonal(grid, axis1=-6, axis2=-3), -1, -5)[..., 1, :, 0, :]
-        halves = inverse.reshape(batch + (pairs, 2, width, width))
-        upper_inverse = halves[..., 0, :, :]
-        lower_inverse = halves[..., 1, :, :]
-        mixed = -matmul(
-            "...ij,...jk->...ik", matmul("...ij,...jk->...ik", lower_inverse, coupling), upper_inverse
+        inside = (rows // (2 * width) == cols // (2 * width)) & (rows // width != cols // width)
+        coupling = jnp.where(inside, lower, 0.0)
+        inverse = inverse - matmul(
+            "...ij,...jk->...ik", matmul("...ij,...jk->...ik", inverse, coupling), inverse
         )
-        top = jnp.concatenate([upper_inverse, jnp.zeros_like(upper_inverse)], axis=-1)
-        bottom = jnp.concatenate([mixed, lower_inverse], axis=-1)
-        inverse = jnp.concatenate([top, bottom], axis=-2)
         width *= 2
-    return inverse.reshape(batch + (size, size))
+    return inverse
 
 
 def block_system(key_block, log_decay, beta_block):
@@ -147,7 +139,7 @@
     row_count, segment, features = query_row.shape
     head_size = gain_row.shape[0]
     head_count = features // head_size
-    line_count = lax.axis_size("line")
+    line_count = lax.axis_size("z") * lax.axis_size("core")
     total_rows = query_col.shape[0]
     column_count = query_col.shape[2]
 
@@ -180,8 +172,14 @@
     values_col = (
         head_norm(row_scan, gain_row).reshape(row_count, segment, features).astype(jnp.bfloat16)
     )
-    arranged = values_col.reshape(row_count, line_count, segment // line_count, features)
-    column_values = lax.all_to_all(arranged, "line", split_axis=1, concat_axis=0, tiled=True)
+    chip_count = lax.axis_size("z")
+    core_count = lax.axis_size("core")
+    arranged = values_col.reshape(
+        row_count, chip_count, core_count, segment // line_count, features
+    )
+    by_chip = lax.all_to_all(arranged, "z", split_axis=1, concat_axis=0, tiled=True)
+    by_core = lax.all_to_all(by_chip, "core", split_axis=2, concat_axis=1, tiled=True)
+    column_values = by_core.reshape(total_rows, column_count, features)
 
     col_out = matmul(
         "bij,bjv->biv",
@@ -192,27 +190,34 @@
     normed = (
         head_norm(col_scan, gain_col)
         .transpose(1, 0, 2, 3)
-        .reshape(total_rows, 1, column_count, features)
+        .reshape(chip_count, core_count, 1, column_count, features)
         .astype(jnp.bfloat16)
     )
-    returned = lax.all_to_all(normed, "line", split_axis=0, concat_axis=1, tiled=True)
-    return returned.reshape(row_count, segment, features)
+    to_core = lax.all_to_all(normed, "core", split_axis=1, concat_axis=2, tiled=True)
+    to_chip = lax.all_to_all(to_core, "z", split_axis=0, concat_axis=1, tiled=True)
+    return to_chip.reshape(row_count, segment, features)
 
 
 def solution(mesh):
+    line_devices, scan_devices = mesh.devices.shape
+    cores = 2 if line_devices % 2 == 0 else 1
+    split = jax.sharding.Mesh(
+        mesh.devices.reshape(line_devices // cores, cores, scan_devices), ("z", "core", "scan")
+    )
+    line = ("z", "core")
     placed = (
-        P("line", "scan", None),
-        P("line", "scan", None),
-        P("line", "scan", None),
-        P("line", "scan", None),
-        P("line", "scan", None),
+        P(line, "scan", None),
+        P(line, "scan", None),
+        P(line, "scan", None),
+        P(line, "scan", None),
+        P(line, "scan", None),
         P(),
-        P(None, "scan", "line", None),
-        P(None, "scan", "line", None),
-        P(None, "scan", "line", None),
-        P(None, "scan", "line", None),
+        P(None, "scan", line, None),
+        P(None, "scan", line, None),
+        P(None, "scan", line, None),
+        P(None, "scan", line, None),
         P(),
     )
     return jax.shard_map(
-        shards, mesh=mesh, in_specs=placed, out_specs=P("line", "scan", None), check_vma=False
-    )
+        shards, mesh=split, in_specs=placed, out_specs=P(line, "scan", None), check_vma=False
+    )

time: 161 us -> 145 us (0.901)
  local copies, waits for them, and re-layouts: 23.5 us -> 8.62 us
  blocking collectives: 20.2 us -> 26.3 us
  waiting for transfers between devices: 65 us -> 61.4 us
  other arithmetic: 4.77 us -> 2.68 us
    reshape x9 -> x1, local copies, waits for them, and re-layouts: 9.74 us -> 0.69 us  [shards(): return to_chip.reshape(row_count, segment, features)]
    all_to_all x1 -> x3, blocking collectives: 20.2 us -> 26.3 us  [the longest x1 18.6 us: shards(): lax.all_to_all(to_core, 'z', split_axis=0, concat_axis=1, tiled=True)]
    gather x6 -> x0, local copies, waits for them, and re-layouts: 5.56 us -> none  [the longest x4 2.84 us: unit_lower_inverse(): jnp.diagonal(grid, axis1=-6, axis2=-3)]
    all_to_all x1, waiting for transfers between devices: 16.2 us -> 11.9 us  [shards(): lax.all_to_all(arranged, 'z', split_axis=1, concat_axis=0, tiled=True)]
    unnamed x68 -> x34, local copies, waits for them, and re-layouts: 0.93 us -> 5.11 us
    slice x4 -> x1, local copies, waits for them, and re-layouts: 1.82 us -> 0.03 us  [the longest x2 1.14 us: unit_lower_inverse(): jnp.moveaxis(jnp.diagonal(grid, axis1=-6, axis2=-3), -1, -5)]
    dot_general x36, matrix products: 19.1 us -> 17.5 us  [matmul(): return jnp.einsum(spec, left, right, precision=HIGHEST)]
  transfers between devices with their start and end apart: 6 -> 6, of which waited for: 6 -> 6; matrix products, arithmetic and copies ran while one was open for 6% -> 5% of each run, Pallas kernels for 0% -> 0%
where the time goes in v2:
time: 145 us; the launch traced here: 144 us
  waiting for transfers between devices  61.4 us (42%)
  starting transfers between devices  26.6 us (18%)
  blocking collectives  26.3 us (18%)
  matrix products  17.5 us (12%)
  local copies, waits for them, and re-layouts  8.62 us (6%)
  other arithmetic  2.68 us (2%)
    ppermute x5, waiting for transfers between devices, from_behind(): return lax.ppermute(block, axis, route)  49.6 us
    all_to_all x1, blocking collectives, shards(): lax.all_to_all(to_core, 'z', split_axis=0, concat_axis=1, tiled=True)  18.6 us
    dot_general x36, matrix products, matmul(): return jnp.einsum(spec, left, right, precision=HIGHEST)  17.5 us
    all_to_all x1, starting transfers between devices, shards(): lax.all_to_all(arranged, 'z', split_axis=1, concat_axis=0, tiled=True)  15.3 us
    all_to_all x1, waiting for transfers between devices, shards(): lax.all_to_all(arranged, 'z', split_axis=1, concat_axis=0, tiled=True)  11.9 us
    ppermute x5, starting transfers between devices, from_behind(): return lax.ppermute(block, axis, route)  11.3 us
    unnamed x34, local copies, waits for them, and re-layouts  5.11 us
    all_to_all x1, blocking collectives, shards(): lax.all_to_all(by_chip, 'core', split_axis=2, concat_axis=1, tiled=True)  3.84 us
  transfers between devices with their start and end apart: 6, of which 6 were waited for; matrix products, arithmetic and copies ran while one was open for 5% of the time, Pallas kernels for 0%

profile of v2, /device:TPU:6, one launch (start us, length us, event | category | flops | bytes accessed | tf_op | source)
XLA Modules:
  0.0 143.8 jit_solution(8294283855989908230)
XLA Ops:
  0.2 0.8 fusion.84
  1.2 0.7 copy-done.13
  1.9 0.3 reduce_window_sum.23
  2.2 0.7 copy-done.5
  2.8 0.8 fusion.6
  3.6 0.3 fusion.58
  3.9 0.4 fusion.32
  4.3 0.4 convolution_add_fusion.2
  4.7 0.4 fusion.89
  5.3 0.4 fusion.90
  5.6 0.4 convolution_add_fusion.1
  6.0 0.4 convolution_add_fusion
  6.4 0.4 fusion.18
  6.8 0.4 convolution_subtract_fusion.2
  7.2 0.4 fusion.16
  7.6 0.4 convolution_subtract_fusion.1
  8.1 0.4 fusion.14
  8.5 0.4 convolution_subtract_fusion
  8.9 0.4 copy-done.1
  9.6 0.3 broadcast_multiply_fusion
  9.9 0.6 fusion.7
  10.5 0.8 fusion.26
  11.2 0.7 convolution_subtract_fusion.4
  12.2 3.5 %collective-permute-start = (f32[4,128,256]{2,1,0:T(8,128)S(1)}, f32[4,128,256]{2,1,0:T(8,128)S(1)}, u32[]{:S(2)}, u32[]{:S(2)}) collective-permute-start(f32[4,128,256]{2,1,0:T(8,128)S(1)} %pad_maximum_fusion), channel_id=1, source_target_pairs={{0,1},{1,2},{2,3},{3,4},{4,5},{5,6},{6,7},{7,8},{8,9},{9,10},{10,1... | collective-permute-start | bytes 1572872 | tf_op jit(solution)/shard_map/ppermute | solution.py:13
  15.8 0.6 copy-done.8
  17.0 0.7 copy-done
  17.7 0.5 convolution_multiply_fusion.1
  18.3 0.7 copy-done.4
  19.0 0.7 fusion.4
  19.7 0.4 fusion.35
  20.1 0.4 fusion.87
  20.4 0.4 fusion.88
  20.8 9.0 %collective-permute-done = f32[4,128,256]{2,1,0:T(8,128)S(1)} collective-permute-done((f32[4,128,256]{2,1,0:T(8,128)S(1)}, f32[4,128,256]{2,1,0:T(8,128)S(1)}, u32[]{:S(2)}, u32[]{:S(2)}) %collective-permute-start) | collective-permute-done | bytes 524320 | tf_op jit(solution)/shard_map/ppermute | solution.py:13
  29.9 1.0 fusion.91
  31.0 3.3 %collective-permute-start.1 = (f32[4,128,256]{1,2,0:T(8,128)S(1)}, f32[4,128,256]{1,2,0:T(8,128)S(1)}, u32[]{:S(2)}, u32[]{:S(2)}) collective-permute-start(f32[4,128,256]{1,2,0:T(8,128)S(1)} %pad_maximum_fusion.1), channel_id=1, source_target_pairs={{0,2},{1,3},{2,4},{3,5},{4,6},{5,7},{6,8},{7,9},{8,10},{9,11},{10,... | collective-permute-start | bytes 1572872 | tf_op jit(solution)/shard_map/ppermute | solution.py:13
  34.4 0.4 convolution_add_fusion.5
  34.8 0.4 convolution_add_fusion.4
  35.2 13.0 %collective-permute-done.1 = f32[4,128,256]{1,2,0:T(8,128)S(1)} collective-permute-done((f32[4,128,256]{1,2,0:T(8,128)S(1)}, f32[4,128,256]{1,2,0:T(8,128)S(1)}, u32[]{:S(2)}, u32[]{:S(2)}) %collective-permute-start.1) | collective-permute-done | bytes 524320 | tf_op jit(solution)/shard_map/ppermute | solution.py:13
  48.2 0.6 fusion.76
  48.9 1.3 collective-permute-start.2
  50.3 0.6 fusion.28
  50.9 0.4 convolution_add_fusion.3
  51.3 11.4 %collective-permute-done.2 = f32[4,128,256]{1,2,0:T(8,128)S(1)} collective-permute-done((f32[4,128,256]{1,2,0:T(8,128)S(1)}, f32[4,128,256]{1,2,0:T(8,128)S(1)}, u32[]{:S(2)}, u32[]{:S(2)}) %collective-permute-start.2) | collective-permute-done | bytes 524320 | tf_op jit(solution)/shard_map/ppermute | solution.py:13
  62.7 0.6 fusion.74
  63.5 1.3 collective-permute-start.3
  64.9 0.4 fusion.21
  65.3 8.1 %collective-permute-done.3 = f32[4,128,128]{1,2,0:T(8,128)S(1)} collective-permute-done((f32[4,128,128]{1,2,0:T(8,128)S(1)}, f32[4,128,128]{1,2,0:T(8,128)S(1)}, u32[]{:S(2)}, u32[]{:S(2)}) %collective-permute-start.3) | collective-permute-done | bytes 262176 | tf_op jit(solution)/shard_map/ppermute | solution.py:13
  73.3 0.7 convolution_add_fusion.7
  74.0 1.9 %collective-permute-start.4 = (f32[4,128,128]{1,2,0:T(8,128)S(1)}, f32[4,128,128]{1,2,0:T(8,128)S(1)}, u32[]{:S(2)}, u32[]{:S(2)}) collective-permute-start(f32[4,128,128]{1,2,0:T(8,128)S(1)} %convolution_add_fusion.7), channel_id=1, source_target_pairs={{0,1},{1,2},{2,3},{3,4},{4,5},{5,6},{6,7},{7,8},{8,9},{9,10},{10,1... | collective-permute-start | bytes 786440 | tf_op jit(solution)/shard_map/ppermute | solution.py:13
  75.9 0.4 convolution_subtract_fusion.5
  76.3 8.0 %collective-permute-done.4 = f32[4,128,128]{1,2,0:T(8,128)S(1)} collective-permute-done((f32[4,128,128]{1,2,0:T(8,128)S(1)}, f32[4,128,128]{1,2,0:T(8,128)S(1)}, u32[]{:S(2)}, u32[]{:S(2)}) %collective-permute-start.4) | collective-permute-done | bytes 262176 | tf_op jit(solution)/shard_map/ppermute | solution.py:13
  84.4 0.7 multiply_reduce_fusion.1
  85.1 0.6 copy-done.14
  85.9 0.7 convert_element_type.85
  86.7 15.3 %all-to-all-start = ((bf16[1,16,2,4,512]{4,3,2,0,1:T(4,128)(2,1)}), bf16[1,16,2,4,512]{4,3,2,0,1:T(4,128)(2,1)S(1)}, u32[]{:S(2)}, u32[]{:S(2)}) async-start(bf16[1,16,2,4,512]{4,3,2,0,1:T(4,128)(2,1)} %bitcast.29), calls=%async_computation | async-start | bytes 262144 | tf_op jit(solution)/shard_map/all_to_all | solution.py:180
  102.0 0.4 convolution_multiply_fusion.4
  102.4 0.4 convolution_subtract_fusion.3
  102.8 0.4 convolution_multiply_fusion.2
  103.2 11.9 %all-to-all-done = bf16[1,16,2,4,512]{4,3,2,0,1:T(4,128)(2,1)S(1)} async-done(((bf16[1,16,2,4,512]{4,3,2,0,1:T(4,128)(2,1)}), bf16[1,16,2,4,512]{4,3,2,0,1:T(4,128)(2,1)S(1)}, u32[]{:S(2)}, u32[]{:S(2)}) %all-to-all-start) | async-done | bytes 131104 | tf_op jit(solution)/shard_map/all_to_all | solution.py:180
  115.1 3.8 %all_to_all.42 = bf16[16,1,2,4,512]{4,3,0,1,2:T(4,128)(2,1)S(1)} all-to-all(bf16[16,1,2,4,512]{4,3,0,1,2:T(4,128)(2,1)S(1)} %copy.91), channel_id=1, replica_groups=mesh['z'=16,'core'=2,'scan'=16] {'core'}, dimensions={2} | all-to-all | bytes 262144 | tf_op jit(solution)/shard_map/all_to_all | solution.py:181
  119.8 0.5 copy-done.15
  120.7 3.8 %all_to_all.43 = bf16[16,2,1,4,512]{4,3,0,2,1:T(4,128)(2,1)S(1)} all-to-all(bf16[16,2,1,4,512]{4,3,0,2,1:T(4,128)(2,1)S(1)} %copy.96), channel_id=1, replica_groups=mesh['z'=16,'core'=2,'scan'=16] {'core'}, dimensions={1} | all-to-all | bytes 262144 | tf_op jit(solution)/shard_map/all_to_all | solution.py:196
  124.5 18.6 %all_to_all.44 = bf16[16,1,2,4,512]{4,3,2,1,0:T(4,128)(2,1)S(1)} all-to-all(bf16[16,1,2,4,512]{4,3,2,1,0:T(4,128)(2,1)S(1)} %copy.97), channel_id=1, replica_groups=mesh['z'=16,'core'=2,'scan'=16] {'z'}, dimensions={0} | all-to-all | bytes 262144 | tf_op jit(solution)/shard_map/all_to_all | solution.py:197
  143.1 0.7 reshape.270
  (85 shorter events, 3.6 us)
Async XLA Ops:
  1.2 0.7 copy-start.13
  2.2 0.7 copy-start.5
  8.4 0.9 copy-start.1
  12.1 4.5 %copy-start.2 = (bf16[32,1,4,512]{3,2,1,0:T(4,128)(2,1)S(1)}, bf16[32,1,4,512]{3,2,1,0:T(4,128)(2,1)}, u32[]{:S(2)}) copy-start(bf16[32,1,4,512]{3,2,1,0:T(4,128)(2,1)} %param.18) | copy-start | bytes 393220
  12.2 17.7 %collective-permute-start = (f32[4,128,256]{2,1,0:T(8,128)S(1)}, f32[4,128,256]{2,1,0:T(8,128)S(1)}, u32[]{:S(2)}, u32[]{:S(2)}) collective-permute-start(f32[4,128,256]{2,1,0:T(8,128)S(1)} %pad_maximum_fusion), channel_id=1, source_target_pairs={{0,1},{1,2},{2,3},{3,4},{4,5},{5,6},{6,7},{7,8},{8,9},{9,10},{10,1... | collective-permute-start | bytes 1572872 | tf_op jit(solution)/shard_map/ppermute | solution.py:13
  15.7 0.7 copy-start.8
  16.6 1.7 %copy-start.9 = (f32[16,32]{1,0:T(8,128)}, f32[16,32]{1,0:T(8,128)S(1)}, u32[]{:S(2)}) copy-start(f32[16,32]{1,0:T(8,128)S(1)} %reduce_window_sum.22) | copy-start | bytes 6148
  16.7 1.6 %copy-start.11 = (pred[32,32]{1,0:T(8,128)(4,1)}, pred[32,32]{1,0:T(8,128)(4,1)S(1)}, u32[]{:S(2)}) copy-start(pred[32,32]{1,0:T(8,128)(4,1)S(1)} %get-tuple-element.53) | copy-start | bytes 3076
  16.7 0.9 copy-start
  17.6 0.7 copy-start.6
  18.3 0.7 copy-start.4
  31.0 3.4 %copy-start.3 = (bf16[32,1,4,512]{3,2,1,0:T(4,128)(2,1)S(1)}, bf16[32,1,4,512]{3,2,1,0:T(4,128)(2,1)}, u32[]{:S(2)}) copy-start(bf16[32,1,4,512]{3,2,1,0:T(4,128)(2,1)} %param.17) | copy-start | bytes 393220
  31.0 17.2 %collective-permute-start.1 = (f32[4,128,256]{1,2,0:T(8,128)S(1)}, f32[4,128,256]{1,2,0:T(8,128)S(1)}, u32[]{:S(2)}, u32[]{:S(2)}) collective-permute-start(f32[4,128,256]{1,2,0:T(8,128)S(1)} %pad_maximum_fusion.1), channel_id=1, source_target_pairs={{0,2},{1,3},{2,4},{3,5},{4,6},{5,7},{6,8},{7,9},{8,10},{9,11},{10,... | collective-permute-start | bytes 1572872 | tf_op jit(solution)/shard_map/ppermute | solution.py:13
  48.9 13.8 %collective-permute-start.2 = (f32[4,128,256]{1,2,0:T(8,128)S(1)}, f32[4,128,256]{1,2,0:T(8,128)S(1)}, u32[]{:S(2)}, u32[]{:S(2)}) collective-permute-start(f32[4,128,256]{1,2,0:T(8,128)S(1)} %pad_maximum_fusion.2), channel_id=1, source_target_pairs={{0,4},{1,5},{2,6},{3,7},{4,8},{5,9},{6,10},{7,11},{8,12},{9,13},{1... | collective-permute-start | bytes 1572872 | tf_op jit(solution)/shard_map/ppermute | solution.py:13
  63.5 9.8 %collective-permute-start.3 = (f32[4,128,128]{1,2,0:T(8,128)S(1)}, f32[4,128,128]{1,2,0:T(8,128)S(1)}, u32[]{:S(2)}, u32[]{:S(2)}) collective-permute-start(f32[4,128,128]{1,2,0:T(8,128)S(1)} %add.148), channel_id=1, source_target_pairs={{0,8},{1,9},{2,10},{3,11},{4,12},{5,13},{6,14},{7,15},{16,24},{17,... | collective-permute-start | bytes 786440 | tf_op jit(solution)/shard_map/ppermute | solution.py:13
  74.0 10.4 %collective-permute-start.4 = (f32[4,128,128]{1,2,0:T(8,128)S(1)}, f32[4,128,128]{1,2,0:T(8,128)S(1)}, u32[]{:S(2)}, u32[]{:S(2)}) collective-permute-start(f32[4,128,128]{1,2,0:T(8,128)S(1)} %convolution_add_fusion.7), channel_id=1, source_target_pairs={{0,1},{1,2},{2,3},{3,4},{4,5},{5,6},{6,7},{7,8},{8,9},{9,10},{10,1... | collective-permute-start | bytes 786440 | tf_op jit(solution)/shard_map/ppermute | solution.py:13
  85.0 0.7 copy-start.14
  86.7 15.3 %copy-start.7 = (f32[16,32]{1,0:T(8,128)S(1)}, f32[16,32]{1,0:T(8,128)}, u32[]{:S(2)}) copy-start(f32[16,32]{1,0:T(8,128)} %copy-done.6) | copy-start | bytes 6148
  86.7 15.3 %copy-start.10 = (f32[16,32]{1,0:T(8,128)S(1)}, f32[16,32]{1,0:T(8,128)}, u32[]{:S(2)}) copy-start(f32[16,32]{1,0:T(8,128)} %copy-done.9) | copy-start | bytes 6148
  86.7 15.3 %copy-start.12 = (pred[32,32]{1,0:T(8,128)(4,1)S(1)}, pred[32,32]{1,0:T(8,128)(4,1)}, u32[]{:S(2)}) copy-start(pred[32,32]{1,0:T(8,128)(4,1)} %copy-done.11) | copy-start | bytes 3076
  86.7 28.4 %all-to-all-start = ((bf16[1,16,2,4,512]{4,3,2,0,1:T(4,128)(2,1)}), bf16[1,16,2,4,512]{4,3,2,0,1:T(4,128)(2,1)S(1)}, u32[]{:S(2)}, u32[]{:S(2)}) async-start(bf16[1,16,2,4,512]{4,3,2,0,1:T(4,128)(2,1)} %bitcast.29), calls=%async_computation | async-start | bytes 262144 | tf_op jit(solution)/shard_map/all_to_all | solution.py:180
  119.6 0.7 copy-start.15

commit v3 on v2

--- a/solution.py
+++ b/solution.py
@@ -5,6 +5,8 @@
 
 HIGHEST = lax.Precision.HIGHEST
 BASE_BLOCK = 16
+INNER = ("near", "core")
+LINE = ("outer",) + INNER
 
 
 def from_behind(block, axis, distance):
@@ -139,7 +141,7 @@
     row_count, segment, features = query_row.shape
     head_size = gain_row.shape[0]
     head_count = features // head_size
-    line_count = lax.axis_size("z") * lax.axis_size("core")
+    line_count = lax.axis_size(LINE)
     total_rows = query_col.shape[0]
     column_count = query_col.shape[2]
 
@@ -172,14 +174,14 @@
     values_col = (
         head_norm(row_scan, gain_row).reshape(row_count, segment, features).astype(jnp.bfloat16)
     )
-    chip_count = lax.axis_size("z")
-    core_count = lax.axis_size("core")
+    outer_count = lax.axis_size("outer")
+    inner_count = lax.axis_size(INNER)
     arranged = values_col.reshape(
-        row_count, chip_count, core_count, segment // line_count, features
-    )
-    by_chip = lax.all_to_all(arranged, "z", split_axis=1, concat_axis=0, tiled=True)
-    by_core = lax.all_to_all(by_chip, "core", split_axis=2, concat_axis=1, tiled=True)
-    column_values = by_core.reshape(total_rows, column_count, features)
+        1, 1, outer_count, inner_count, segment // line_count, features
+    )
+    by_inner = lax.all_to_all(arranged, INNER, split_axis=3, concat_axis=1, tiled=True)
+    by_outer = lax.all_to_all(by_inner, "outer", split_axis=2, concat_axis=0, tiled=True)
+    column_values = by_outer.reshape(total_rows, column_count, features)
 
     col_out = matmul(
         "bij,bjv->biv",
@@ -190,34 +192,36 @@
     normed = (
         head_norm(col_scan, gain_col)
         .transpose(1, 0, 2, 3)
-        .reshape(chip_count, core_count, 1, column_count, features)
+        .reshape(outer_count, inner_count, 1, 1, column_count, features)
         .astype(jnp.bfloat16)
     )
-    to_core = lax.all_to_all(normed, "core", split_axis=1, concat_axis=2, tiled=True)
-    to_chip = lax.all_to_all(to_core, "z", split_axis=0, concat_axis=1, tiled=True)
-    return to_chip.reshape(row_count, segment, features)
+    to_inner = lax.all_to_all(normed, INNER, split_axis=1, concat_axis=3, tiled=True)
+    to_outer = lax.all_to_all(to_inner, "outer", split_axis=0, concat_axis=2, tiled=True)
+    return to_outer.reshape(row_count, segment, features)
 
 
 def solution(mesh):
     line_devices, scan_devices = mesh.devices.shape
     cores = 2 if line_devices % 2 == 0 else 1
+    chips = line_devices // cores
+    near = 4 if chips % 4 == 0 else 1
     split = jax.sharding.Mesh(
-        mesh.devices.reshape(line_devices // cores, cores, scan_devices), ("z", "core", "scan")
-    )
-    line = ("z", "core")
+        mesh.devices.reshape(chips // near, near, cores, scan_devices),
+        ("outer", "near", "core", "scan"),
+    )
     placed = (
-        P(line, "scan", None),
-        P(line, "scan", None),
-        P(line, "scan", None),
-        P(line, "scan", None),
-        P(line, "scan", None),
+        P(LINE, "scan", None),
+        P(LINE, "scan", None),
+        P(LINE, "scan", None),
+        P(LINE, "scan", None),
+        P(LINE, "scan", None),
         P(),
-        P(None, "scan", line, None),
-        P(None, "scan", line, None),
-        P(None, "scan", line, None),
-        P(None, "scan", line, None),
+        P(None, "scan", LINE, None),
+        P(None, "scan", LINE, None),
+        P(None, "scan", LINE, None),
+        P(None, "scan", LINE, None),
         P(),
     )
     return jax.shard_map(
-        shards, mesh=split, in_specs=placed, out_specs=P(line, "scan", None), check_vma=False
-    )
+        shards, mesh=split, in_specs=placed, out_specs=P(LINE, "scan", None), check_vma=False
+    )

time: 145 us -> 158 us (1.090)
  waiting for transfers between devices: 61.4 us -> 67.2 us
  starting transfers between devices: 26.6 us -> 30 us
  local copies, waits for them, and re-layouts: 8.62 us -> 11.5 us
    all_to_all x1 -> x2, waiting for transfers between devices: 11.9 us -> 19.2 us  [the longest x1 13.2 us: shards(): lax.all_to_all(by_inner, 'outer', split_axis=2, concat_axis=0, tiled=True)]
    all_to_all x1 -> x2, starting transfers between devices: 15.3 us -> 18.7 us  [the longest x1 12.6 us: shards(): lax.all_to_all(by_inner, 'outer', split_axis=2, concat_axis=0, tiled=True)]
    all_to_all x3 -> x2, blocking collectives: 26.3 us -> 27.4 us  [the longest x1 16.8 us: shards(): lax.all_to_all(to_inner, 'outer', split_axis=0, concat_axis=2, tiled=True)]
    unnamed x34 -> x54, local copies, waits for them, and re-layouts: 5.11 us -> 6.01 us
  transfers between devices with their start and end apart: 6 -> 7, of which waited for: 6 -> 7; matrix products, arithmetic and copies ran while one was open for 5% -> 6% of each run, Pallas kernels for 0% -> 0%
where the time goes in v3:
time: 158 us; the launch traced here: 157 us
  waiting for transfers between devices  67.2 us (43%)
  starting transfers between devices  30 us (19%)
  blocking collectives  27.4 us (17%)
  matrix products  17.5 us (11%)
  local copies, waits for them, and re-layouts  11.5 us (7%)
  other arithmetic  3.18 us (2%)
    ppermute x5, waiting for transfers between devices, from_behind(): return lax.ppermute(block, axis, route)  48 us
    dot_general x36, matrix products, matmul(): return jnp.einsum(spec, left, right, precision=HIGHEST)  17.5 us
    all_to_all x1, blocking collectives, shards(): lax.all_to_all(to_inner, 'outer', split_axis=0, concat_axis=2, tiled=True)  16.8 us
    all_to_all x1, waiting for transfers between devices, shards(): lax.all_to_all(by_inner, 'outer', split_axis=2, concat_axis=0, tiled=True)  13.2 us
    all_to_all x1, starting transfers between devices, shards(): lax.all_to_all(by_inner, 'outer', split_axis=2, concat_axis=0, tiled=True)  12.6 us
    ppermute x5, starting transfers between devices, from_behind(): return lax.ppermute(block, axis, route)  11.3 us
    all_to_all x1, blocking collectives, shards(): lax.all_to_all(normed, INNER, split_axis=1, concat_axis=3, tiled=True)  10.6 us
    all_to_all x1, starting transfers between devices, shards(): lax.all_to_all(arranged, INNER, split_axis=3, concat_axis=1, tiled=True)  6.04 us
  transfers between devices with their start and end apart: 7, of which 7 were waited for; matrix products, arithmetic and copies ran while one was open for 6% of the time, Pallas kernels for 0%

profile of v3, /device:TPU:6, one launch (start us, length us, event | category | flops | bytes accessed | tf_op | source)
XLA Modules:
  0.0 157.5 jit_solution(11216460713182418546)
XLA Ops:
  0.2 0.8 fusion.84
  1.2 0.7 copy-done.23
  2.2 0.7 copy-done.15
  2.8 0.8 fusion.6
  4.3 0.4 convolution_add_fusion.2
  5.6 0.4 convolution_add_fusion.1
  6.0 0.4 convolution_add_fusion
  6.4 0.4 fusion.18
  6.8 0.4 convolution_subtract_fusion.2
  7.2 0.4 fusion.16
  7.6 0.4 convolution_subtract_fusion.1
  8.0 0.4 fusion.14
  8.5 0.4 convolution_subtract_fusion
  8.9 0.4 copy-done.1
  9.4 0.6 copy-done.10
  10.4 0.6 fusion.7
  11.0 0.8 fusion.26
  11.8 0.7 convolution_subtract_fusion.4
  12.7 3.5 %collective-permute-start = (f32[4,128,256]{2,1,0:T(8,128)S(1)}, f32[4,128,256]{2,1,0:T(8,128)S(1)}, u32[]{:S(2)}, u32[]{:S(2)}) collective-permute-start(f32[4,128,256]{2,1,0:T(8,128)S(1)} %pad_maximum_fusion), channel_id=1, source_target_pairs={{0,1},{1,2},{2,3},{3,4},{4,5},{5,6},{6,7},{7,8},{8,9},{9,10},{10,1... | collective-permute-start | bytes 1572872 | tf_op jit(solution)/shard_map/ppermute | solution.py:15
  16.3 0.6 copy-done.18
  17.5 0.7 copy-done
  18.2 0.7 fusion.62
  18.9 0.7 copy-done.13
  19.6 0.7 fusion.4
  20.3 0.4 fusion.35
  20.7 0.5 convolution_multiply_fusion.1
  21.2 0.4 fusion.87
  21.6 8.8 %collective-permute-done = f32[4,128,256]{2,1,0:T(8,128)S(1)} collective-permute-done((f32[4,128,256]{2,1,0:T(8,128)S(1)}, f32[4,128,256]{2,1,0:T(8,128)S(1)}, u32[]{:S(2)}, u32[]{:S(2)}) %collective-permute-start) | collective-permute-done | bytes 524320 | tf_op jit(solution)/shard_map/ppermute | solution.py:15
  30.4 1.0 fusion.91
  31.6 3.3 %collective-permute-start.1 = (f32[4,128,256]{1,2,0:T(8,128)S(1)}, f32[4,128,256]{1,2,0:T(8,128)S(1)}, u32[]{:S(2)}, u32[]{:S(2)}) collective-permute-start(f32[4,128,256]{1,2,0:T(8,128)S(1)} %pad_maximum_fusion.1), channel_id=1, source_target_pairs={{0,2},{1,3},{2,4},{3,5},{4,6},{5,7},{6,8},{7,9},{8,10},{9,11},{10,... | collective-permute-start | bytes 1572872 | tf_op jit(solution)/shard_map/ppermute | solution.py:15
  34.9 0.7 fusion.82
  35.6 0.4 fusion.88
  36.0 0.4 convolution_add_fusion.5
  36.4 12.4 %collective-permute-done.1 = f32[4,128,256]{1,2,0:T(8,128)S(1)} collective-permute-done((f32[4,128,256]{1,2,0:T(8,128)S(1)}, f32[4,128,256]{1,2,0:T(8,128)S(1)}, u32[]{:S(2)}, u32[]{:S(2)}) %collective-permute-start.1) | collective-permute-done | bytes 524320 | tf_op jit(solution)/shard_map/ppermute | solution.py:15
  48.8 0.6 fusion.76
  49.5 1.3 collective-permute-start.2
  50.8 0.7 fusion.86
  51.4 0.4 convolution_add_fusion.4
  51.8 0.6 fusion.28
  52.4 10.8 %collective-permute-done.2 = f32[4,128,256]{1,2,0:T(8,128)S(1)} collective-permute-done((f32[4,128,256]{1,2,0:T(8,128)S(1)}, f32[4,128,256]{1,2,0:T(8,128)S(1)}, u32[]{:S(2)}, u32[]{:S(2)}) %collective-permute-start.2) | collective-permute-done | bytes 524320 | tf_op jit(solution)/shard_map/ppermute | solution.py:15
  63.2 0.6 fusion.74
  64.1 1.3 collective-permute-start.3
  65.5 0.4 convolution_add_fusion.3
  65.9 8.0 %collective-permute-done.3 = f32[4,128,128]{1,2,0:T(8,128)S(1)} collective-permute-done((f32[4,128,128]{1,2,0:T(8,128)S(1)}, f32[4,128,128]{1,2,0:T(8,128)S(1)}, u32[]{:S(2)}, u32[]{:S(2)}) %collective-permute-start.3) | collective-permute-done | bytes 262176 | tf_op jit(solution)/shard_map/ppermute | solution.py:15
  73.9 0.7 convolution_add_fusion.7
  74.5 1.9 %collective-permute-start.4 = (f32[4,128,128]{1,2,0:T(8,128)S(1)}, f32[4,128,128]{1,2,0:T(8,128)S(1)}, u32[]{:S(2)}, u32[]{:S(2)}) collective-permute-start(f32[4,128,128]{1,2,0:T(8,128)S(1)} %convolution_add_fusion.7), channel_id=1, source_target_pairs={{0,1},{1,2},{2,3},{3,4},{4,5},{5,6},{6,7},{7,8},{8,9},{9,10},{10,1... | collective-permute-start | bytes 786440 | tf_op jit(solution)/shard_map/ppermute | solution.py:15
  76.5 0.4 convolution_subtract_fusion.5
  76.9 8.0 %collective-permute-done.4 = f32[4,128,128]{1,2,0:T(8,128)S(1)} collective-permute-done((f32[4,128,128]{1,2,0:T(8,128)S(1)}, f32[4,128,128]{1,2,0:T(8,128)S(1)}, u32[]{:S(2)}, u32[]{:S(2)}) %collective-permute-start.4) | collective-permute-done | bytes 262176 | tf_op jit(solution)/shard_map/ppermute | solution.py:15
  84.9 0.7 multiply_reduce_fusion.1
  85.6 0.6 copy-done.24
  86.6 0.7 copy.87
  87.3 6.0 %all-to-all-start = ((bf16[1,1,4,8,4,512]{5,4,2,1,0,3:T(4,128)(2,1)}), bf16[1,1,4,8,4,512]{5,4,2,1,0,3:T(4,128)(2,1)S(1)}, u32[]{:S(2)}, u32[]{:S(2)}) async-start(bf16[1,1,4,8,4,512]{5,4,2,1,0,3:T(4,128)(2,1)} %copy.87), calls=%async_computation | async-start | bytes 262144 | tf_op jit(solution)/shard_map/all_to_all | solution.py:182
  93.3 0.4 fusion.21
  93.7 0.4 convolution_subtract_fusion.3
  94.1 6.0 %all-to-all-done = bf16[1,1,4,8,4,512]{5,4,2,1,0,3:T(4,128)(2,1)S(1)} async-done(((bf16[1,1,4,8,4,512]{5,4,2,1,0,3:T(4,128)(2,1)}), bf16[1,1,4,8,4,512]{5,4,2,1,0,3:T(4,128)(2,1)S(1)}, u32[]{:S(2)}, u32[]{:S(2)}) %all-to-all-start) | async-done | bytes 131104 | tf_op jit(solution)/shard_map/all_to_all | solution.py:182
  100.1 0.7 copy.88
  100.8 12.6 %all-to-all-start.1 = ((bf16[1,8,4,1,4,512]{5,4,1,3,0,2:T(4,128)(2,1)}), bf16[1,8,4,1,4,512]{5,4,1,3,0,2:T(4,128)(2,1)S(1)}, u32[]{:S(2)}, u32[]{:S(2)}) async-start(bf16[1,8,4,1,4,512]{5,4,1,3,0,2:T(4,128)(2,1)} %copy.88), calls=%async_computation.1 | async-start | bytes 262144 | tf_op jit(solution)/shard_map/all_to_all | solution.py:183
  113.5 0.4 convolution_multiply_fusion.4
  114.2 0.4 convolution_multiply_fusion.2
  114.5 13.2 %all-to-all-done.1 = bf16[1,8,4,1,4,512]{5,4,1,3,0,2:T(4,128)(2,1)S(1)} async-done(((bf16[1,8,4,1,4,512]{5,4,1,3,0,2:T(4,128)(2,1)}), bf16[1,8,4,1,4,512]{5,4,1,3,0,2:T(4,128)(2,1)S(1)}, u32[]{:S(2)}, u32[]{:S(2)}) %all-to-all-start.1) | async-done | bytes 131104 | tf_op jit(solution)/shard_map/all_to_all | solution.py:183
  128.3 0.5 copy-done.25
  129.3 10.6 %all_to_all.54 = bf16[4,8,1,1,4,512]{5,0,4,3,2,1:T(4,128)(2,1)S(1)} all-to-all(bf16[4,8,1,1,4,512]{5,0,4,3,2,1:T(4,128)(2,1)S(1)} %copy.92), channel_id=1, replica_groups=mesh['outer'=4,'near'=4,'core'=2,'scan'=16] {'near','core'}, dimensions={1} | all-to-all | bytes 262144 | tf_op jit(solution)/shard_map/all_to_all | solution.py:198
  140.0 16.8 %all_to_all.55 = bf16[4,1,1,8,4,512]{5,3,4,2,1,0:T(8,128)(2,1)S(1)} all-to-all(bf16[4,1,1,8,4,512]{5,3,4,2,1,0:T(8,128)(2,1)S(1)} %copy.93), channel_id=1, replica_groups=mesh['outer'=4,'near'=4,'core'=2,'scan'=16] {'outer'}, dimensions={0} | all-to-all | bytes 262144 | tf_op jit(solution)/shard_map/all_to_all | solution.py:199
  156.8 0.7 reshape.264
  (107 shorter events, 5.6 us)
Async XLA Ops:
  1.2 0.7 copy-start.23
  2.2 0.7 copy-start.15
  8.4 0.9 copy-start.1
  9.4 0.6 copy-start.10
  12.7 4.5 %copy-start.4 = (bf16[32,1,4,512]{3,2,1,0:T(4,128)(2,1)S(1)}, bf16[32,1,4,512]{3,2,1,0:T(4,128)(2,1)}, u32[]{:S(2)}) copy-start(bf16[32,1,4,512]{3,2,1,0:T(4,128)(2,1)} %param.18) | copy-start | bytes 393220
  12.7 17.7 %collective-permute-start = (f32[4,128,256]{2,1,0:T(8,128)S(1)}, f32[4,128,256]{2,1,0:T(8,128)S(1)}, u32[]{:S(2)}, u32[]{:S(2)}) collective-permute-start(f32[4,128,256]{2,1,0:T(8,128)S(1)} %pad_maximum_fusion), channel_id=1, source_target_pairs={{0,1},{1,2},{2,3},{3,4},{4,5},{5,6},{6,7},{7,8},{8,9},{9,10},{10,1... | collective-permute-start | bytes 1572872 | tf_op jit(solution)/shard_map/ppermute | solution.py:15
  16.2 0.7 copy-start.18
  17.1 1.8 %copy-start.19 = (f32[16,32]{1,0:T(8,128)}, f32[16,32]{1,0:T(8,128)S(1)}, u32[]{:S(2)}) copy-start(f32[16,32]{1,0:T(8,128)S(1)} %reduce_window_sum.22) | copy-start | bytes 6148
  17.2 1.7 %copy-start.21 = (pred[32,32]{1,0:T(8,128)(4,1)}, pred[32,32]{1,0:T(8,128)(4,1)S(1)}, u32[]{:S(2)}) copy-start(pred[32,32]{1,0:T(8,128)(4,1)S(1)} %get-tuple-element.53) | copy-start | bytes 3076
  17.3 0.9 copy-start
  18.2 0.7 copy-start.16
  18.9 0.7 copy-start.13
  31.6 4.0 %copy-start.5 = (bf16[32,1,4,512]{3,2,1,0:T(4,128)(2,1)S(1)}, bf16[32,1,4,512]{3,2,1,0:T(4,128)(2,1)}, u32[]{:S(2)}) copy-start(bf16[32,1,4,512]{3,2,1,0:T(4,128)(2,1)} %param.17) | copy-start | bytes 393220
  31.6 17.2 %collective-permute-start.1 = (f32[4,128,256]{1,2,0:T(8,128)S(1)}, f32[4,128,256]{1,2,0:T(8,128)S(1)}, u32[]{:S(2)}, u32[]{:S(2)}) collective-permute-start(f32[4,128,256]{1,2,0:T(8,128)S(1)} %pad_maximum_fusion.1), channel_id=1, source_target_pairs={{0,2},{1,3},{2,4},{3,5},{4,6},{5,7},{6,8},{7,9},{8,10},{9,11},{10,... | collective-permute-start | bytes 1572872 | tf_op jit(solution)/shard_map/ppermute | solution.py:15
  49.5 13.8 %collective-permute-start.2 = (f32[4,128,256]{1,2,0:T(8,128)S(1)}, f32[4,128,256]{1,2,0:T(8,128)S(1)}, u32[]{:S(2)}, u32[]{:S(2)}) collective-permute-start(f32[4,128,256]{1,2,0:T(8,128)S(1)} %pad_maximum_fusion.2), channel_id=1, source_target_pairs={{0,4},{1,5},{2,6},{3,7},{4,8},{5,9},{6,10},{7,11},{8,12},{9,13},{1... | collective-permute-start | bytes 1572872 | tf_op jit(solution)/shard_map/ppermute | solution.py:15
  64.0 1.4 copy-start.2
  64.1 1.4 copy-start.3
  64.1 9.8 %collective-permute-start.3 = (f32[4,128,128]{1,2,0:T(8,128)S(1)}, f32[4,128,128]{1,2,0:T(8,128)S(1)}, u32[]{:S(2)}, u32[]{:S(2)}) collective-permute-start(f32[4,128,128]{1,2,0:T(8,128)S(1)} %add.148), channel_id=1, source_target_pairs={{0,8},{1,9},{2,10},{3,11},{4,12},{5,13},{6,14},{7,15},{16,24},{17,... | collective-permute-start | bytes 786440 | tf_op jit(solution)/shard_map/ppermute | solution.py:15
  65.8 10.6 %copy-start.6 = (bf16[4,32,128]{2,1,0:T(8,128)(2,1)S(1)}, bf16[4,32,128]{2,1,0:T(8,128)(2,1)}, u32[]{:S(2)}) copy-start(bf16[4,32,128]{2,1,0:T(8,128)(2,1)} %get-tuple-element.37) | copy-start | bytes 98308
  65.9 10.6 %copy-start.7 = (bf16[4,32,128]{2,1,0:T(8,128)(2,1)S(1)}, bf16[4,32,128]{2,1,0:T(8,128)(2,1)}, u32[]{:S(2)}) copy-start(bf16[4,32,128]{2,1,0:T(8,128)(2,1)} %get-tuple-element.38) | copy-start | bytes 98308
  65.9 10.6 %copy-start.8 = (bf16[4,32,128]{2,1,0:T(8,128)(2,1)S(1)}, bf16[4,32,128]{2,1,0:T(8,128)(2,1)}, u32[]{:S(2)}) copy-start(bf16[4,32,128]{2,1,0:T(8,128)(2,1)} %get-tuple-element.39) | copy-start | bytes 98308
  65.9 10.6 %copy-start.9 = (bf16[4,32,128]{2,1,0:T(8,128)(2,1)S(1)}, bf16[4,32,128]{2,1,0:T(8,128)(2,1)}, u32[]{:S(2)}) copy-start(bf16[4,32,128]{2,1,0:T(8,128)(2,1)} %get-tuple-element.40) | copy-start | bytes 98308
  73.9 2.7 %copy-start.11 = (f32[4,128]{1,0:T(4,128)S(1)}, f32[4,128]{1,0:T(4,128)}, u32[]{:S(2)}) copy-start(f32[4,128]{1,0:T(4,128)} %copy-done.10) | copy-start | bytes 6148
  74.5 10.4 %collective-permute-start.4 = (f32[4,128,128]{1,2,0:T(8,128)S(1)}, f32[4,128,128]{1,2,0:T(8,128)S(1)}, u32[]{:S(2)}, u32[]{:S(2)}) collective-permute-start(f32[4,128,128]{1,2,0:T(8,128)S(1)} %convolution_add_fusion.7), channel_id=1, source_target_pairs={{0,1},{1,2},{2,3},{3,4},{4,5},{5,6},{6,7},{7,8},{8,9},{9,10},{10,1... | collective-permute-start | bytes 786440 | tf_op jit(solution)/shard_map/ppermute | solution.py:15
  85.6 0.7 copy-start.24
  87.3 6.0 %copy-start.12 = (pred[32,32]{1,0:T(8,128)(4,1)S(1)}, pred[32,32]{1,0:T(8,128)(4,1)}, u32[]{:S(2)}) copy-start(pred[32,32]{1,0:T(8,128)(4,1)} %get-tuple-element.48) | copy-start | bytes 3076
  87.3 12.8 %all-to-all-start = ((bf16[1,1,4,8,4,512]{5,4,2,1,0,3:T(4,128)(2,1)}), bf16[1,1,4,8,4,512]{5,4,2,1,0,3:T(4,128)(2,1)S(1)}, u32[]{:S(2)}, u32[]{:S(2)}) async-start(bf16[1,1,4,8,4,512]{5,4,2,1,0,3:T(4,128)(2,1)} %copy.87), calls=%async_computation | async-start | bytes 262144 | tf_op jit(solution)/shard_map/all_to_all | solution.py:182
  100.8 12.6 %copy-start.17 = (f32[16,32]{1,0:T(8,128)S(1)}, f32[16,32]{1,0:T(8,128)}, u32[]{:S(2)}) copy-start(f32[16,32]{1,0:T(8,128)} %copy-done.16) | copy-start | bytes 6148
  100.8 12.6 %copy-start.20 = (f32[16,32]{1,0:T(8,128)S(1)}, f32[16,32]{1,0:T(8,128)}, u32[]{:S(2)}) copy-start(f32[16,32]{1,0:T(8,128)} %copy-done.19) | copy-start | bytes 6148
  100.8 12.6 %copy-start.22 = (pred[32,32]{1,0:T(8,128)(4,1)S(1)}, pred[32,32]{1,0:T(8,128)(4,1)}, u32[]{:S(2)}) copy-start(pred[32,32]{1,0:T(8,128)(4,1)} %copy-done.21) | copy-start | bytes 3076
  100.8 26.9 %all-to-all-start.1 = ((bf16[1,8,4,1,4,512]{5,4,1,3,0,2:T(4,128)(2,1)}), bf16[1,8,4,1,4,512]{5,4,1,3,0,2:T(4,128)(2,1)S(1)}, u32[]{:S(2)}, u32[]{:S(2)}) async-start(bf16[1,8,4,1,4,512]{5,4,1,3,0,2:T(4,128)(2,1)} %copy.88), calls=%async_computation.1 | async-start | bytes 262144 | tf_op jit(solution)/shard_map/all_to_all | solution.py:183
  113.5 0.7 copy-start.14
  128.2 0.7 copy-start.25

commit v4 on v1

--- a/solution.py
+++ b/solution.py
@@ -18,17 +18,16 @@
 
 
 def unit_lower_inverse(system):
-    batch = system.shape[:-2]
     size = system.shape[-1]
     base = min(BASE_BLOCK, size)
-    count = size // base
-    assert count * base == size and count & (count - 1) == 0
-    eye = jnp.eye(base, dtype=jnp.float32)
-    grid = system.reshape(batch + (count, base, count, base))
-    diagonal = jnp.moveaxis(jnp.diagonal(grid, axis1=-4, axis2=-2), -1, -3)
-    lower = diagonal - eye
-    inverse = eye - lower
-    power = lower
+    assert size % base == 0
+    rows = lax.broadcasted_iota(jnp.int32, (size, size), 0)
+    cols = lax.broadcasted_iota(jnp.int32, (size, size), 1)
+    eye = jnp.eye(size, dtype=jnp.float32)
+    lower = system - eye
+    diagonal = jnp.where(rows // base == cols // base, lower, 0.0)
+    inverse = eye - diagonal
+    power = diagonal
     reach = 2
     while reach < base:
         power = matmul("...ij,...jk->...ik", power, power)
@@ -36,20 +35,13 @@
         reach *= 2
     width = base
     while width < size:
-        pairs = size // (2 * width)
-        grid = system.reshape(batch + (pairs, 2, width, pairs, 2, width))
-        coupling = jnp.moveaxis(jnp.diagonal(grid, axis1=-6, axis2=-3), -1, -5)[..., 1, :, 0, :]
-        halves = inverse.reshape(batch + (pairs, 2, width, width))
-        upper_inverse = halves[..., 0, :, :]
-        lower_inverse = halves[..., 1, :, :]
-        mixed = -matmul(
-            "...ij,...jk->...ik", matmul("...ij,...jk->...ik", lower_inverse, coupling), upper_inverse
+        inside = (rows // (2 * width) == cols // (2 * width)) & (rows // width != cols // width)
+        coupling = jnp.where(inside, lower, 0.0)
+        inverse = inverse - matmul(
+            "...ij,...jk->...ik", matmul("...ij,...jk->...ik", inverse, coupling), inverse
         )
-        top = jnp.concatenate([upper_inverse, jnp.zeros_like(upper_inverse)], axis=-1)
-        bottom = jnp.concatenate([mixed, lower_inverse], axis=-1)
-        inverse = jnp.concatenate([top, bottom], axis=-2)
         width *= 2
-    return inverse.reshape(batch + (size, size))
+    return inverse
 
 
 def block_system(key_block, log_decay, beta_block):
@@ -116,14 +108,14 @@
 
 def prefix_states(transfer, offset):
     scan_count = lax.axis_size("scan")
-    head_size = offset.shape[-1]
     distance = 1
     while distance < scan_count:
         if 2 * distance < scan_count:
-            arrived = from_behind(jnp.concatenate([transfer, offset], axis=-1), "scan", distance)
-            composed = matmul("bij,bjv->biv", transfer, arrived)
-            transfer = composed[:, :, :head_size]
-            offset = composed[:, :, head_size:] + offset
+            sent_transfer, arrived = from_behind(
+                (transfer.astype(jnp.bfloat16), offset), "scan", distance
+            )
+            offset = matmul("bij,bjv->biv", transfer, arrived) + offset
+            transfer = matmul("bij,bjv->biv", transfer, sent_transfer.astype(jnp.float32))
         else:
             arrived = from_behind(offset, "scan", distance)
             offset = matmul("bij,bjv->biv", transfer, arrived) + offset
@@ -180,6 +172,7 @@
     values_col = (
         head_norm(row_scan, gain_row).reshape(row_count, segment, features).astype(jnp.bfloat16)
     )
+    values_col, operator = lax.optimization_barrier((values_col, operator))
     arranged = values_col.reshape(row_count, line_count, segment // line_count, features)
     column_values = lax.all_to_all(arranged, "line", split_axis=1, concat_axis=0, tiled=True)
 

time: 161 us -> 129 us (0.80)
  waiting for transfers between devices: 65 us -> 27.3 us
  blocking collectives: 20.2 us -> 52.7 us
  local copies, waits for them, and re-layouts: 23.5 us -> 8.28 us
  starting transfers between devices: 26.8 us -> 19.3 us
  other arithmetic: 4.77 us -> 2.44 us
  matrix products: 19.1 us -> 16.8 us
    all_to_all x0 -> x1, blocking collectives: none -> 32.5 us  [shards(): lax.all_to_all(arranged, 'line', split_axis=1, concat_axis=0, tiled=True)]
    ppermute x5 -> x8, waiting for transfers between devices: 48.8 us -> 27.3 us  [from_behind(): return lax.ppermute(block, axis, route)]
    all_to_all x1 -> x0, waiting for transfers between devices: 16.2 us -> none  [shards(): lax.all_to_all(arranged, 'line', split_axis=1, concat_axis=0, tiled=True)]
    all_to_all x1 -> x0, starting transfers between devices: 15.5 us -> none  [shards(): lax.all_to_all(arranged, 'line', split_axis=1, concat_axis=0, tiled=True)]
    reshape x8 -> x1, local copies, waits for them, and re-layouts: 9.05 us -> 0.04 us  [shards(): values_col.reshape(row_count, line_count, segment // line_count, features)]
    ppermute x5 -> x8, starting transfers between devices: 11.3 us -> 19.3 us  [from_behind(): return lax.ppermute(block, axis, route)]
    gather x6 -> x0, local copies, waits for them, and re-layouts: 5.56 us -> none  [the longest x4 2.84 us: unit_lower_inverse(): jnp.diagonal(grid, axis1=-6, axis2=-3)]
    unnamed x68 -> x21, local copies, waits for them, and re-layouts: 0.93 us -> 5.72 us
  transfers between devices with their start and end apart: 6 -> 8, of which waited for: 6 -> 4; matrix products, arithmetic and copies ran while one was open for 6% -> 8% of each run, Pallas kernels for 0% -> 0%
where the time goes in v4:
time: 129 us; the launch traced here: 128 us
  blocking collectives  52.7 us (41%)
  waiting for transfers between devices  27.3 us (21%)
  starting transfers between devices  19.3 us (15%)
  matrix products  16.8 us (13%)
  local copies, waits for them, and re-layouts  8.28 us (6%)
  other arithmetic  2.44 us (2%)
    all_to_all x1, blocking collectives, shards(): lax.all_to_all(arranged, 'line', split_axis=1, concat_axis=0, tiled=True)  32.5 us
    ppermute x8, waiting for transfers between devices, from_behind(): return lax.ppermute(block, axis, route)  27.3 us
    all_to_all x1, blocking collectives, shards(): lax.all_to_all(normed, 'line', split_axis=0, concat_axis=1, tiled=True)  20.2 us
    ppermute x8, starting transfers between devices, from_behind(): return lax.ppermute(block, axis, route)  19.3 us
    dot_general x39, matrix products, matmul(): return jnp.einsum(spec, left, right, precision=HIGHEST)  16.8 us
    unnamed x21, local copies, waits for them, and re-layouts  5.72 us
  transfers between devices with their start and end apart: 8, of which 4 were waited for; matrix products, arithmetic and copies ran while one was open for 8% of the time, Pallas kernels for 0%

profile of v4, /device:TPU:6, one launch (start us, length us, event | category | flops | bytes accessed | tf_op | source)
XLA Modules:
  0.0 127.5 jit_solution(13424525152259932014)
XLA Ops:
  0.2 0.8 fusion.78
  1.2 0.7 copy-done.7
  1.8 0.3 reduce_window_sum.22
  2.2 0.7 copy-done.5
  2.8 0.8 fusion.4
  3.6 0.3 fusion.57
  3.9 0.4 fusion.34
  4.3 0.4 convolution_add_fusion.5
  4.7 0.4 fusion.83
  5.3 0.4 fusion.84
  5.6 0.4 convolution_add_fusion.4
  6.0 0.4 convolution_add_fusion.3
  6.4 0.4 fusion.20
  6.8 0.4 convolution_subtract_fusion.3
  7.2 0.4 fusion.18
  7.6 0.4 convolution_subtract_fusion.2
  8.0 0.4 fusion.16
  8.5 0.4 convolution_subtract_fusion.1
  8.9 0.4 copy-done.1
  9.4 0.3 broadcast_multiply_fusion
  9.7 0.6 fusion.7
  10.3 0.7 fusion.25
  11.0 3.5 %collective-permute-start.3 = (f32[4,128,128]{2,1,0:T(8,128)S(1)}, f32[4,128,128]{2,1,0:T(8,128)S(1)}, u32[]{:S(2)}, u32[]{:S(2)}) collective-permute-start(f32[4,128,128]{2,1,0:T(8,128)S(1)} %fusion.25), channel_id=1, source_target_pairs={{0,1},{1,2},{2,3},{3,4},{4,5},{5,6},{6,7},{7,8},{8,9},{9,10},{10,1... | collective-permute-start | bytes 786440 | tf_op jit(solution)/shard_map/ppermute | solution.py:13
  14.7 0.7 fusion.80
  15.5 3.7 %collective-permute-start = (bf16[4,128,128]{2,1,0:T(8,128)(2,1)S(1)}, bf16[4,128,128]{2,1,0:T(8,128)(2,1)S(1)}, u32[]{:S(2)}, u32[]{:S(2)}) collective-permute-start(bf16[4,128,128]{2,1,0:T(8,128)(2,1)S(1)} %get-tuple-element.50), channel_id=1, source_target_pairs={{0,1},{1,2},{2,3},{3,4},{4,5},{5,6},{6,7},{7,8},{8,9},{9,10},{10,1... | collective-permute-start | bytes 393224 | tf_op jit(solution)/shard_map/ppermute | solution.py:13
  19.2 0.6 copy-done.6
  20.5 0.7 copy-done.4
  21.2 0.7 fusion.6
  21.9 0.4 fusion.29
  22.3 0.4 convolution_add_fusion.2
  22.7 0.4 fusion.86
  23.1 0.5 copy-done
  23.7 0.9 copy-done.3
  24.6 0.4 convolution_multiply_fusion.2
  25.0 0.4 fusion.87
  25.4 0.4 convolution_add_fusion.1
  25.8 0.4 convolution_add_fusion
  26.2 0.4 fusion.13
  26.6 0.4 convolution_subtract_fusion
  27.0 0.4 convolution_multiply_fusion
  27.4 0.4 convolution_add_fusion.10
  27.8 3.2 %collective-permute-start.4 = (f32[4,128,128]{2,1,0:T(8,128)S(1)}, f32[4,128,128]{2,1,0:T(8,128)S(1)}, u32[]{:S(2)}, u32[]{:S(2)}) collective-permute-start(f32[4,128,128]{2,1,0:T(8,128)S(1)} %convolution_add_fusion.10), channel_id=1, source_target_pairs={{0,2},{1,3},{2,4},{3,5},{4,6},{5,7},{6,8},{7,9},{8,10},{9,11},{10,... | collective-permute-start | bytes 786440 | tf_op jit(solution)/shard_map/ppermute | solution.py:13
  31.1 0.5 convolution_multiply_fusion.4
  31.8 1.9 %collective-permute-start.1 = (bf16[4,128,128]{2,1,0:T(8,128)(2,1)S(1)}, bf16[4,128,128]{2,1,0:T(8,128)(2,1)S(1)}, u32[]{:S(2)}, u32[]{:S(2)}) collective-permute-start(bf16[4,128,128]{2,1,0:T(8,128)(2,1)S(1)} %get-tuple-element.52), channel_id=1, source_target_pairs={{0,2},{1,3},{2,4},{3,5},{4,6},{5,7},{6,8},{7,9},{8,10},{9,11},{10,... | collective-permute-start | bytes 393224 | tf_op jit(solution)/shard_map/ppermute | solution.py:13
  33.8 7.2 %collective-permute-done.4 = f32[4,128,128]{2,1,0:T(8,128)S(1)} collective-permute-done((f32[4,128,128]{2,1,0:T(8,128)S(1)}, f32[4,128,128]{2,1,0:T(8,128)S(1)}, u32[]{:S(2)}, u32[]{:S(2)}) %collective-permute-start.4) | collective-permute-done | bytes 262176 | tf_op jit(solution)/shard_map/ppermute | solution.py:13
  41.0 0.4 convolution_add_fusion.9
  41.4 1.3 %collective-permute-start.5 = (f32[4,128,128]{2,1,0:T(8,128)S(1)}, f32[4,128,128]{2,1,0:T(8,128)S(1)}, u32[]{:S(2)}, u32[]{:S(2)}) collective-permute-start(f32[4,128,128]{2,1,0:T(8,128)S(1)} %convolution_add_fusion.9), channel_id=1, source_target_pairs={{0,4},{1,5},{2,6},{3,7},{4,8},{5,9},{6,10},{7,11},{8,12},{9,13},{1... | collective-permute-start | bytes 786440 | tf_op jit(solution)/shard_map/ppermute | solution.py:13
  42.7 0.6 fusion.27
  43.3 0.3 fusion.82
  43.6 1.3 %collective-permute-start.2 = (bf16[4,128,128]{2,1,0:T(8,128)(2,1)S(1)}, bf16[4,128,128]{2,1,0:T(8,128)(2,1)S(1)}, u32[]{:S(2)}, u32[]{:S(2)}) collective-permute-start(bf16[4,128,128]{2,1,0:T(8,128)(2,1)S(1)} %get-tuple-element.54), channel_id=1, source_target_pairs={{0,4},{1,5},{2,6},{3,7},{4,8},{5,9},{6,10},{7,11},{8,12},{9,13},{1... | collective-permute-start | bytes 393224 | tf_op jit(solution)/shard_map/ppermute | solution.py:13
  44.9 5.1 %collective-permute-done.5 = f32[4,128,128]{2,1,0:T(8,128)S(1)} collective-permute-done((f32[4,128,128]{2,1,0:T(8,128)S(1)}, f32[4,128,128]{2,1,0:T(8,128)S(1)}, u32[]{:S(2)}, u32[]{:S(2)}) %collective-permute-start.5) | collective-permute-done | bytes 262176 | tf_op jit(solution)/shard_map/ppermute | solution.py:13
  50.0 0.4 convolution_add_fusion.8
  50.4 1.3 %collective-permute-start.6 = (f32[4,128,128]{2,1,0:T(8,128)S(1)}, f32[4,128,128]{2,1,0:T(8,128)S(1)}, u32[]{:S(2)}, u32[]{:S(2)}) collective-permute-start(f32[4,128,128]{2,1,0:T(8,128)S(1)} %convolution_add_fusion.8), channel_id=1, source_target_pairs={{0,8},{1,9},{2,10},{3,11},{4,12},{5,13},{6,14},{7,15},{16,24},{17,... | collective-permute-start | bytes 786440 | tf_op jit(solution)/shard_map/ppermute | solution.py:13
  52.0 8.2 %collective-permute-done.6 = f32[4,128,128]{2,1,0:T(8,128)S(1)} collective-permute-done((f32[4,128,128]{2,1,0:T(8,128)S(1)}, f32[4,128,128]{2,1,0:T(8,128)S(1)}, u32[]{:S(2)}, u32[]{:S(2)}) %collective-permute-start.6) | collective-permute-done | bytes 262176 | tf_op jit(solution)/shard_map/ppermute | solution.py:13
  60.1 0.4 convolution_add_fusion.7
  60.5 3.1 %collective-permute-start.7 = (f32[4,128,128]{2,1,0:T(8,128)S(1)}, f32[4,128,128]{2,1,0:T(8,128)S(1)}, u32[]{:S(2)}, u32[]{:S(2)}) collective-permute-start(f32[4,128,128]{2,1,0:T(8,128)S(1)} %convolution_add_fusion.7), channel_id=1, source_target_pairs={{0,1},{1,2},{2,3},{3,4},{4,5},{5,6},{6,7},{7,8},{8,9},{9,10},{10,1... | collective-permute-start | bytes 786440 | tf_op jit(solution)/shard_map/ppermute | solution.py:13
  63.7 0.4 convolution_subtract_fusion.5
  64.1 6.8 %collective-permute-done.7 = f32[4,128,128]{2,1,0:T(8,128)S(1)} collective-permute-done((f32[4,128,128]{2,1,0:T(8,128)S(1)}, f32[4,128,128]{2,1,0:T(8,128)S(1)}, u32[]{:S(2)}, u32[]{:S(2)}) %collective-permute-start.7) | collective-permute-done | bytes 262176 | tf_op jit(solution)/shard_map/ppermute | solution.py:13
  70.9 0.6 multiply_reduce_fusion.2
  71.6 0.7 copy-done.8
  72.5 32.5 %all_to_all.8 = bf16[1,32,4,512]{3,2,0,1:T(4,128)(2,1)S(1)} all-to-all(bf16[1,32,4,512]{3,2,0,1:T(4,128)(2,1)S(1)} %bitcast.124), channel_id=1, replica_groups=mesh['line'=32,'scan'=16] {'line'}, dimensions={1} | all-to-all | bytes 262144 | tf_op jit(solution)/shard_map/all_to_all | solution.py:177
  105.7 0.5 copy-done.9
  106.7 20.2 %all_to_all.9 = bf16[32,1,4,512]{3,2,1,0:T(4,128)(2,1)S(1)} all-to-all(bf16[32,1,4,512]{3,2,1,0:T(4,128)(2,1)S(1)} %copy.47), channel_id=1, replica_groups=mesh['line'=32,'scan'=16] {'line'}, dimensions={0} | all-to-all | bytes 262144 | tf_op jit(solution)/shard_map/all_to_all | solution.py:191
  126.8 0.7 reshape.266
  (67 shorter events, 3.5 us)
Async XLA Ops:
  1.2 0.7 copy-start.7
  2.2 0.7 copy-start.5
  8.4 0.9 copy-start.1
  11.0 16.4 %collective-permute-start.3 = (f32[4,128,128]{2,1,0:T(8,128)S(1)}, f32[4,128,128]{2,1,0:T(8,128)S(1)}, u32[]{:S(2)}, u32[]{:S(2)}) collective-permute-start(f32[4,128,128]{2,1,0:T(8,128)S(1)} %fusion.25), channel_id=1, source_target_pairs={{0,1},{1,2},{2,3},{3,4},{4,5},{5,6},{6,7},{7,8},{8,9},{9,10},{10,1... | collective-permute-start | bytes 786440 | tf_op jit(solution)/shard_map/ppermute | solution.py:13
  14.7 5.4 %copy-start.2 = (bf16[32,1,4,512]{3,2,1,0:T(4,128)(2,1)S(1)}, bf16[32,1,4,512]{3,2,1,0:T(4,128)(2,1)}, u32[]{:S(2)}) copy-start(bf16[32,1,4,512]{3,2,1,0:T(4,128)(2,1)} %param.18) | copy-start | bytes 393220
  15.5 16.1 %collective-permute-start = (bf16[4,128,128]{2,1,0:T(8,128)(2,1)S(1)}, bf16[4,128,128]{2,1,0:T(8,128)(2,1)S(1)}, u32[]{:S(2)}, u32[]{:S(2)}) collective-permute-start(bf16[4,128,128]{2,1,0:T(8,128)(2,1)S(1)} %get-tuple-element.50), channel_id=1, source_target_pairs={{0,1},{1,2},{2,3},{3,4},{4,5},{5,6},{6,7},{7,8},{8,9},{9,10},{10,1... | collective-permute-start | bytes 393224 | tf_op jit(solution)/shard_map/ppermute | solution.py:13
  19.1 0.7 copy-start.6
  20.5 0.7 copy-start.4
  22.7 0.9 copy-start
  23.6 0.9 copy-start.3
  27.8 13.2 %collective-permute-start.4 = (f32[4,128,128]{2,1,0:T(8,128)S(1)}, f32[4,128,128]{2,1,0:T(8,128)S(1)}, u32[]{:S(2)}, u32[]{:S(2)}) collective-permute-start(f32[4,128,128]{2,1,0:T(8,128)S(1)} %convolution_add_fusion.10), channel_id=1, source_target_pairs={{0,2},{1,3},{2,4},{3,5},{4,6},{5,7},{6,8},{7,9},{8,10},{9,11},{10,... | collective-permute-start | bytes 786440 | tf_op jit(solution)/shard_map/ppermute | solution.py:13
  31.8 11.5 %collective-permute-start.1 = (bf16[4,128,128]{2,1,0:T(8,128)(2,1)S(1)}, bf16[4,128,128]{2,1,0:T(8,128)(2,1)S(1)}, u32[]{:S(2)}, u32[]{:S(2)}) collective-permute-start(bf16[4,128,128]{2,1,0:T(8,128)(2,1)S(1)} %get-tuple-element.52), channel_id=1, source_target_pairs={{0,2},{1,3},{2,4},{3,5},{4,6},{5,7},{6,8},{7,9},{8,10},{9,11},{10,... | collective-permute-start | bytes 393224 | tf_op jit(solution)/shard_map/ppermute | solution.py:13
  41.4 8.5 %collective-permute-start.5 = (f32[4,128,128]{2,1,0:T(8,128)S(1)}, f32[4,128,128]{2,1,0:T(8,128)S(1)}, u32[]{:S(2)}, u32[]{:S(2)}) collective-permute-start(f32[4,128,128]{2,1,0:T(8,128)S(1)} %convolution_add_fusion.9), channel_id=1, source_target_pairs={{0,4},{1,5},{2,6},{3,7},{4,8},{5,9},{6,10},{7,11},{8,12},{9,13},{1... | collective-permute-start | bytes 786440 | tf_op jit(solution)/shard_map/ppermute | solution.py:13
  43.6 8.1 %collective-permute-start.2 = (bf16[4,128,128]{2,1,0:T(8,128)(2,1)S(1)}, bf16[4,128,128]{2,1,0:T(8,128)(2,1)S(1)}, u32[]{:S(2)}, u32[]{:S(2)}) collective-permute-start(bf16[4,128,128]{2,1,0:T(8,128)(2,1)S(1)} %get-tuple-element.54), channel_id=1, source_target_pairs={{0,4},{1,5},{2,6},{3,7},{4,8},{5,9},{6,10},{7,11},{8,12},{9,13},{1... | collective-permute-start | bytes 393224 | tf_op jit(solution)/shard_map/ppermute | solution.py:13
  50.4 9.8 %collective-permute-start.6 = (f32[4,128,128]{2,1,0:T(8,128)S(1)}, f32[4,128,128]{2,1,0:T(8,128)S(1)}, u32[]{:S(2)}, u32[]{:S(2)}) collective-permute-start(f32[4,128,128]{2,1,0:T(8,128)S(1)} %convolution_add_fusion.8), channel_id=1, source_target_pairs={{0,8},{1,9},{2,10},{3,11},{4,12},{5,13},{6,14},{7,15},{16,24},{17,... | collective-permute-start | bytes 786440 | tf_op jit(solution)/shard_map/ppermute | solution.py:13
  60.5 10.4 %collective-permute-start.7 = (f32[4,128,128]{2,1,0:T(8,128)S(1)}, f32[4,128,128]{2,1,0:T(8,128)S(1)}, u32[]{:S(2)}, u32[]{:S(2)}) collective-permute-start(f32[4,128,128]{2,1,0:T(8,128)S(1)} %convolution_add_fusion.7), channel_id=1, source_target_pairs={{0,1},{1,2},{2,3},{3,4},{4,5},{5,6},{6,7},{7,8},{8,9},{9,10},{10,1... | collective-permute-start | bytes 786440 | tf_op jit(solution)/shard_map/ppermute | solution.py:13
  71.5 0.7 copy-start.8
  105.6 0.7 copy-start.9

commit v5 on v4

--- a/solution.py
+++ b/solution.py
@@ -108,19 +108,31 @@
 
 def prefix_states(transfer, offset):
     scan_count = lax.axis_size("scan")
+    head_size = offset.shape[-1]
+    ahead_transfer = jnp.zeros_like(transfer)
+    ahead_offset = jnp.zeros_like(offset)
     distance = 1
     while distance < scan_count:
         if 2 * distance < scan_count:
-            sent_transfer, arrived = from_behind(
-                (transfer.astype(jnp.bfloat16), offset), "scan", distance
-            )
-            offset = matmul("bij,bjv->biv", transfer, arrived) + offset
-            transfer = matmul("bij,bjv->biv", transfer, sent_transfer.astype(jnp.float32))
+            arrived = from_behind(jnp.concatenate([transfer, offset], axis=-1), "scan", distance)
+            composed = matmul("bij,bjv->biv", transfer, arrived)
+            if distance == 1:
+                ahead_transfer = arrived[:, :, :head_size]
+                ahead_offset = arrived[:, :, head_size:]
+            else:
+                ahead = matmul("bij,bjv->biv", ahead_transfer, arrived)
+                ahead_transfer = ahead[:, :, :head_size]
+                ahead_offset = ahead[:, :, head_size:] + ahead_offset
+            transfer = composed[:, :, :head_size]
+            offset = composed[:, :, head_size:] + offset
         else:
             arrived = from_behind(offset, "scan", distance)
-            offset = matmul("bij,bjv->biv", transfer, arrived) + offset
+            if distance == 1:
+                ahead_offset = arrived
+            else:
+                ahead_offset = matmul("bij,bjv->biv", ahead_transfer, arrived) + ahead_offset
         distance *= 2
-    return from_behind(offset, "scan", 1)
+    return ahead_offset
 
 
 def shards(

time: 129 us -> 130 us (level); the launches traced: 128 us -> 130 us
  waiting for transfers between devices: 27.3 us -> 38.5 us
  starting transfers between devices: 19.3 us -> 9.24 us
  matrix products: 16.8 us -> 18.4 us
    ppermute x8 -> x4, waiting for transfers between devices: 27.3 us -> 38.5 us  [from_behind(): return lax.ppermute(block, axis, route)]
    ppermute x8 -> x4, starting transfers between devices: 19.3 us -> 9.24 us  [from_behind(): return lax.ppermute(block, axis, route)]
    dot_general x39 -> x38, matrix products: 16.8 us -> 18.4 us  [matmul(): return jnp.einsum(spec, left, right, precision=HIGHEST)]
  transfers between devices with their start and end apart: 8 -> 4, of which waited for: 4 -> 4; matrix products, arithmetic and copies ran while one was open for 8% -> 6% of each run, Pallas kernels for 0% -> 0%
where the time goes in v5:
time: 130 us
  blocking collectives  52.7 us (41%)
  waiting for transfers between devices  38.5 us (30%)
  matrix products  18.4 us (14%)
  starting transfers between devices  9.24 us (7%)
  local copies, waits for them, and re-layouts  7.84 us (6%)
  other arithmetic  2.65 us (2%)
    ppermute x4, waiting for transfers between devices, from_behind(): return lax.ppermute(block, axis, route)  38.5 us
    all_to_all x1, blocking collectives, shards(): lax.all_to_all(arranged, 'line', split_axis=1, concat_axis=0, tiled=True)  32.5 us
    all_to_all x1, blocking collectives, shards(): lax.all_to_all(normed, 'line', split_axis=0, concat_axis=1, tiled=True)  20.2 us
    dot_general x38, matrix products, matmul(): return jnp.einsum(spec, left, right, precision=HIGHEST)  18.4 us
    ppermute x4, starting transfers between devices, from_behind(): return lax.ppermute(block, axis, route)  9.24 us
    unnamed x21, local copies, waits for them, and re-layouts  5.15 us
  transfers between devices with their start and end apart: 4, of which 4 were waited for; matrix products, arithmetic and copies ran while one was open for 6% of the time, Pallas kernels for 0%

profile of v5, /device:TPU:6, one launch (start us, length us, event | category | flops | bytes accessed | tf_op | source)
XLA Modules:
  0.0 130.0 jit_solution(13634027506247486254)
XLA Ops:
  0.2 0.8 fusion.90
  1.2 0.7 copy-done.7
  1.8 0.3 reduce_window_sum.22
  2.2 0.7 copy-done.5
  2.8 0.8 fusion.4
  3.6 0.3 fusion.64
  3.9 0.4 fusion.41
  4.3 0.4 convolution_add_fusion.5
  4.7 0.4 fusion.92
  5.3 0.4 fusion.93
  5.6 0.4 convolution_add_fusion.4
  6.0 0.4 convolution_add_fusion.3
  6.4 0.4 fusion.27
  6.8 0.4 convolution_subtract_fusion.3
  7.2 0.4 fusion.25
  7.6 0.4 convolution_subtract_fusion.2
  8.0 0.4 fusion.23
  8.5 0.4 convolution_subtract_fusion.1
  8.9 0.4 copy-done.1
  9.6 0.3 broadcast_multiply_fusion
  9.9 0.6 fusion.7
  10.5 0.8 fusion.32
  11.2 0.7 convolution_subtract_fusion.4
  12.2 3.7 %collective-permute-start = (f32[4,128,256]{2,1,0:T(8,128)S(1)}, f32[4,128,256]{2,1,0:T(8,128)S(1)}, u32[]{:S(2)}, u32[]{:S(2)}) collective-permute-start(f32[4,128,256]{2,1,0:T(8,128)S(1)} %pad_maximum_fusion), channel_id=1, source_target_pairs={{0,1},{1,2},{2,3},{3,4},{4,5},{5,6},{6,7},{7,8},{8,9},{9,10},{10,1... | collective-permute-start | bytes 1572872 | tf_op jit(solution)/shard_map/ppermute | solution.py:13
  15.9 0.6 copy-done.6
  16.6 0.2 reduce_window_sum.23
  17.3 0.7 copy-done.4
  17.9 0.7 fusion.6
  18.6 0.4 fusion.36
  19.0 0.4 convolution_add_fusion.2
  19.5 0.4 fusion.95
  19.8 0.5 copy-done
  20.4 0.5 convolution_multiply_fusion.4
  20.9 0.6 fusion.34
  21.5 0.3 copy-done.3
  21.9 0.4 fusion.96
  22.3 0.4 convolution_multiply_fusion.2
  22.7 0.4 convolution_add_fusion.1
  23.1 0.4 convolution_add_fusion
  23.5 6.4 %collective-permute-done = f32[4,128,256]{2,1,0:T(8,128)S(1)} collective-permute-done((f32[4,128,256]{2,1,0:T(8,128)S(1)}, f32[4,128,256]{2,1,0:T(8,128)S(1)}, u32[]{:S(2)}, u32[]{:S(2)}) %collective-permute-start) | collective-permute-done | bytes 524320 | tf_op jit(solution)/shard_map/ppermute | solution.py:13
  29.8 1.0 fusion.94
  31.0 3.0 %collective-permute-start.1 = (f32[4,128,256]{1,2,0:T(8,128)S(1)}, f32[4,128,256]{1,2,0:T(8,128)S(1)}, u32[]{:S(2)}, u32[]{:S(2)}) collective-permute-start(f32[4,128,256]{1,2,0:T(8,128)S(1)} %pad_maximum_fusion.1), channel_id=1, source_target_pairs={{0,2},{1,3},{2,4},{3,5},{4,6},{5,7},{6,8},{7,9},{8,10},{9,11},{10,... | collective-permute-start | bytes 1572872 | tf_op jit(solution)/shard_map/ppermute | solution.py:13
  34.0 0.4 fusion.20
  34.4 0.4 convolution_subtract_fusion
  34.8 13.3 %collective-permute-done.1 = f32[4,128,256]{1,2,0:T(8,128)S(1)} collective-permute-done((f32[4,128,256]{1,2,0:T(8,128)S(1)}, f32[4,128,256]{1,2,0:T(8,128)S(1)}, u32[]{:S(2)}, u32[]{:S(2)}) %collective-permute-start.1) | collective-permute-done | bytes 524320 | tf_op jit(solution)/shard_map/ppermute | solution.py:13
  48.1 0.6 fusion.81
  48.8 1.3 collective-permute-start.2
  50.1 0.4 convolution_multiply_fusion
  50.5 0.4 convolution_subtract_fusion.5
  50.9 11.6 %collective-permute-done.2 = f32[4,128,256]{1,2,0:T(8,128)S(1)} collective-permute-done((f32[4,128,256]{1,2,0:T(8,128)S(1)}, f32[4,128,256]{1,2,0:T(8,128)S(1)}, u32[]{:S(2)}, u32[]{:S(2)}) %collective-permute-start.2) | collective-permute-done | bytes 524320 | tf_op jit(solution)/shard_map/ppermute | solution.py:13
  62.5 0.4 convolution_add_fusion.6
  62.9 1.3 collective-permute-start.3
  64.2 0.6 fusion.16
  64.8 0.6 fusion.14
  65.4 7.3 %collective-permute-done.3 = f32[4,128,128]{1,2,0:T(8,128)S(1)} collective-permute-done((f32[4,128,128]{1,2,0:T(8,128)S(1)}, f32[4,128,128]{1,2,0:T(8,128)S(1)}, u32[]{:S(2)}, u32[]{:S(2)}) %collective-permute-start.3) | collective-permute-done | bytes 262176 | tf_op jit(solution)/shard_map/ppermute | solution.py:13
  72.7 0.7 convolution_add_fusion.8
  73.4 0.6 multiply_reduce_fusion.2
  74.0 0.7 copy-done.8
  74.9 32.5 %all_to_all.8 = bf16[1,32,4,512]{3,2,0,1:T(4,128)(2,1)S(1)} all-to-all(bf16[1,32,4,512]{3,2,0,1:T(4,128)(2,1)S(1)} %bitcast.116), channel_id=1, replica_groups=mesh['line'=32,'scan'=16] {'line'}, dimensions={1} | all-to-all | bytes 262144 | tf_op jit(solution)/shard_map/all_to_all | solution.py:189
  107.6 0.2 fusion.97
  108.2 0.5 copy-done.9
  108.7 0.2 fusion.19
  109.1 20.2 %all_to_all.9 = bf16[32,1,4,512]{3,2,1,0:T(4,128)(2,1)S(1)} all-to-all(bf16[32,1,4,512]{3,2,1,0:T(4,128)(2,1)S(1)} %copy.95), channel_id=1, replica_groups=mesh['line'=32,'scan'=16] {'line'}, dimensions={0} | all-to-all | bytes 262144 | tf_op jit(solution)/shard_map/all_to_all | solution.py:203
  129.3 0.7 reshape.266
  (64 shorter events, 2.6 us)
Async XLA Ops:
  1.2 0.7 copy-start.7
  2.2 0.7 copy-start.5
  8.4 0.9 copy-start.1
  12.1 4.7 %copy-start.2 = (bf16[32,1,4,512]{3,2,1,0:T(4,128)(2,1)S(1)}, bf16[32,1,4,512]{3,2,1,0:T(4,128)(2,1)}, u32[]{:S(2)}) copy-start(bf16[32,1,4,512]{3,2,1,0:T(4,128)(2,1)} %param.18) | copy-start | bytes 393220
  12.2 17.7 %collective-permute-start = (f32[4,128,256]{2,1,0:T(8,128)S(1)}, f32[4,128,256]{2,1,0:T(8,128)S(1)}, u32[]{:S(2)}, u32[]{:S(2)}) collective-permute-start(f32[4,128,256]{2,1,0:T(8,128)S(1)} %pad_maximum_fusion), channel_id=1, source_target_pairs={{0,1},{1,2},{2,3},{3,4},{4,5},{5,6},{6,7},{7,8},{8,9},{9,10},{10,1... | collective-permute-start | bytes 1572872 | tf_op jit(solution)/shard_map/ppermute | solution.py:13
  15.9 0.7 copy-start.6
  17.2 0.7 copy-start.4
  19.4 0.9 copy-start
  20.9 0.9 copy-start.3
  31.0 17.1 %collective-permute-start.1 = (f32[4,128,256]{1,2,0:T(8,128)S(1)}, f32[4,128,256]{1,2,0:T(8,128)S(1)}, u32[]{:S(2)}, u32[]{:S(2)}) collective-permute-start(f32[4,128,256]{1,2,0:T(8,128)S(1)} %pad_maximum_fusion.1), channel_id=1, source_target_pairs={{0,2},{1,3},{2,4},{3,5},{4,6},{5,7},{6,8},{7,9},{8,10},{9,11},{10,... | collective-permute-start | bytes 1572872 | tf_op jit(solution)/shard_map/ppermute | solution.py:13
  48.8 13.8 %collective-permute-start.2 = (f32[4,128,256]{1,2,0:T(8,128)S(1)}, f32[4,128,256]{1,2,0:T(8,128)S(1)}, u32[]{:S(2)}, u32[]{:S(2)}) collective-permute-start(f32[4,128,256]{1,2,0:T(8,128)S(1)} %pad_maximum_fusion.2), channel_id=1, source_target_pairs={{0,4},{1,5},{2,6},{3,7},{4,8},{5,9},{6,10},{7,11},{8,12},{9,13},{1... | collective-permute-start | bytes 1572872 | tf_op jit(solution)/shard_map/ppermute | solution.py:13
  62.9 9.8 %collective-permute-start.3 = (f32[4,128,128]{1,2,0:T(8,128)S(1)}, f32[4,128,128]{1,2,0:T(8,128)S(1)}, u32[]{:S(2)}, u32[]{:S(2)}) collective-permute-start(f32[4,128,128]{1,2,0:T(8,128)S(1)} %convolution_add_fusion.6), channel_id=1, source_target_pairs={{0,8},{1,9},{2,10},{3,11},{4,12},{5,13},{6,14},{7,15},{16,24},{17,... | collective-permute-start | bytes 786440 | tf_op jit(solution)/shard_map/ppermute | solution.py:13
  74.0 0.7 copy-start.8
  108.0 0.7 copy-start.9

commit v6 on v5

--- a/solution.py
+++ b/solution.py
@@ -106,15 +106,20 @@
     return array * lax.rsqrt(jnp.mean(array * array, axis=-1, keepdims=True) + 1e-05) * gain
 
 
-def prefix_states(transfer, offset):
+def prefix_states(transfer, offset, fillers):
     scan_count = lax.axis_size("scan")
     head_size = offset.shape[-1]
     ahead_transfer = jnp.zeros_like(transfer)
     ahead_offset = jnp.zeros_like(offset)
+    filled = []
     distance = 1
     while distance < scan_count:
         if 2 * distance < scan_count:
             arrived = from_behind(jnp.concatenate([transfer, offset], axis=-1), "scan", distance)
+            if len(filled) < len(fillers):
+                work, inputs = fillers[len(filled)]
+                inputs, arrived = lax.optimization_barrier((inputs, arrived))
+                filled.append(work(*inputs))
             composed = matmul("bij,bjv->biv", transfer, arrived)
             if distance == 1:
                 ahead_transfer = arrived[:, :, :head_size]
@@ -132,7 +137,8 @@
             else:
                 ahead_offset = matmul("bij,bjv->biv", ahead_transfer, arrived) + ahead_offset
         distance *= 2
-    return ahead_offset
+    filled += [work(*inputs) for work, inputs in fillers[len(filled):]]
+    return ahead_offset, filled
 
 
 def shards(
@@ -171,14 +177,25 @@
     transfer = ending[:, None, None] * identity - matmul("bjk,bjl->bkl", key_tail, weighted)
     offset = matmul("bjk,bjv->bkv", key_tail, updates)
 
-    operator = column_operator(
-        to_heads(columns(query_col), column_count, total_rows, head_count, head_size),
-        to_heads(columns(key_col), column_count, total_rows, head_count, head_size),
-        gates_to_heads(columns(decay_col), column_count, total_rows, head_count),
-        gates_to_heads(columns(beta_col), column_count, total_rows, head_count),
-    )
-
-    incoming = prefix_states(transfer, offset)
+    def column_part(query_part, key_part, decay_part, beta_part):
+        def part_columns(array):
+            return array.reshape(total_rows, query_part.shape[2], -1).transpose(1, 0, 2)
+
+        count = query_part.shape[2]
+        return column_operator(
+            to_heads(part_columns(query_part), count, total_rows, head_count, head_size),
+            to_heads(part_columns(key_part), count, total_rows, head_count, head_size),
+            gates_to_heads(part_columns(decay_part), count, total_rows, head_count),
+            gates_to_heads(part_columns(beta_part), count, total_rows, head_count),
+        )
+
+    column_inputs = (query_col, key_col, decay_col, beta_col)
+    half = column_count // 2 if column_count % 2 == 0 else column_count
+    fillers = [(column_part, tuple(piece[:, :, :half] for piece in column_inputs))]
+    if half < column_count:
+        fillers.append((column_part, tuple(piece[:, :, half:] for piece in column_inputs)))
+    incoming, operators = prefix_states(transfer, offset, fillers)
+    operator = jnp.concatenate(operators, axis=0)
     row_out = local_out + matmul("bik,bkv->biv", state_query, incoming)
     row_scan = from_heads(row_out, row_count, segment, head_count, head_size)
     values_col = (

time: 130 us -> 136 us (1.046)
  waiting for transfers between devices: 38.5 us -> 41.8 us
  matrix products: 18.4 us -> 19.8 us
    ppermute x4, waiting for transfers between devices: 38.5 us -> 41.8 us  [from_behind(): return lax.ppermute(block, axis, route)]
    dot_general x38 -> x49, matrix products: 18.4 us -> 19.8 us  [matmul(): return jnp.einsum(spec, left, right, precision=HIGHEST)]
    unnamed x21 -> x20, local copies, waits for them, and re-layouts: 5.15 us -> 4.85 us
  transfers between devices with their start and end apart: 4 -> 4, of which waited for: 4 -> 4; matrix products, arithmetic and copies ran while one was open for 6% -> 4% of each run, Pallas kernels for 0% -> 0%
where the time goes in v6:
time: 136 us; the launch traced here: 135 us
  blocking collectives  52.7 us (39%)
  waiting for transfers between devices  41.8 us (31%)
  matrix products  19.8 us (15%)
  starting transfers between devices  9.24 us (7%)
  local copies, waits for them, and re-layouts  7.86 us (6%)
  other arithmetic  2.93 us (2%)
    ppermute x4, waiting for transfers between devices, from_behind(): return lax.ppermute(block, axis, route)  41.8 us
    all_to_all x1, blocking collectives, shards(): lax.all_to_all(arranged, 'line', split_axis=1, concat_axis=0, tiled=True)  32.5 us
    all_to_all x1, blocking collectives, shards(): lax.all_to_all(normed, 'line', split_axis=0, concat_axis=1, tiled=True)  20.2 us
    dot_general x49, matrix products, matmul(): return jnp.einsum(spec, left, right, precision=HIGHEST)  19.8 us
    ppermute x4, starting transfers between devices, from_behind(): return lax.ppermute(block, axis, route)  9.24 us
    unnamed x20, local copies, waits for them, and re-layouts  4.85 us
  transfers between devices with their start and end apart: 4, of which 4 were waited for; matrix products, arithmetic and copies ran while one was open for 4% of the time, Pallas kernels for 0%

profile of v6, /device:TPU:6, one launch (start us, length us, event | category | flops | bytes accessed | tf_op | source)
XLA Modules:
  0.0 135.2 jit_solution(15028438429737318935)
XLA Ops:
  0.1 0.7 copy-done.7
  0.8 0.3 reduce_window_sum.28
  1.3 0.8 fusion.111
  2.4 0.7 copy-done.4
  3.0 0.8 fusion.3
  3.8 0.3 fusion.74
  4.1 0.4 fusion.38
  4.5 0.4 convolution_add_fusion.2
  4.9 0.4 fusion.117
  5.5 0.4 fusion.118
  5.9 0.4 convolution_add_fusion.1
  6.3 0.4 convolution_add_fusion
  6.7 0.4 fusion.27
  7.1 0.4 convolution_subtract_fusion.2
  7.5 0.4 fusion.25
  7.9 0.4 convolution_subtract_fusion.1
  8.3 0.4 fusion.23
  8.7 0.4 convolution_subtract_fusion
  9.1 0.5 copy-done.1
  9.7 0.3 broadcast_multiply_fusion
  9.9 0.6 fusion.10
  10.5 0.8 fusion.32
  11.3 0.7 convolution_subtract_fusion.3
  12.3 3.7 %collective-permute-start = (f32[4,128,256]{2,1,0:T(8,128)S(1)}, f32[4,128,256]{2,1,0:T(8,128)S(1)}, u32[]{:S(2)}, u32[]{:S(2)}) collective-permute-start(f32[4,128,256]{2,1,0:T(8,128)S(1)} %pad_maximum_fusion), channel_id=1, source_target_pairs={{0,1},{1,2},{2,3},{3,4},{4,5},{5,6},{6,7},{7,8},{8,9},{9,10},{10,1... | collective-permute-start | bytes 1572872 | tf_op jit(solution)/shard_map/ppermute | solution.py:13
  16.1 0.8 copy-done.2
  17.0 0.8 copy-done.3
  18.0 0.5 convolution_multiply_fusion.1
  18.9 0.6 fusion.34
  19.5 0.4 convolution_subtract_fusion.4
  19.9 10.0 %collective-permute-done = f32[4,128,256]{2,1,0:T(8,128)S(1)} collective-permute-done((f32[4,128,256]{2,1,0:T(8,128)S(1)}, f32[4,128,256]{2,1,0:T(8,128)S(1)}, u32[]{:S(2)}, u32[]{:S(2)}) %collective-permute-start) | collective-permute-done | bytes 524320 | tf_op jit(solution)/shard_map/ppermute | solution.py:13
  30.4 0.4 fusion.9
  30.8 0.3 fusion.63
  31.1 0.3 fusion.120
  31.3 0.3 convolution_add_fusion.11
  31.9 0.3 convolution_add_fusion.10
  32.1 1.1 fusion.119
  33.3 3.0 %collective-permute-start.1 = (f32[4,128,256]{1,2,0:T(8,128)S(1)}, f32[4,128,256]{1,2,0:T(8,128)S(1)}, u32[]{:S(2)}, u32[]{:S(2)}) collective-permute-start(f32[4,128,256]{1,2,0:T(8,128)S(1)} %pad_maximum_fusion.1), channel_id=1, source_target_pairs={{0,2},{1,3},{2,4},{3,5},{4,6},{5,7},{6,8},{7,9},{8,10},{9,11},{10,... | collective-permute-start | bytes 1572872 | tf_op jit(solution)/shard_map/ppermute | solution.py:13
  36.3 0.3 convolution_add_fusion.9
  36.6 0.3 fusion.44
  36.8 0.3 convolution_multiply_fusion.3
  37.7 12.7 %collective-permute-done.1 = f32[4,128,256]{1,2,0:T(8,128)S(1)} collective-permute-done((f32[4,128,256]{1,2,0:T(8,128)S(1)}, f32[4,128,256]{1,2,0:T(8,128)S(1)}, u32[]{:S(2)}, u32[]{:S(2)}) %collective-permute-start.1) | collective-permute-done | bytes 524320 | tf_op jit(solution)/shard_map/ppermute | solution.py:13
  50.8 0.4 fusion.6
  51.2 0.3 fusion.60
  51.5 0.3 convolution_add_fusion.8
  51.8 0.3 fusion.122
  52.0 0.6 fusion.100
  52.6 0.3 fusion.123
  53.4 0.3 fusion.41
  53.7 0.3 convolution_subtract_fusion.5
  54.0 1.3 collective-permute-start.2
  55.4 0.3 convolution_multiply_fusion.2
  55.9 0.6 fusion.21
  56.5 11.3 %collective-permute-done.2 = f32[4,128,256]{1,2,0:T(8,128)S(1)} collective-permute-done((f32[4,128,256]{1,2,0:T(8,128)S(1)}, f32[4,128,256]{1,2,0:T(8,128)S(1)}, u32[]{:S(2)}, u32[]{:S(2)}) %collective-permute-start.2) | collective-permute-done | bytes 524320 | tf_op jit(solution)/shard_map/ppermute | solution.py:13
  67.8 0.4 convolution_add_fusion.3
  68.2 1.3 collective-permute-start.3
  69.5 0.6 fusion.17
  70.1 7.8 %collective-permute-done.3 = f32[4,128,128]{1,2,0:T(8,128)S(1)} collective-permute-done((f32[4,128,128]{1,2,0:T(8,128)S(1)}, f32[4,128,128]{1,2,0:T(8,128)S(1)}, u32[]{:S(2)}, u32[]{:S(2)}) %collective-permute-start.3) | collective-permute-done | bytes 262176 | tf_op jit(solution)/shard_map/ppermute | solution.py:13
  78.0 0.7 convolution_add_fusion.5
  78.6 0.6 multiply_reduce_fusion.1
  79.3 0.7 copy-done.8
  80.2 32.5 %all_to_all.8 = bf16[1,32,4,512]{3,2,0,1:T(4,128)(2,1)S(1)} all-to-all(bf16[1,32,4,512]{3,2,0,1:T(4,128)(2,1)S(1)} %bitcast.148), channel_id=1, replica_groups=mesh['line'=32,'scan'=16] {'line'}, dimensions={1} | all-to-all | bytes 262144 | tf_op jit(solution)/shard_map/all_to_all | solution.py:206
  113.4 0.5 copy-done.9
  114.4 20.2 %all_to_all.9 = bf16[32,1,4,512]{3,2,1,0:T(4,128)(2,1)S(1)} all-to-all(bf16[32,1,4,512]{3,2,1,0:T(4,128)(2,1)S(1)} %copy.101), channel_id=1, replica_groups=mesh['line'=32,'scan'=16] {'line'}, dimensions={0} | all-to-all | bytes 262144 | tf_op jit(solution)/shard_map/all_to_all | solution.py:220
  134.5 0.7 reshape.312
  (90 shorter events, 5.6 us)
Async XLA Ops:
  0.1 0.7 copy-start.7
  2.3 0.7 copy-start.4
  8.7 0.9 copy-start.1
  12.2 3.8 %copy-start = (bf16[1,128,512]{2,1,0:T(8,128)(2,1)S(1)}, bf16[1,128,512]{2,1,0:T(8,128)(2,1)}, u32[]{:S(2)}) copy-start(bf16[1,128,512]{2,1,0:T(8,128)(2,1)} %param.11) | copy-start | bytes 393220
  12.3 17.7 %collective-permute-start = (f32[4,128,256]{2,1,0:T(8,128)S(1)}, f32[4,128,256]{2,1,0:T(8,128)S(1)}, u32[]{:S(2)}, u32[]{:S(2)}) collective-permute-start(f32[4,128,256]{2,1,0:T(8,128)S(1)} %pad_maximum_fusion), channel_id=1, source_target_pairs={{0,1},{1,2},{2,3},{3,4},{4,5},{5,6},{6,7},{7,8},{8,9},{9,10},{10,1... | collective-permute-start | bytes 1572872 | tf_op jit(solution)/shard_map/ppermute | solution.py:13
  16.0 0.9 copy-start.2
  16.9 0.9 copy-start.3
  18.0 0.7 copy-start.5
  18.0 0.7 copy-start.6
  33.3 17.1 %collective-permute-start.1 = (f32[4,128,256]{1,2,0:T(8,128)S(1)}, f32[4,128,256]{1,2,0:T(8,128)S(1)}, u32[]{:S(2)}, u32[]{:S(2)}) collective-permute-start(f32[4,128,256]{1,2,0:T(8,128)S(1)} %pad_maximum_fusion.1), channel_id=1, source_target_pairs={{0,2},{1,3},{2,4},{3,5},{4,6},{5,7},{6,8},{7,9},{8,10},{9,11},{10,... | collective-permute-start | bytes 1572872 | tf_op jit(solution)/shard_map/ppermute | solution.py:13
  54.0 13.8 %collective-permute-start.2 = (f32[4,128,256]{1,2,0:T(8,128)S(1)}, f32[4,128,256]{1,2,0:T(8,128)S(1)}, u32[]{:S(2)}, u32[]{:S(2)}) collective-permute-start(f32[4,128,256]{1,2,0:T(8,128)S(1)} %pad_maximum_fusion.2), channel_id=1, source_target_pairs={{0,4},{1,5},{2,6},{3,7},{4,8},{5,9},{6,10},{7,11},{8,12},{9,13},{1... | collective-permute-start | bytes 1572872 | tf_op jit(solution)/shard_map/ppermute | solution.py:13
  68.2 9.8 %collective-permute-start.3 = (f32[4,128,128]{1,2,0:T(8,128)S(1)}, f32[4,128,128]{1,2,0:T(8,128)S(1)}, u32[]{:S(2)}, u32[]{:S(2)}) collective-permute-start(f32[4,128,128]{1,2,0:T(8,128)S(1)} %convolution_add_fusion.3), channel_id=1, source_target_pairs={{0,8},{1,9},{2,10},{3,11},{4,12},{5,13},{6,14},{7,15},{16,24},{17,... | collective-permute-start | bytes 786440 | tf_op jit(solution)/shard_map/ppermute | solution.py:13
  79.3 0.7 copy-start.8
  113.3 0.7 copy-start.9

commit v7 on v5

--- a/solution.py
+++ b/solution.py
@@ -114,7 +114,7 @@
     distance = 1
     while distance < scan_count:
         if 2 * distance < scan_count:
-            arrived = from_behind(jnp.concatenate([transfer, offset], axis=-1), "scan", distance)
+            arrived = jnp.concatenate(from_behind((transfer, offset), "scan", distance), axis=-1)
             composed = matmul("bij,bjv->biv", transfer, arrived)
             if distance == 1:
                 ahead_transfer = arrived[:, :, :head_size]

time: 130 us -> 126 us (0.969)
  waiting for transfers between devices: 38.5 us -> 28.3 us
  starting transfers between devices: 9.24 us -> 15.9 us
    ppermute x4 -> x7, waiting for transfers between devices: 38.5 us -> 28.3 us  [from_behind(): return lax.ppermute(block, axis, route)]
    ppermute x4 -> x7, starting transfers between devices: 9.24 us -> 15.9 us  [from_behind(): return lax.ppermute(block, axis, route)]
    unnamed x21 -> x23, local copies, waits for them, and re-layouts: 5.15 us -> 4.82 us
  transfers between devices with their start and end apart: 4 -> 7, of which waited for: 4 -> 6; matrix products, arithmetic and copies ran while one was open for 6% -> 8% of each run, Pallas kernels for 0% -> 0%
where the time goes in v7:
time: 126 us; the launch traced here: 125 us
  blocking collectives  52.7 us (42%)
  waiting for transfers between devices  28.3 us (22%)
  matrix products  17.6 us (14%)
  starting transfers between devices  15.9 us (13%)
  local copies, waits for them, and re-layouts  7.42 us (6%)
  other arithmetic  2.55 us (2%)
    all_to_all x1, blocking collectives, shards(): lax.all_to_all(arranged, 'line', split_axis=1, concat_axis=0, tiled=True)  32.5 us
    ppermute x7, waiting for transfers between devices, from_behind(): return lax.ppermute(block, axis, route)  28.3 us
    all_to_all x1, blocking collectives, shards(): lax.all_to_all(normed, 'line', split_axis=0, concat_axis=1, tiled=True)  20.2 us
    dot_general x38, matrix products, matmul(): return jnp.einsum(spec, left, right, precision=HIGHEST)  17.6 us
    ppermute x7, starting transfers between devices, from_behind(): return lax.ppermute(block, axis, route)  15.9 us
    unnamed x23, local copies, waits for them, and re-layouts  4.82 us
  transfers between devices with their start and end apart: 7, of which 6 were waited for; matrix products, arithmetic and copies ran while one was open for 8% of the time, Pallas kernels for 0%

profile of v7, /device:TPU:6, one launch (start us, length us, event | category | flops | bytes accessed | tf_op | source)
XLA Modules:
  0.0 125.3 jit_solution(2751516491581087867)
XLA Ops:
  0.2 0.8 fusion.92
  1.2 0.7 copy-done.7
  1.9 0.3 reduce_window_sum.22
  2.2 0.7 copy-done.5
  2.8 0.8 fusion.4
  3.6 0.3 fusion.65
  3.9 0.4 fusion.42
  4.3 0.4 convolution_add_fusion.5
  4.7 0.4 fusion.94
  5.3 0.4 fusion.95
  5.6 0.4 convolution_add_fusion.4
  6.0 0.4 convolution_add_fusion.3
  6.4 0.4 fusion.28
  6.8 0.4 convolution_subtract_fusion.3
  7.3 0.4 fusion.26
  7.6 0.4 convolution_subtract_fusion.2
  8.1 0.4 fusion.24
  8.5 0.4 convolution_subtract_fusion.1
  8.9 0.4 copy-done.1
  9.7 0.6 fusion.7
  10.3 0.7 fusion.33
  11.0 3.5 %collective-permute-start.1 = (f32[4,128,128]{2,1,0:T(8,128)S(1)}, f32[4,128,128]{2,1,0:T(8,128)S(1)}, u32[]{:S(2)}, u32[]{:S(2)}) collective-permute-start(f32[4,128,128]{2,1,0:T(8,128)S(1)} %fusion.33), channel_id=1, source_target_pairs={{0,1},{1,2},{2,3},{3,4},{4,5},{5,6},{6,7},{7,8},{8,9},{9,10},{10,1... | collective-permute-start | bytes 786440 | tf_op jit(solution)/shard_map/ppermute | solution.py:13
  14.7 0.7 convolution_subtract_fusion.4
  15.5 3.7 %collective-permute-start = (f32[4,128,128]{2,1,0:T(8,128)S(1)}, f32[4,128,128]{2,1,0:T(8,128)S(1)}, u32[]{:S(2)}, u32[]{:S(2)}) collective-permute-start(f32[4,128,128]{2,1,0:T(8,128)S(1)} %convolution_subtract_fusion.4), channel_id=1, source_target_pairs={{0,1},{1,2},{2,3},{3,4},{4,5},{5,6},{6,7},{7,8},{8,9},{9,10},{10,1... | collective-permute-start | bytes 786440 | tf_op jit(solution)/shard_map/ppermute | solution.py:13
  19.3 0.7 copy-done.6
  20.7 0.7 copy-done.4
  21.3 0.7 fusion.6
  22.0 0.4 fusion.37
  22.4 0.4 convolution_add_fusion.2
  22.8 0.4 fusion.97
  23.3 0.5 convolution_multiply_fusion.4
  23.8 0.4 copy-done.3
  24.2 0.4 fusion.98
  24.6 0.4 convolution_add_fusion.1
  25.0 0.4 convolution_add_fusion
  25.4 0.4 fusion.21
  25.8 0.4 convolution_subtract_fusion
  26.2 0.4 convolution_subtract_fusion.5
  26.7 2.0 %collective-permute-done = f32[4,128,128]{2,1,0:T(8,128)S(1)} collective-permute-done((f32[4,128,128]{2,1,0:T(8,128)S(1)}, f32[4,128,128]{2,1,0:T(8,128)S(1)}, u32[]{:S(2)}, u32[]{:S(2)}) %collective-permute-start) | collective-permute-done | bytes 262176 | tf_op jit(solution)/shard_map/ppermute | solution.py:13
  28.7 0.6 fusion.11
  29.4 3.0 %collective-permute-start.2 = (f32[4,128,128]{2,1,0:T(8,128)S(1)}, f32[4,128,128]{2,1,0:T(8,128)S(1)}, u32[]{:S(2)}, u32[]{:S(2)}) collective-permute-start(f32[4,128,128]{2,1,0:T(8,128)S(1)} %get-tuple-element.11), channel_id=1, source_target_pairs={{0,2},{1,3},{2,4},{3,5},{4,6},{5,7},{6,8},{7,9},{8,10},{9,11},{10,... | collective-permute-start | bytes 786440 | tf_op jit(solution)/shard_map/ppermute | solution.py:13
  32.4 0.4 convolution_multiply_fusion.2
  32.8 1.9 %collective-permute-start.3 = (f32[4,128,128]{2,1,0:T(8,128)S(1)}, f32[4,128,128]{2,1,0:T(8,128)S(1)}, u32[]{:S(2)}, u32[]{:S(2)}) collective-permute-start(f32[4,128,128]{2,1,0:T(8,128)S(1)} %get-tuple-element.12), channel_id=1, source_target_pairs={{0,2},{1,3},{2,4},{3,5},{4,6},{5,7},{6,8},{7,9},{8,10},{9,11},{10,... | collective-permute-start | bytes 786440 | tf_op jit(solution)/shard_map/ppermute | solution.py:13
  34.7 0.4 convolution_multiply_fusion
  35.1 7.8 %collective-permute-done.2 = f32[4,128,128]{2,1,0:T(8,128)S(1)} collective-permute-done((f32[4,128,128]{2,1,0:T(8,128)S(1)}, f32[4,128,128]{2,1,0:T(8,128)S(1)}, u32[]{:S(2)}, u32[]{:S(2)}) %collective-permute-start.2) | collective-permute-done | bytes 262176 | tf_op jit(solution)/shard_map/ppermute | solution.py:13
  42.9 3.5 %collective-permute-done.3 = f32[4,128,128]{2,1,0:T(8,128)S(1)} collective-permute-done((f32[4,128,128]{2,1,0:T(8,128)S(1)}, f32[4,128,128]{2,1,0:T(8,128)S(1)}, u32[]{:S(2)}, u32[]{:S(2)}) %collective-permute-start.3) | collective-permute-done | bytes 262176 | tf_op jit(solution)/shard_map/ppermute | solution.py:13
  46.5 0.6 fusion.83
  47.1 1.3 %collective-permute-start.5 = (f32[4,128,128]{2,1,0:T(8,128)S(1)}, f32[4,128,128]{2,1,0:T(8,128)S(1)}, u32[]{:S(2)}, u32[]{:S(2)}) collective-permute-start(f32[4,128,128]{2,1,0:T(8,128)S(1)} %get-tuple-element.10), channel_id=1, source_target_pairs={{0,4},{1,5},{2,6},{3,7},{4,8},{5,9},{6,10},{7,11},{8,12},{9,13},{1... | collective-permute-start | bytes 786440 | tf_op jit(solution)/shard_map/ppermute | solution.py:13
  48.4 0.6 fusion.35
  49.0 1.3 %collective-permute-start.4 = (f32[4,128,128]{2,1,0:T(8,128)S(1)}, f32[4,128,128]{2,1,0:T(8,128)S(1)}, u32[]{:S(2)}, u32[]{:S(2)}) collective-permute-start(f32[4,128,128]{2,1,0:T(8,128)S(1)} %get-tuple-element.9), channel_id=1, source_target_pairs={{0,4},{1,5},{2,6},{3,7},{4,8},{5,9},{6,10},{7,11},{8,12},{9,13},{1... | collective-permute-start | bytes 786440 | tf_op jit(solution)/shard_map/ppermute | solution.py:13
  50.3 0.6 fusion.96
  50.9 7.2 %collective-permute-done.5 = f32[4,128,128]{2,1,0:T(8,128)S(1)} collective-permute-done((f32[4,128,128]{2,1,0:T(8,128)S(1)}, f32[4,128,128]{2,1,0:T(8,128)S(1)}, u32[]{:S(2)}, u32[]{:S(2)}) %collective-permute-start.5) | collective-permute-done | bytes 262176 | tf_op jit(solution)/shard_map/ppermute | solution.py:13
  58.1 0.4 convolution_add_fusion.6
  58.5 1.3 %collective-permute-start.6 = (f32[4,128,128]{2,1,0:T(8,128)S(1)}, f32[4,128,128]{2,1,0:T(8,128)S(1)}, u32[]{:S(2)}, u32[]{:S(2)}) collective-permute-start(f32[4,128,128]{2,1,0:T(8,128)S(1)} %convolution_add_fusion.6), channel_id=1, source_target_pairs={{0,8},{1,9},{2,10},{3,11},{4,12},{5,13},{6,14},{7,15},{16,24},{17,... | collective-permute-start | bytes 786440 | tf_op jit(solution)/shard_map/ppermute | solution.py:13
  59.8 1.1 collective-permute-done.4
  60.9 0.6 fusion.17
  61.5 6.7 %collective-permute-done.6 = f32[4,128,128]{2,1,0:T(8,128)S(1)} collective-permute-done((f32[4,128,128]{2,1,0:T(8,128)S(1)}, f32[4,128,128]{2,1,0:T(8,128)S(1)}, u32[]{:S(2)}, u32[]{:S(2)}) %collective-permute-start.6) | collective-permute-done | bytes 262176 | tf_op jit(solution)/shard_map/ppermute | solution.py:13
  68.2 0.4 convolution_add_fusion.8
  68.7 0.6 multiply_reduce_fusion.2
  69.3 0.7 copy-done.8
  70.2 32.5 %all_to_all.8 = bf16[1,32,4,512]{3,2,0,1:T(4,128)(2,1)S(1)} all-to-all(bf16[1,32,4,512]{3,2,0,1:T(4,128)(2,1)S(1)} %bitcast.117), channel_id=1, replica_groups=mesh['line'=32,'scan'=16] {'line'}, dimensions={1} | all-to-all | bytes 262144 | tf_op jit(solution)/shard_map/all_to_all | solution.py:189
  103.5 0.5 copy-done.9
  104.4 20.2 %all_to_all.9 = bf16[32,1,4,512]{3,2,1,0:T(4,128)(2,1)S(1)} all-to-all(bf16[32,1,4,512]{3,2,1,0:T(4,128)(2,1)S(1)} %copy.47), channel_id=1, replica_groups=mesh['line'=32,'scan'=16] {'line'}, dimensions={0} | all-to-all | bytes 262144 | tf_op jit(solution)/shard_map/all_to_all | solution.py:203
  124.6 0.7 reshape.266
  (70 shorter events, 3.4 us)
Async XLA Ops:
  1.2 0.7 copy-start.7
  2.2 0.7 copy-start.5
  8.5 0.9 copy-start.1
  11.0 15.6 %collective-permute-start.1 = (f32[4,128,128]{2,1,0:T(8,128)S(1)}, f32[4,128,128]{2,1,0:T(8,128)S(1)}, u32[]{:S(2)}, u32[]{:S(2)}) collective-permute-start(f32[4,128,128]{2,1,0:T(8,128)S(1)} %fusion.33), channel_id=1, source_target_pairs={{0,1},{1,2},{2,3},{3,4},{4,5},{5,6},{6,7},{7,8},{8,9},{9,10},{10,1... | collective-permute-start | bytes 786440 | tf_op jit(solution)/shard_map/ppermute | solution.py:13
  14.7 4.4 %copy-start = (bf16[1,128,512]{2,1,0:T(8,128)(2,1)S(1)}, bf16[1,128,512]{2,1,0:T(8,128)(2,1)}, u32[]{:S(2)}) copy-start(bf16[1,128,512]{2,1,0:T(8,128)(2,1)} %param.11) | copy-start | bytes 393220
  15.5 13.2 %collective-permute-start = (f32[4,128,128]{2,1,0:T(8,128)S(1)}, f32[4,128,128]{2,1,0:T(8,128)S(1)}, u32[]{:S(2)}, u32[]{:S(2)}) collective-permute-start(f32[4,128,128]{2,1,0:T(8,128)S(1)} %convolution_subtract_fusion.4), channel_id=1, source_target_pairs={{0,1},{1,2},{2,3},{3,4},{4,5},{5,6},{6,7},{7,8},{8,9},{9,10},{10,1... | collective-permute-start | bytes 786440 | tf_op jit(solution)/shard_map/ppermute | solution.py:13
  19.2 1.0 copy-start.2
  19.2 0.7 copy-start.6
  20.6 0.7 copy-start.4
  23.3 0.9 copy-start.3
  29.4 13.5 %collective-permute-start.2 = (f32[4,128,128]{2,1,0:T(8,128)S(1)}, f32[4,128,128]{2,1,0:T(8,128)S(1)}, u32[]{:S(2)}, u32[]{:S(2)}) collective-permute-start(f32[4,128,128]{2,1,0:T(8,128)S(1)} %get-tuple-element.11), channel_id=1, source_target_pairs={{0,2},{1,3},{2,4},{3,5},{4,6},{5,7},{6,8},{7,9},{8,10},{9,11},{10,... | collective-permute-start | bytes 786440 | tf_op jit(solution)/shard_map/ppermute | solution.py:13
  32.8 13.7 %collective-permute-start.3 = (f32[4,128,128]{2,1,0:T(8,128)S(1)}, f32[4,128,128]{2,1,0:T(8,128)S(1)}, u32[]{:S(2)}, u32[]{:S(2)}) collective-permute-start(f32[4,128,128]{2,1,0:T(8,128)S(1)} %get-tuple-element.12), channel_id=1, source_target_pairs={{0,2},{1,3},{2,4},{3,5},{4,6},{5,7},{6,8},{7,9},{8,10},{9,11},{10,... | collective-permute-start | bytes 786440 | tf_op jit(solution)/shard_map/ppermute | solution.py:13
  47.1 10.9 %collective-permute-start.5 = (f32[4,128,128]{2,1,0:T(8,128)S(1)}, f32[4,128,128]{2,1,0:T(8,128)S(1)}, u32[]{:S(2)}, u32[]{:S(2)}) collective-permute-start(f32[4,128,128]{2,1,0:T(8,128)S(1)} %get-tuple-element.10), channel_id=1, source_target_pairs={{0,4},{1,5},{2,6},{3,7},{4,8},{5,9},{6,10},{7,11},{8,12},{9,13},{1... | collective-permute-start | bytes 786440 | tf_op jit(solution)/shard_map/ppermute | solution.py:13
  49.0 11.9 %collective-permute-start.4 = (f32[4,128,128]{2,1,0:T(8,128)S(1)}, f32[4,128,128]{2,1,0:T(8,128)S(1)}, u32[]{:S(2)}, u32[]{:S(2)}) collective-permute-start(f32[4,128,128]{2,1,0:T(8,128)S(1)} %get-tuple-element.9), channel_id=1, source_target_pairs={{0,4},{1,5},{2,6},{3,7},{4,8},{5,9},{6,10},{7,11},{8,12},{9,13},{1... | collective-permute-start | bytes 786440 | tf_op jit(solution)/shard_map/ppermute | solution.py:13
  58.5 9.8 %collective-permute-start.6 = (f32[4,128,128]{2,1,0:T(8,128)S(1)}, f32[4,128,128]{2,1,0:T(8,128)S(1)}, u32[]{:S(2)}, u32[]{:S(2)}) collective-permute-start(f32[4,128,128]{2,1,0:T(8,128)S(1)} %convolution_add_fusion.6), channel_id=1, source_target_pairs={{0,8},{1,9},{2,10},{3,11},{4,12},{5,13},{6,14},{7,15},{16,24},{17,... | collective-permute-start | bytes 786440 | tf_op jit(solution)/shard_map/ppermute | solution.py:13
  69.3 0.7 copy-start.8
  103.3 0.7 copy-start.9

commit v8 on v7

--- a/solution.py
+++ b/solution.py
@@ -106,6 +106,11 @@
     return array * lax.rsqrt(jnp.mean(array * array, axis=-1, keepdims=True) + 1e-05) * gain
 
 
+def split_heads(array):
+    half = array.shape[0] // 2 if array.shape[0] % 2 == 0 else array.shape[0]
+    return tuple(array[start:start + half] for start in range(0, array.shape[0], half))
+
+
 def prefix_states(transfer, offset):
     scan_count = lax.axis_size("scan")
     head_size = offset.shape[-1]
@@ -114,7 +119,13 @@
     distance = 1
     while distance < scan_count:
         if 2 * distance < scan_count:
-            arrived = jnp.concatenate(from_behind((transfer, offset), "scan", distance), axis=-1)
+            arrived = jnp.concatenate(
+                [
+                    jnp.concatenate(from_behind(split_heads(part), "scan", distance), axis=0)
+                    for part in (transfer, offset)
+                ],
+                axis=-1,
+            )
             composed = matmul("bij,bjv->biv", transfer, arrived)
             if distance == 1:
                 ahead_transfer = arrived[:, :, :head_size]
@@ -126,7 +137,7 @@
             transfer = composed[:, :, :head_size]
             offset = composed[:, :, head_size:] + offset
         else:
-            arrived = from_behind(offset, "scan", distance)
+            arrived = jnp.concatenate(from_behind(split_heads(offset), "scan", distance), axis=0)
             if distance == 1:
                 ahead_offset = arrived
             else:

time: 126 us -> 139 us (1.10); the launches traced: 125 us -> 137 us
  starting transfers between devices: 15.9 us -> 27.9 us
  waiting for transfers between devices: 28.3 us -> 26.7 us
    ppermute x7 -> x14, starting transfers between devices: 15.9 us -> 27.9 us  [from_behind(): return lax.ppermute(block, axis, route)]
    ppermute x7 -> x14, waiting for transfers between devices: 28.3 us -> 26.7 us  [from_behind(): return lax.ppermute(block, axis, route)]
  transfers between devices with their start and end apart: 7 -> 14, of which waited for: 6 -> 10; matrix products, arithmetic and copies ran while one was open for 8% -> 7% of each run, Pallas kernels for 0% -> 0%
where the time goes in v8:
time: 139 us; the launch traced here: 137 us
  blocking collectives  52.6 us (38%)
  starting transfers between devices  27.9 us (20%)
  waiting for transfers between devices  26.7 us (19%)
  matrix products  17.6 us (13%)
  local copies, waits for them, and re-layouts  8.5 us (6%)
  other arithmetic  2.5 us (2%)
    all_to_all x1, blocking collectives, shards(): lax.all_to_all(arranged, 'line', split_axis=1, concat_axis=0, tiled=True)  32.5 us
    ppermute x14, starting transfers between devices, from_behind(): return lax.ppermute(block, axis, route)  27.9 us
    ppermute x14, waiting for transfers between devices, from_behind(): return lax.ppermute(block, axis, route)  26.7 us
    all_to_all x1, blocking collectives, shards(): lax.all_to_all(normed, 'line', split_axis=0, concat_axis=1, tiled=True)  20.2 us
    dot_general x38, matrix products, matmul(): return jnp.einsum(spec, left, right, precision=HIGHEST)  17.6 us
    unnamed x23, local copies, waits for them, and re-layouts  5.77 us
  transfers between devices with their start and end apart: 14, of which 10 were waited for; matrix products, arithmetic and copies ran while one was open for 7% of the time, Pallas kernels for 0%

profile of v8, /device:TPU:6, one launch (start us, length us, event | category | flops | bytes accessed | tf_op | source)
XLA Modules:
  0.0 136.7 jit_solution(3237389603519115324)
XLA Ops:
  0.1 0.7 copy-done.7
  1.3 0.8 fusion.120
  2.4 0.7 copy-done.5
  3.0 0.8 fusion.4
  4.5 0.4 convolution_add_fusion.5
  5.7 0.4 convolution_add_fusion.4
  6.1 0.4 convolution_add_fusion.3
  6.5 0.4 fusion.49
  6.9 0.4 convolution_subtract_fusion.3
  7.3 0.4 fusion.47
  7.7 0.4 convolution_subtract_fusion.2
  8.1 0.4 fusion.45
  8.5 0.4 convolution_subtract_fusion.1
  8.9 0.5 copy-done.1
  9.8 0.6 fusion.7
  10.4 0.7 fusion.54
  11.1 3.5 %collective-permute-start.3 = (f32[2,128,128]{2,1,0:T(8,128)S(1)}, f32[2,128,128]{2,1,0:T(8,128)S(1)}, u32[]{:S(2)}, u32[]{:S(2)}) collective-permute-start(f32[2,128,128]{2,1,0:T(8,128)S(1)} %get-tuple-element.27), channel_id=1, source_target_pairs={{0,1},{1,2},{2,3},{3,4},{4,5},{5,6},{6,7},{7,8},{8,9},{9,10},{10,1... | collective-permute-start | bytes 393224 | tf_op jit(solution)/shard_map/ppermute | solution.py:13
  14.6 3.5 %collective-permute-start.2 = (f32[2,128,128]{2,1,0:T(8,128)S(1)}, f32[2,128,128]{2,1,0:T(8,128)S(1)}, u32[]{:S(2)}, u32[]{:S(2)}) collective-permute-start(f32[2,128,128]{2,1,0:T(8,128)S(1)} %get-tuple-element.28), channel_id=1, source_target_pairs={{0,1},{1,2},{2,3},{3,4},{4,5},{5,6},{6,7},{7,8},{8,9},{9,10},{10,1... | collective-permute-start | bytes 393224 | tf_op jit(solution)/shard_map/ppermute | solution.py:13
  18.3 0.7 convolution_subtract_fusion.4
  19.1 3.3 %collective-permute-start.1 = (f32[2,128,128]{2,1,0:T(8,128)S(1)}, f32[2,128,128]{2,1,0:T(8,128)S(1)}, u32[]{:S(2)}, u32[]{:S(2)}) collective-permute-start(f32[2,128,128]{2,1,0:T(8,128)S(1)} %get-tuple-element.25), channel_id=1, source_target_pairs={{0,1},{1,2},{2,3},{3,4},{4,5},{5,6},{6,7},{7,8},{8,9},{9,10},{10,1... | collective-permute-start | bytes 393224 | tf_op jit(solution)/shard_map/ppermute | solution.py:13
  22.4 2.1 %collective-permute-start = (f32[2,128,128]{2,1,0:T(8,128)S(1)}, f32[2,128,128]{2,1,0:T(8,128)S(1)}, u32[]{:S(2)}, u32[]{:S(2)}) collective-permute-start(f32[2,128,128]{2,1,0:T(8,128)S(1)} %get-tuple-element.26), channel_id=1, source_target_pairs={{0,1},{1,2},{2,3},{3,4},{4,5},{5,6},{6,7},{7,8},{8,9},{9,10},{10,1... | collective-permute-start | bytes 393224 | tf_op jit(solution)/shard_map/ppermute | solution.py:13
  24.7 0.6 copy-done.6
  25.9 0.7 copy-done.4
  26.6 0.7 fusion.6
  27.7 0.4 convolution_add_fusion.2
  28.5 0.5 copy-done
  29.1 0.9 copy-done.3
  30.0 0.4 convolution_multiply_fusion.2
  30.8 0.4 convolution_add_fusion.1
  32.4 0.5 convolution_multiply_fusion.4
  32.9 0.4 convolution_subtract_fusion.5
  33.9 0.6 fusion.11
  34.6 2.0 %collective-permute-start.6 = (f32[2,128,128]{2,1,0:T(8,128)S(1)}, f32[2,128,128]{2,1,0:T(8,128)S(1)}, u32[]{:S(2)}, u32[]{:S(2)}) collective-permute-start(f32[2,128,128]{2,1,0:T(8,128)S(1)} %get-tuple-element.23), channel_id=1, source_target_pairs={{0,2},{1,3},{2,4},{3,5},{4,6},{5,7},{6,8},{7,9},{8,10},{9,11},{10,... | collective-permute-start | bytes 393224 | tf_op jit(solution)/shard_map/ppermute | solution.py:13
  36.5 1.9 %collective-permute-start.7 = (f32[2,128,128]{2,1,0:T(8,128)S(1)}, f32[2,128,128]{2,1,0:T(8,128)S(1)}, u32[]{:S(2)}, u32[]{:S(2)}) collective-permute-start(f32[2,128,128]{2,1,0:T(8,128)S(1)} %get-tuple-element.24), channel_id=1, source_target_pairs={{0,2},{1,3},{2,4},{3,5},{4,6},{5,7},{6,8},{7,9},{8,10},{9,11},{10,... | collective-permute-start | bytes 393224 | tf_op jit(solution)/shard_map/ppermute | solution.py:13
  38.5 1.9 %collective-permute-start.4 = (f32[2,128,128]{2,1,0:T(8,128)S(1)}, f32[2,128,128]{2,1,0:T(8,128)S(1)}, u32[]{:S(2)}, u32[]{:S(2)}) collective-permute-start(f32[2,128,128]{2,1,0:T(8,128)S(1)} %get-tuple-element.11), channel_id=1, source_target_pairs={{0,2},{1,3},{2,4},{3,5},{4,6},{5,7},{6,8},{7,9},{8,10},{9,11},{10,... | collective-permute-start | bytes 393224 | tf_op jit(solution)/shard_map/ppermute | solution.py:13
  40.4 1.9 %collective-permute-start.5 = (f32[2,128,128]{2,1,0:T(8,128)S(1)}, f32[2,128,128]{2,1,0:T(8,128)S(1)}, u32[]{:S(2)}, u32[]{:S(2)}) collective-permute-start(f32[2,128,128]{2,1,0:T(8,128)S(1)} %get-tuple-element.12), channel_id=1, source_target_pairs={{0,2},{1,3},{2,4},{3,5},{4,6},{5,7},{6,8},{7,9},{8,10},{9,11},{10,... | collective-permute-start | bytes 393224 | tf_op jit(solution)/shard_map/ppermute | solution.py:13
  42.3 0.6 fusion.56
  42.9 2.0 %collective-permute-done.6 = f32[2,128,128]{2,1,0:T(8,128)S(1)} collective-permute-done((f32[2,128,128]{2,1,0:T(8,128)S(1)}, f32[2,128,128]{2,1,0:T(8,128)S(1)}, u32[]{:S(2)}, u32[]{:S(2)}) %collective-permute-start.6) | collective-permute-done | bytes 131104 | tf_op jit(solution)/shard_map/ppermute | solution.py:13
  44.9 2.8 %collective-permute-done.7 = f32[2,128,128]{2,1,0:T(8,128)S(1)} collective-permute-done((f32[2,128,128]{2,1,0:T(8,128)S(1)}, f32[2,128,128]{2,1,0:T(8,128)S(1)}, u32[]{:S(2)}, u32[]{:S(2)}) %collective-permute-start.7) | collective-permute-done | bytes 131104 | tf_op jit(solution)/shard_map/ppermute | solution.py:13
  47.7 2.8 %collective-permute-done.4 = f32[2,128,128]{2,1,0:T(8,128)S(1)} collective-permute-done((f32[2,128,128]{2,1,0:T(8,128)S(1)}, f32[2,128,128]{2,1,0:T(8,128)S(1)}, u32[]{:S(2)}, u32[]{:S(2)}) %collective-permute-start.4) | collective-permute-done | bytes 131104 | tf_op jit(solution)/shard_map/ppermute | solution.py:13
  50.5 1.7 %collective-permute-done.5 = f32[2,128,128]{2,1,0:T(8,128)S(1)} collective-permute-done((f32[2,128,128]{2,1,0:T(8,128)S(1)}, f32[2,128,128]{2,1,0:T(8,128)S(1)}, u32[]{:S(2)}, u32[]{:S(2)}) %collective-permute-start.5) | collective-permute-done | bytes 131104 | tf_op jit(solution)/shard_map/ppermute | solution.py:13
  52.2 0.6 fusion.23
  52.9 1.3 collective-permute-start.10
  54.2 1.3 collective-permute-start.11
  55.5 1.3 collective-permute-start.8
  56.8 1.3 collective-permute-start.9
  58.1 0.6 fusion.24
  58.7 3.9 %collective-permute-done.10 = f32[2,128,128]{2,1,0:T(8,128)S(1)} collective-permute-done((f32[2,128,128]{2,1,0:T(8,128)S(1)}, f32[2,128,128]{2,1,0:T(8,128)S(1)}, u32[]{:S(2)}, u32[]{:S(2)}) %collective-permute-start.10) | collective-permute-done | bytes 131104 | tf_op jit(solution)/shard_map/ppermute | solution.py:13
  62.6 2.8 %collective-permute-done.11 = f32[2,128,128]{2,1,0:T(8,128)S(1)} collective-permute-done((f32[2,128,128]{2,1,0:T(8,128)S(1)}, f32[2,128,128]{2,1,0:T(8,128)S(1)}, u32[]{:S(2)}, u32[]{:S(2)}) %collective-permute-start.11) | collective-permute-done | bytes 131104 | tf_op jit(solution)/shard_map/ppermute | solution.py:13
  65.4 2.4 %collective-permute-done.8 = f32[2,128,128]{2,1,0:T(8,128)S(1)} collective-permute-done((f32[2,128,128]{2,1,0:T(8,128)S(1)}, f32[2,128,128]{2,1,0:T(8,128)S(1)}, u32[]{:S(2)}, u32[]{:S(2)}) %collective-permute-start.8) | collective-permute-done | bytes 131104 | tf_op jit(solution)/shard_map/ppermute | solution.py:13
  67.8 1.4 %collective-permute-done.9 = f32[2,128,128]{2,1,0:T(8,128)S(1)} collective-permute-done((f32[2,128,128]{2,1,0:T(8,128)S(1)}, f32[2,128,128]{2,1,0:T(8,128)S(1)}, u32[]{:S(2)}, u32[]{:S(2)}) %collective-permute-start.9) | collective-permute-done | bytes 131104 | tf_op jit(solution)/shard_map/ppermute | solution.py:13
  69.2 0.4 convolution_add_fusion.6
  69.6 1.3 collective-permute-start.12
  70.9 1.3 collective-permute-start.13
  72.2 0.6 fusion.15
  72.8 5.5 %collective-permute-done.12 = f32[2,128,128]{2,1,0:T(8,128)S(1)} collective-permute-done((f32[2,128,128]{2,1,0:T(8,128)S(1)}, f32[2,128,128]{2,1,0:T(8,128)S(1)}, u32[]{:S(2)}, u32[]{:S(2)}) %collective-permute-start.12) | collective-permute-done | bytes 131104 | tf_op jit(solution)/shard_map/ppermute | solution.py:13
  78.3 1.4 %collective-permute-done.13 = f32[2,128,128]{2,1,0:T(8,128)S(1)} collective-permute-done((f32[2,128,128]{2,1,0:T(8,128)S(1)}, f32[2,128,128]{2,1,0:T(8,128)S(1)}, u32[]{:S(2)}, u32[]{:S(2)}) %collective-permute-start.13) | collective-permute-done | bytes 131104 | tf_op jit(solution)/shard_map/ppermute | solution.py:13
  79.7 0.4 convolution_add_fusion.8
  80.1 0.6 multiply_reduce_fusion.2
  80.8 0.7 copy-done.8
  81.7 32.5 %all_to_all.8 = bf16[1,32,4,512]{3,2,0,1:T(4,128)(2,1)S(1)} all-to-all(bf16[1,32,4,512]{3,2,0,1:T(4,128)(2,1)S(1)} %bitcast.112), channel_id=1, replica_groups=mesh['line'=32,'scan'=16] {'line'}, dimensions={1} | all-to-all | bytes 262144 | tf_op jit(solution)/shard_map/all_to_all | solution.py:200
  114.9 0.5 copy-done.9
  115.9 20.2 %all_to_all.9 = bf16[32,1,4,512]{3,2,1,0:T(4,128)(2,1)S(1)} all-to-all(bf16[32,1,4,512]{3,2,1,0:T(4,128)(2,1)S(1)} %copy.47), channel_id=1, replica_groups=mesh['line'=32,'scan'=16] {'line'}, dimensions={0} | all-to-all | bytes 262144 | tf_op jit(solution)/shard_map/all_to_all | solution.py:214
  136.0 0.7 reshape.266
  (91 shorter events, 7.8 us)
Async XLA Ops:
  0.1 0.7 copy-start.7
  2.3 0.7 copy-start.5
  8.5 0.9 copy-start.1
  11.1 22.7 %collective-permute-start.3 = (f32[2,128,128]{2,1,0:T(8,128)S(1)}, f32[2,128,128]{2,1,0:T(8,128)S(1)}, u32[]{:S(2)}, u32[]{:S(2)}) collective-permute-start(f32[2,128,128]{2,1,0:T(8,128)S(1)} %get-tuple-element.27), channel_id=1, source_target_pairs={{0,1},{1,2},{2,3},{3,4},{4,5},{5,6},{6,7},{7,8},{8,9},{9,10},{10,1... | collective-permute-start | bytes 393224 | tf_op jit(solution)/shard_map/ppermute | solution.py:13
  14.6 19.1 %collective-permute-start.2 = (f32[2,128,128]{2,1,0:T(8,128)S(1)}, f32[2,128,128]{2,1,0:T(8,128)S(1)}, u32[]{:S(2)}, u32[]{:S(2)}) collective-permute-start(f32[2,128,128]{2,1,0:T(8,128)S(1)} %get-tuple-element.28), channel_id=1, source_target_pairs={{0,1},{1,2},{2,3},{3,4},{4,5},{5,6},{6,7},{7,8},{8,9},{9,10},{10,1... | collective-permute-start | bytes 393224 | tf_op jit(solution)/shard_map/ppermute | solution.py:13
  19.1 6.4 %copy-start.2 = (bf16[32,1,4,512]{3,2,1,0:T(4,128)(2,1)S(1)}, bf16[32,1,4,512]{3,2,1,0:T(4,128)(2,1)}, u32[]{:S(2)}) copy-start(bf16[32,1,4,512]{3,2,1,0:T(4,128)(2,1)} %param.18) | copy-start | bytes 393220
  19.1 14.7 %collective-permute-start.1 = (f32[2,128,128]{2,1,0:T(8,128)S(1)}, f32[2,128,128]{2,1,0:T(8,128)S(1)}, u32[]{:S(2)}, u32[]{:S(2)}) collective-permute-start(f32[2,128,128]{2,1,0:T(8,128)S(1)} %get-tuple-element.25), channel_id=1, source_target_pairs={{0,1},{1,2},{2,3},{3,4},{4,5},{5,6},{6,7},{7,8},{8,9},{9,10},{10,1... | collective-permute-start | bytes 393224 | tf_op jit(solution)/shard_map/ppermute | solution.py:13
  22.4 11.4 %collective-permute-start = (f32[2,128,128]{2,1,0:T(8,128)S(1)}, f32[2,128,128]{2,1,0:T(8,128)S(1)}, u32[]{:S(2)}, u32[]{:S(2)}) collective-permute-start(f32[2,128,128]{2,1,0:T(8,128)S(1)} %get-tuple-element.26), channel_id=1, source_target_pairs={{0,1},{1,2},{2,3},{3,4},{4,5},{5,6},{6,7},{7,8},{8,9},{9,10},{10,1... | collective-permute-start | bytes 393224 | tf_op jit(solution)/shard_map/ppermute | solution.py:13
  24.6 0.7 copy-start.6
  25.9 0.7 copy-start.4
  28.1 0.9 copy-start
  29.0 0.9 copy-start.3
  34.6 10.4 %collective-permute-start.6 = (f32[2,128,128]{2,1,0:T(8,128)S(1)}, f32[2,128,128]{2,1,0:T(8,128)S(1)}, u32[]{:S(2)}, u32[]{:S(2)}) collective-permute-start(f32[2,128,128]{2,1,0:T(8,128)S(1)} %get-tuple-element.23), channel_id=1, source_target_pairs={{0,2},{1,3},{2,4},{3,5},{4,6},{5,7},{6,8},{7,9},{8,10},{9,11},{10,... | collective-permute-start | bytes 393224 | tf_op jit(solution)/shard_map/ppermute | solution.py:13
  36.5 11.2 %collective-permute-start.7 = (f32[2,128,128]{2,1,0:T(8,128)S(1)}, f32[2,128,128]{2,1,0:T(8,128)S(1)}, u32[]{:S(2)}, u32[]{:S(2)}) collective-permute-start(f32[2,128,128]{2,1,0:T(8,128)S(1)} %get-tuple-element.24), channel_id=1, source_target_pairs={{0,2},{1,3},{2,4},{3,5},{4,6},{5,7},{6,8},{7,9},{8,10},{9,11},{10,... | collective-permute-start | bytes 393224 | tf_op jit(solution)/shard_map/ppermute | solution.py:13
  38.5 12.1 %collective-permute-start.4 = (f32[2,128,128]{2,1,0:T(8,128)S(1)}, f32[2,128,128]{2,1,0:T(8,128)S(1)}, u32[]{:S(2)}, u32[]{:S(2)}) collective-permute-start(f32[2,128,128]{2,1,0:T(8,128)S(1)} %get-tuple-element.11), channel_id=1, source_target_pairs={{0,2},{1,3},{2,4},{3,5},{4,6},{5,7},{6,8},{7,9},{8,10},{9,11},{10,... | collective-permute-start | bytes 393224 | tf_op jit(solution)/shard_map/ppermute | solution.py:13
  40.4 11.9 %collective-permute-start.5 = (f32[2,128,128]{2,1,0:T(8,128)S(1)}, f32[2,128,128]{2,1,0:T(8,128)S(1)}, u32[]{:S(2)}, u32[]{:S(2)}) collective-permute-start(f32[2,128,128]{2,1,0:T(8,128)S(1)} %get-tuple-element.12), channel_id=1, source_target_pairs={{0,2},{1,3},{2,4},{3,5},{4,6},{5,7},{6,8},{7,9},{8,10},{9,11},{10,... | collective-permute-start | bytes 393224 | tf_op jit(solution)/shard_map/ppermute | solution.py:13
  52.9 9.7 %collective-permute-start.10 = (f32[2,128,128]{2,1,0:T(8,128)S(1)}, f32[2,128,128]{2,1,0:T(8,128)S(1)}, u32[]{:S(2)}, u32[]{:S(2)}) collective-permute-start(f32[2,128,128]{2,1,0:T(8,128)S(1)} %get-tuple-element.21), channel_id=1, source_target_pairs={{0,4},{1,5},{2,6},{3,7},{4,8},{5,9},{6,10},{7,11},{8,12},{9,13},{1... | collective-permute-start | bytes 393224 | tf_op jit(solution)/shard_map/ppermute | solution.py:13
  54.2 11.2 %collective-permute-start.11 = (f32[2,128,128]{2,1,0:T(8,128)S(1)}, f32[2,128,128]{2,1,0:T(8,128)S(1)}, u32[]{:S(2)}, u32[]{:S(2)}) collective-permute-start(f32[2,128,128]{2,1,0:T(8,128)S(1)} %get-tuple-element.22), channel_id=1, source_target_pairs={{0,4},{1,5},{2,6},{3,7},{4,8},{5,9},{6,10},{7,11},{8,12},{9,13},{1... | collective-permute-start | bytes 393224 | tf_op jit(solution)/shard_map/ppermute | solution.py:13
  55.5 12.3 %collective-permute-start.8 = (f32[2,128,128]{2,1,0:T(8,128)S(1)}, f32[2,128,128]{2,1,0:T(8,128)S(1)}, u32[]{:S(2)}, u32[]{:S(2)}) collective-permute-start(f32[2,128,128]{2,1,0:T(8,128)S(1)} %get-tuple-element.9), channel_id=1, source_target_pairs={{0,4},{1,5},{2,6},{3,7},{4,8},{5,9},{6,10},{7,11},{8,12},{9,13},{1... | collective-permute-start | bytes 393224 | tf_op jit(solution)/shard_map/ppermute | solution.py:13
  56.8 12.4 %collective-permute-start.9 = (f32[2,128,128]{2,1,0:T(8,128)S(1)}, f32[2,128,128]{2,1,0:T(8,128)S(1)}, u32[]{:S(2)}, u32[]{:S(2)}) collective-permute-start(f32[2,128,128]{2,1,0:T(8,128)S(1)} %get-tuple-element.10), channel_id=1, source_target_pairs={{0,4},{1,5},{2,6},{3,7},{4,8},{5,9},{6,10},{7,11},{8,12},{9,13},{1... | collective-permute-start | bytes 393224 | tf_op jit(solution)/shard_map/ppermute | solution.py:13
  69.6 8.7 %collective-permute-start.12 = (f32[2,128,128]{2,1,0:T(8,128)S(1)}, f32[2,128,128]{2,1,0:T(8,128)S(1)}, u32[]{:S(2)}, u32[]{:S(2)}) collective-permute-start(f32[2,128,128]{2,1,0:T(8,128)S(1)} %get-tuple-element.19), channel_id=1, source_target_pairs={{0,8},{1,9},{2,10},{3,11},{4,12},{5,13},{6,14},{7,15},{16,24},{17,... | collective-permute-start | bytes 393224 | tf_op jit(solution)/shard_map/ppermute | solution.py:13
  70.9 8.8 %collective-permute-start.13 = (f32[2,128,128]{2,1,0:T(8,128)S(1)}, f32[2,128,128]{2,1,0:T(8,128)S(1)}, u32[]{:S(2)}, u32[]{:S(2)}) collective-permute-start(f32[2,128,128]{2,1,0:T(8,128)S(1)} %get-tuple-element.20), channel_id=1, source_target_pairs={{0,8},{1,9},{2,10},{3,11},{4,12},{5,13},{6,14},{7,15},{16,24},{17,... | collective-permute-start | bytes 393224 | tf_op jit(solution)/shard_map/ppermute | solution.py:13
  80.7 0.7 copy-start.8
  114.8 0.7 copy-start.9

commit v9 on v7

--- a/solution.py
+++ b/solution.py
@@ -106,6 +106,11 @@
     return array * lax.rsqrt(jnp.mean(array * array, axis=-1, keepdims=True) + 1e-05) * gain
 
 
+def split_heads(array):
+    half = array.shape[0] // 2 if array.shape[0] % 2 == 0 else array.shape[0]
+    return tuple(array[start:start + half] for start in range(0, array.shape[0], half))
+
+
 def prefix_states(transfer, offset):
     scan_count = lax.axis_size("scan")
     head_size = offset.shape[-1]
@@ -126,7 +131,7 @@
             transfer = composed[:, :, :head_size]
             offset = composed[:, :, head_size:] + offset
         else:
-            arrived = from_behind(offset, "scan", distance)
+            arrived = jnp.concatenate(from_behind(split_heads(offset), "scan", distance), axis=0)
             if distance == 1:
                 ahead_offset = arrived
             else:

time: 126 us -> 126 us (level)
  waiting for transfers between devices: 28.3 us -> 26.1 us
  starting transfers between devices: 15.9 us -> 17.2 us
    ppermute x7 -> x8, waiting for transfers between devices: 28.3 us -> 26.1 us  [from_behind(): return lax.ppermute(block, axis, route)]
    ppermute x7 -> x8, starting transfers between devices: 15.9 us -> 17.2 us  [from_behind(): return lax.ppermute(block, axis, route)]
  transfers between devices with their start and end apart: 7 -> 8, of which waited for: 6 -> 6; matrix products, arithmetic and copies ran while one was open for 8% -> 8% of each run, Pallas kernels for 0% -> 0%
where the time goes in v9:
time: 126 us; the launch traced here: 125 us
  blocking collectives  52.7 us (42%)
  waiting for transfers between devices  26.1 us (21%)
  matrix products  17.6 us (14%)
  starting transfers between devices  17.2 us (14%)
  local copies, waits for them, and re-layouts  8.41 us (7%)
  other arithmetic  2.55 us (2%)
    all_to_all x1, blocking collectives, shards(): lax.all_to_all(arranged, 'line', split_axis=1, concat_axis=0, tiled=True)  32.5 us
    ppermute x8, waiting for transfers between devices, from_behind(): return lax.ppermute(block, axis, route)  26.1 us
    all_to_all x1, blocking collectives, shards(): lax.all_to_all(normed, 'line', split_axis=0, concat_axis=1, tiled=True)  20.2 us
    dot_general x38, matrix products, matmul(): return jnp.einsum(spec, left, right, precision=HIGHEST)  17.6 us
    ppermute x8, starting transfers between devices, from_behind(): return lax.ppermute(block, axis, route)  17.2 us
    unnamed x23, local copies, waits for them, and re-layouts  5.79 us
  transfers between devices with their start and end apart: 8, of which 6 were waited for; matrix products, arithmetic and copies ran while one was open for 8% of the time, Pallas kernels for 0%

profile of v9, /device:TPU:6, one launch (start us, length us, event | category | flops | bytes accessed | tf_op | source)
XLA Modules:
  0.0 125.4 jit_solution(11076086741898155901)
XLA Ops:
  0.1 0.7 copy-done.7
  1.3 0.8 fusion.95
  2.4 0.7 copy-done.5
  3.0 0.8 fusion.4
  4.1 0.4 fusion.45
  4.5 0.4 convolution_add_fusion.5
  4.9 0.4 fusion.97
  5.3 0.4 fusion.98
  5.7 0.4 convolution_add_fusion.4
  6.1 0.4 convolution_add_fusion.3
  6.5 0.4 fusion.31
  6.9 0.4 convolution_subtract_fusion.3
  7.3 0.4 fusion.29
  7.7 0.4 convolution_subtract_fusion.2
  8.1 0.4 fusion.27
  8.5 0.4 convolution_subtract_fusion.1
  9.0 0.5 copy-done.1
  9.8 0.6 fusion.7
  10.4 0.7 fusion.36
  11.1 3.5 %collective-permute-start.1 = (f32[4,128,128]{2,1,0:T(8,128)S(1)}, f32[4,128,128]{2,1,0:T(8,128)S(1)}, u32[]{:S(2)}, u32[]{:S(2)}) collective-permute-start(f32[4,128,128]{2,1,0:T(8,128)S(1)} %fusion.36), channel_id=1, source_target_pairs={{0,1},{1,2},{2,3},{3,4},{4,5},{5,6},{6,7},{7,8},{8,9},{9,10},{10,1... | collective-permute-start | bytes 786440 | tf_op jit(solution)/shard_map/ppermute | solution.py:13
  14.8 0.7 convolution_subtract_fusion.4
  15.5 3.7 %collective-permute-start = (f32[4,128,128]{2,1,0:T(8,128)S(1)}, f32[4,128,128]{2,1,0:T(8,128)S(1)}, u32[]{:S(2)}, u32[]{:S(2)}) collective-permute-start(f32[4,128,128]{2,1,0:T(8,128)S(1)} %convolution_subtract_fusion.4), channel_id=1, source_target_pairs={{0,1},{1,2},{2,3},{3,4},{4,5},{5,6},{6,7},{7,8},{8,9},{9,10},{10,1... | collective-permute-start | bytes 786440 | tf_op jit(solution)/shard_map/ppermute | solution.py:13
  19.4 0.6 copy-done.6
  20.6 0.7 copy-done.4
  21.3 0.7 fusion.6
  22.0 0.4 fusion.40
  22.4 0.4 convolution_add_fusion.2
  22.8 0.4 fusion.100
  23.2 0.5 copy-done
  23.8 0.9 copy-done.3
  24.7 0.4 fusion.101
  25.1 0.4 convolution_add_fusion.1
  25.5 0.4 convolution_add_fusion
  25.9 0.4 fusion.24
  26.3 0.4 convolution_subtract_fusion
  26.7 0.5 convolution_multiply_fusion.4
  27.2 0.4 convolution_subtract_fusion.5
  27.6 1.2 collective-permute-done
  28.8 0.6 fusion.11
  29.4 3.0 %collective-permute-start.2 = (f32[4,128,128]{2,1,0:T(8,128)S(1)}, f32[4,128,128]{2,1,0:T(8,128)S(1)}, u32[]{:S(2)}, u32[]{:S(2)}) collective-permute-start(f32[4,128,128]{2,1,0:T(8,128)S(1)} %get-tuple-element.12), channel_id=1, source_target_pairs={{0,2},{1,3},{2,4},{3,5},{4,6},{5,7},{6,8},{7,9},{8,10},{9,11},{10,... | collective-permute-start | bytes 786440 | tf_op jit(solution)/shard_map/ppermute | solution.py:13
  32.4 0.4 convolution_multiply_fusion.2
  32.9 1.9 %collective-permute-start.3 = (f32[4,128,128]{2,1,0:T(8,128)S(1)}, f32[4,128,128]{2,1,0:T(8,128)S(1)}, u32[]{:S(2)}, u32[]{:S(2)}) collective-permute-start(f32[4,128,128]{2,1,0:T(8,128)S(1)} %get-tuple-element.11), channel_id=1, source_target_pairs={{0,2},{1,3},{2,4},{3,5},{4,6},{5,7},{6,8},{7,9},{8,10},{9,11},{10,... | collective-permute-start | bytes 786440 | tf_op jit(solution)/shard_map/ppermute | solution.py:13
  34.8 0.4 convolution_multiply_fusion
  35.2 7.8 %collective-permute-done.2 = f32[4,128,128]{2,1,0:T(8,128)S(1)} collective-permute-done((f32[4,128,128]{2,1,0:T(8,128)S(1)}, f32[4,128,128]{2,1,0:T(8,128)S(1)}, u32[]{:S(2)}, u32[]{:S(2)}) %collective-permute-start.2) | collective-permute-done | bytes 262176 | tf_op jit(solution)/shard_map/ppermute | solution.py:13
  43.0 3.5 %collective-permute-done.3 = f32[4,128,128]{2,1,0:T(8,128)S(1)} collective-permute-done((f32[4,128,128]{2,1,0:T(8,128)S(1)}, f32[4,128,128]{2,1,0:T(8,128)S(1)}, u32[]{:S(2)}, u32[]{:S(2)}) %collective-permute-start.3) | collective-permute-done | bytes 262176 | tf_op jit(solution)/shard_map/ppermute | solution.py:13
  46.5 0.6 fusion.87
  47.2 1.3 %collective-permute-start.5 = (f32[4,128,128]{2,1,0:T(8,128)S(1)}, f32[4,128,128]{2,1,0:T(8,128)S(1)}, u32[]{:S(2)}, u32[]{:S(2)}) collective-permute-start(f32[4,128,128]{2,1,0:T(8,128)S(1)} %get-tuple-element.9), channel_id=1, source_target_pairs={{0,4},{1,5},{2,6},{3,7},{4,8},{5,9},{6,10},{7,11},{8,12},{9,13},{1... | collective-permute-start | bytes 786440 | tf_op jit(solution)/shard_map/ppermute | solution.py:13
  48.5 0.6 fusion.38
  49.1 1.3 %collective-permute-start.4 = (f32[4,128,128]{2,1,0:T(8,128)S(1)}, f32[4,128,128]{2,1,0:T(8,128)S(1)}, u32[]{:S(2)}, u32[]{:S(2)}) collective-permute-start(f32[4,128,128]{2,1,0:T(8,128)S(1)} %get-tuple-element.10), channel_id=1, source_target_pairs={{0,4},{1,5},{2,6},{3,7},{4,8},{5,9},{6,10},{7,11},{8,12},{9,13},{1... | collective-permute-start | bytes 786440 | tf_op jit(solution)/shard_map/ppermute | solution.py:13
  50.4 0.6 fusion.99
  51.0 7.2 %collective-permute-done.5 = f32[4,128,128]{2,1,0:T(8,128)S(1)} collective-permute-done((f32[4,128,128]{2,1,0:T(8,128)S(1)}, f32[4,128,128]{2,1,0:T(8,128)S(1)}, u32[]{:S(2)}, u32[]{:S(2)}) %collective-permute-start.5) | collective-permute-done | bytes 262176 | tf_op jit(solution)/shard_map/ppermute | solution.py:13
  58.1 0.4 convolution_add_fusion.6
  58.6 1.3 %collective-permute-start.6 = (f32[2,128,128]{2,1,0:T(8,128)S(1)}, f32[2,128,128]{2,1,0:T(8,128)S(1)}, u32[]{:S(2)}, u32[]{:S(2)}) collective-permute-start(f32[2,128,128]{2,1,0:T(8,128)S(1)} %get-tuple-element.19), channel_id=1, source_target_pairs={{0,8},{1,9},{2,10},{3,11},{4,12},{5,13},{6,14},{7,15},{16,24},{17,... | collective-permute-start | bytes 393224 | tf_op jit(solution)/shard_map/ppermute | solution.py:13
  59.9 1.3 %collective-permute-start.7 = (f32[2,128,128]{2,1,0:T(8,128)S(1)}, f32[2,128,128]{2,1,0:T(8,128)S(1)}, u32[]{:S(2)}, u32[]{:S(2)}) collective-permute-start(f32[2,128,128]{2,1,0:T(8,128)S(1)} %get-tuple-element.20), channel_id=1, source_target_pairs={{0,8},{1,9},{2,10},{3,11},{4,12},{5,13},{6,14},{7,15},{16,24},{17,... | collective-permute-start | bytes 393224 | tf_op jit(solution)/shard_map/ppermute | solution.py:13
  61.2 0.6 fusion.17
  61.8 5.1 %collective-permute-done.6 = f32[2,128,128]{2,1,0:T(8,128)S(1)} collective-permute-done((f32[2,128,128]{2,1,0:T(8,128)S(1)}, f32[2,128,128]{2,1,0:T(8,128)S(1)}, u32[]{:S(2)}, u32[]{:S(2)}) %collective-permute-start.6) | collective-permute-done | bytes 131104 | tf_op jit(solution)/shard_map/ppermute | solution.py:13
  66.9 1.4 %collective-permute-done.7 = f32[2,128,128]{2,1,0:T(8,128)S(1)} collective-permute-done((f32[2,128,128]{2,1,0:T(8,128)S(1)}, f32[2,128,128]{2,1,0:T(8,128)S(1)}, u32[]{:S(2)}, u32[]{:S(2)}) %collective-permute-start.7) | collective-permute-done | bytes 131104 | tf_op jit(solution)/shard_map/ppermute | solution.py:13
  68.3 0.4 convolution_add_fusion.8
  68.8 0.6 multiply_reduce_fusion.2
  69.4 0.7 copy-done.8
  70.3 32.5 %all_to_all.8 = bf16[1,32,4,512]{3,2,0,1:T(4,128)(2,1)S(1)} all-to-all(bf16[1,32,4,512]{3,2,0,1:T(4,128)(2,1)S(1)} %bitcast.116), channel_id=1, replica_groups=mesh['line'=32,'scan'=16] {'line'}, dimensions={1} | all-to-all | bytes 262144 | tf_op jit(solution)/shard_map/all_to_all | solution.py:194
  103.6 0.5 copy-done.9
  104.5 20.2 %all_to_all.9 = bf16[32,1,4,512]{3,2,1,0:T(4,128)(2,1)S(1)} all-to-all(bf16[32,1,4,512]{3,2,1,0:T(4,128)(2,1)S(1)} %copy.47), channel_id=1, replica_groups=mesh['line'=32,'scan'=16] {'line'}, dimensions={0} | all-to-all | bytes 262144 | tf_op jit(solution)/shard_map/all_to_all | solution.py:208
  124.7 0.7 reshape.266
  (73 shorter events, 4.0 us)
Async XLA Ops:
  0.1 0.7 copy-start.7
  2.3 0.7 copy-start.5
  8.5 0.9 copy-start.1
  11.1 16.5 %collective-permute-start.1 = (f32[4,128,128]{2,1,0:T(8,128)S(1)}, f32[4,128,128]{2,1,0:T(8,128)S(1)}, u32[]{:S(2)}, u32[]{:S(2)}) collective-permute-start(f32[4,128,128]{2,1,0:T(8,128)S(1)} %fusion.36), channel_id=1, source_target_pairs={{0,1},{1,2},{2,3},{3,4},{4,5},{5,6},{6,7},{7,8},{8,9},{9,10},{10,1... | collective-permute-start | bytes 786440 | tf_op jit(solution)/shard_map/ppermute | solution.py:13
  14.8 5.4 %copy-start.2 = (bf16[32,1,4,512]{3,2,1,0:T(4,128)(2,1)S(1)}, bf16[32,1,4,512]{3,2,1,0:T(4,128)(2,1)}, u32[]{:S(2)}) copy-start(bf16[32,1,4,512]{3,2,1,0:T(4,128)(2,1)} %param.18) | copy-start | bytes 393220
  15.5 13.2 %collective-permute-start = (f32[4,128,128]{2,1,0:T(8,128)S(1)}, f32[4,128,128]{2,1,0:T(8,128)S(1)}, u32[]{:S(2)}, u32[]{:S(2)}) collective-permute-start(f32[4,128,128]{2,1,0:T(8,128)S(1)} %convolution_subtract_fusion.4), channel_id=1, source_target_pairs={{0,1},{1,2},{2,3},{3,4},{4,5},{5,6},{6,7},{7,8},{8,9},{9,10},{10,1... | collective-permute-start | bytes 786440 | tf_op jit(solution)/shard_map/ppermute | solution.py:13
  19.3 0.7 copy-start.6
  20.6 0.7 copy-start.4
  22.8 0.9 copy-start
  23.7 0.9 copy-start.3
  29.4 13.5 %collective-permute-start.2 = (f32[4,128,128]{2,1,0:T(8,128)S(1)}, f32[4,128,128]{2,1,0:T(8,128)S(1)}, u32[]{:S(2)}, u32[]{:S(2)}) collective-permute-start(f32[4,128,128]{2,1,0:T(8,128)S(1)} %get-tuple-element.12), channel_id=1, source_target_pairs={{0,2},{1,3},{2,4},{3,5},{4,6},{5,7},{6,8},{7,9},{8,10},{9,11},{10,... | collective-permute-start | bytes 786440 | tf_op jit(solution)/shard_map/ppermute | solution.py:13
  32.9 13.7 %collective-permute-start.3 = (f32[4,128,128]{2,1,0:T(8,128)S(1)}, f32[4,128,128]{2,1,0:T(8,128)S(1)}, u32[]{:S(2)}, u32[]{:S(2)}) collective-permute-start(f32[4,128,128]{2,1,0:T(8,128)S(1)} %get-tuple-element.11), channel_id=1, source_target_pairs={{0,2},{1,3},{2,4},{3,5},{4,6},{5,7},{6,8},{7,9},{8,10},{9,11},{10,... | collective-permute-start | bytes 786440 | tf_op jit(solution)/shard_map/ppermute | solution.py:13
  47.2 10.9 %collective-permute-start.5 = (f32[4,128,128]{2,1,0:T(8,128)S(1)}, f32[4,128,128]{2,1,0:T(8,128)S(1)}, u32[]{:S(2)}, u32[]{:S(2)}) collective-permute-start(f32[4,128,128]{2,1,0:T(8,128)S(1)} %get-tuple-element.9), channel_id=1, source_target_pairs={{0,4},{1,5},{2,6},{3,7},{4,8},{5,9},{6,10},{7,11},{8,12},{9,13},{1... | collective-permute-start | bytes 786440 | tf_op jit(solution)/shard_map/ppermute | solution.py:13
  49.1 12.1 %collective-permute-start.4 = (f32[4,128,128]{2,1,0:T(8,128)S(1)}, f32[4,128,128]{2,1,0:T(8,128)S(1)}, u32[]{:S(2)}, u32[]{:S(2)}) collective-permute-start(f32[4,128,128]{2,1,0:T(8,128)S(1)} %get-tuple-element.10), channel_id=1, source_target_pairs={{0,4},{1,5},{2,6},{3,7},{4,8},{5,9},{6,10},{7,11},{8,12},{9,13},{1... | collective-permute-start | bytes 786440 | tf_op jit(solution)/shard_map/ppermute | solution.py:13
  58.6 8.4 %collective-permute-start.6 = (f32[2,128,128]{2,1,0:T(8,128)S(1)}, f32[2,128,128]{2,1,0:T(8,128)S(1)}, u32[]{:S(2)}, u32[]{:S(2)}) collective-permute-start(f32[2,128,128]{2,1,0:T(8,128)S(1)} %get-tuple-element.19), channel_id=1, source_target_pairs={{0,8},{1,9},{2,10},{3,11},{4,12},{5,13},{6,14},{7,15},{16,24},{17,... | collective-permute-start | bytes 393224 | tf_op jit(solution)/shard_map/ppermute | solution.py:13
  59.9 8.5 %collective-permute-start.7 = (f32[2,128,128]{2,1,0:T(8,128)S(1)}, f32[2,128,128]{2,1,0:T(8,128)S(1)}, u32[]{:S(2)}, u32[]{:S(2)}) collective-permute-start(f32[2,128,128]{2,1,0:T(8,128)S(1)} %get-tuple-element.20), channel_id=1, source_target_pairs={{0,8},{1,9},{2,10},{3,11},{4,12},{5,13},{6,14},{7,15},{16,24},{17,... | collective-permute-start | bytes 393224 | tf_op jit(solution)/shard_map/ppermute | solution.py:13
  69.4 0.7 copy-start.8
  103.4 0.7 copy-start.9

commit v10 on v7

--- a/solution.py
+++ b/solution.py
@@ -71,10 +71,11 @@
     updates = solved[:, :, :value_size]
     weighted = solved[:, :, value_size:]
     attend = ratios * matmul("bik,bjk->bij", query_block, key_unit)
-    local_out = matmul("bij,bjv->biv", attend, updates)
-    state_query = growth[:, :, None] * query_block - matmul("bij,bjk->bik", attend, weighted)
+    attended = matmul("bij,bjv->biv", attend, solved)
+    local_out = attended[:, :, :value_size]
+    state_query = growth[:, :, None] * query_block - attended[:, :, value_size:]
     key_tail = jnp.exp(cumulative[:, -1:] - cumulative)[:, :, None] * key_unit
-    return (local_out, state_query, key_tail, weighted, updates, growth[:, -1])
+    return (local_out, state_query, key_tail, solved, growth[:, -1])
 
 
 def column_operator(query_block, key_block, log_decay, beta_block):
@@ -158,7 +159,7 @@
     def columns(array):
         return array.reshape(total_rows, column_count, -1).transpose(1, 0, 2)
 
-    local_out, state_query, key_tail, weighted, updates, ending = block_terms(
+    local_out, state_query, key_tail, solved, ending = block_terms(
         to_heads(query_row, row_count, segment, head_count, head_size),
         to_heads(key_row, row_count, segment, head_count, head_size),
         to_heads(value_row, row_count, segment, head_count, head_size),
@@ -168,8 +169,9 @@
     identity = jnp.broadcast_to(
         jnp.eye(head_size, dtype=jnp.float32), (row_count * head_count, head_size, head_size)
     )
-    transfer = ending[:, None, None] * identity - matmul("bjk,bjl->bkl", key_tail, weighted)
-    offset = matmul("bjk,bjv->bkv", key_tail, updates)
+    tail_solved = matmul("bjk,bjv->bkv", key_tail, solved)
+    transfer = ending[:, None, None] * identity - tail_solved[:, :, head_size:]
+    offset = tail_solved[:, :, :head_size]
 
     operator = column_operator(
         to_heads(columns(query_col), column_count, total_rows, head_count, head_size),

time: 126 us -> 126 us (level)
    dot_general x38 -> x36, matrix products: 17.6 us -> 16.5 us  [matmul(): return jnp.einsum(spec, left, right, precision=HIGHEST)]
  transfers between devices with their start and end apart: 7 -> 7, of which waited for: 6 -> 6; matrix products, arithmetic and copies ran while one was open for 8% -> 6% of each run, Pallas kernels for 0% -> 0%
where the time goes in v10:
time: 126 us
  blocking collectives  52.6 us (42%)
  waiting for transfers between devices  28.8 us (23%)
  matrix products  16.5 us (13%)
  starting transfers between devices  15.9 us (13%)
  local copies, waits for them, and re-layouts  8.49 us (7%)
  other arithmetic  2.68 us (2%)
    all_to_all x1, blocking collectives, shards(): lax.all_to_all(arranged, 'line', split_axis=1, concat_axis=0, tiled=True)  32.5 us
    ppermute x7, waiting for transfers between devices, from_behind(): return lax.ppermute(block, axis, route)  28.8 us
    all_to_all x1, blocking collectives, shards(): lax.all_to_all(normed, 'line', split_axis=0, concat_axis=1, tiled=True)  20.2 us
    dot_general x36, matrix products, matmul(): return jnp.einsum(spec, left, right, precision=HIGHEST)  16.5 us
    ppermute x7, starting transfers between devices, from_behind(): return lax.ppermute(block, axis, route)  15.9 us
    unnamed x23, local copies, waits for them, and re-layouts  5.76 us
  transfers between devices with their start and end apart: 7, of which 6 were waited for; matrix products, arithmetic and copies ran while one was open for 6% of the time, Pallas kernels for 0%

profile of v10, /device:TPU:6, one launch (start us, length us, event | category | flops | bytes accessed | tf_op | source)
XLA Modules:
  0.0 125.7 jit_solution(11086918376883652228)
XLA Ops:
  0.2 0.8 fusion.89
  1.2 0.7 copy-done.7
  1.9 0.3 reduce_window_sum.22
  2.2 0.7 copy-done.5
  2.8 0.8 fusion.4
  3.6 0.3 fusion.60
  3.9 0.4 fusion.37
  4.3 0.4 convolution_add_fusion.5
  4.7 0.4 fusion.91
  5.3 0.4 fusion.92
  5.6 0.4 convolution_add_fusion.4
  6.0 0.4 convolution_add_fusion.3
  6.4 0.4 fusion.31
  6.8 0.4 convolution_subtract_fusion.3
  7.2 0.4 fusion.29
  7.6 0.4 convolution_subtract_fusion.2
  8.0 0.4 fusion.27
  8.5 0.4 convolution_subtract_fusion.1
  8.9 0.4 copy-done.1
  9.6 0.3 broadcast_multiply_fusion
  9.9 0.6 fusion.7
  10.5 0.8 fusion.24
  11.4 3.5 %collective-permute-start.1 = (f32[4,128,128]{2,1,0:T(8,128)S(1)}, f32[4,128,128]{2,1,0:T(8,128)S(1)}, u32[]{:S(2)}, u32[]{:S(2)}) collective-permute-start(f32[4,128,128]{2,1,0:T(8,128)S(1)} %get-tuple-element.13), channel_id=1, source_target_pairs={{0,1},{1,2},{2,3},{3,4},{4,5},{5,6},{6,7},{7,8},{8,9},{9,10},{10,1... | collective-permute-start | bytes 786440 | tf_op jit(solution)/shard_map/ppermute | solution.py:13
  14.9 3.7 %collective-permute-start = (f32[4,128,128]{2,1,0:T(8,128)S(1)}, f32[4,128,128]{2,1,0:T(8,128)S(1)}, u32[]{:S(2)}, u32[]{:S(2)}) collective-permute-start(f32[4,128,128]{2,1,0:T(8,128)S(1)} %get-tuple-element.14), channel_id=1, source_target_pairs={{0,1},{1,2},{2,3},{3,4},{4,5},{5,6},{6,7},{7,8},{8,9},{9,10},{10,1... | collective-permute-start | bytes 786440 | tf_op jit(solution)/shard_map/ppermute | solution.py:13
  18.6 0.6 copy-done.6
  19.9 0.7 copy-done.4
  20.6 0.7 fusion.6
  21.3 0.4 fusion.34
  21.7 0.4 convolution_add_fusion.2
  22.1 0.4 fusion.95
  22.5 0.5 copy-done
  23.1 0.9 copy-done.3
  24.0 0.4 convolution_multiply_fusion.2
  24.4 0.4 fusion.96
  24.8 0.4 convolution_add_fusion.1
  25.2 0.4 convolution_add_fusion
  25.6 0.4 fusion.21
  26.0 0.4 convolution_subtract_fusion
  26.4 0.5 convolution_multiply_fusion.4
  26.9 0.6 fusion.93
  27.5 1.5 %collective-permute-done = f32[4,128,128]{2,1,0:T(8,128)S(1)} collective-permute-done((f32[4,128,128]{2,1,0:T(8,128)S(1)}, f32[4,128,128]{2,1,0:T(8,128)S(1)}, u32[]{:S(2)}, u32[]{:S(2)}) %collective-permute-start) | collective-permute-done | bytes 262176 | tf_op jit(solution)/shard_map/ppermute | solution.py:13
  29.0 0.6 fusion.11
  29.7 3.0 %collective-permute-start.2 = (f32[4,128,128]{2,1,0:T(8,128)S(1)}, f32[4,128,128]{2,1,0:T(8,128)S(1)}, u32[]{:S(2)}, u32[]{:S(2)}) collective-permute-start(f32[4,128,128]{2,1,0:T(8,128)S(1)} %get-tuple-element.11), channel_id=1, source_target_pairs={{0,2},{1,3},{2,4},{3,5},{4,6},{5,7},{6,8},{7,9},{8,10},{9,11},{10,... | collective-permute-start | bytes 786440 | tf_op jit(solution)/shard_map/ppermute | solution.py:13
  32.7 0.4 convolution_multiply_fusion
  33.1 1.9 %collective-permute-start.3 = (f32[4,128,128]{2,1,0:T(8,128)S(1)}, f32[4,128,128]{2,1,0:T(8,128)S(1)}, u32[]{:S(2)}, u32[]{:S(2)}) collective-permute-start(f32[4,128,128]{2,1,0:T(8,128)S(1)} %get-tuple-element.12), channel_id=1, source_target_pairs={{0,2},{1,3},{2,4},{3,5},{4,6},{5,7},{6,8},{7,9},{8,10},{9,11},{10,... | collective-permute-start | bytes 786440 | tf_op jit(solution)/shard_map/ppermute | solution.py:13
  35.0 8.2 %collective-permute-done.2 = f32[4,128,128]{2,1,0:T(8,128)S(1)} collective-permute-done((f32[4,128,128]{2,1,0:T(8,128)S(1)}, f32[4,128,128]{2,1,0:T(8,128)S(1)}, u32[]{:S(2)}, u32[]{:S(2)}) %collective-permute-start.2) | collective-permute-done | bytes 262176 | tf_op jit(solution)/shard_map/ppermute | solution.py:13
  43.2 3.5 %collective-permute-done.3 = f32[4,128,128]{2,1,0:T(8,128)S(1)} collective-permute-done((f32[4,128,128]{2,1,0:T(8,128)S(1)}, f32[4,128,128]{2,1,0:T(8,128)S(1)}, u32[]{:S(2)}, u32[]{:S(2)}) %collective-permute-start.3) | collective-permute-done | bytes 262176 | tf_op jit(solution)/shard_map/ppermute | solution.py:13
  46.8 0.6 fusion.78
  47.5 1.3 %collective-permute-start.5 = (f32[4,128,128]{2,1,0:T(8,128)S(1)}, f32[4,128,128]{2,1,0:T(8,128)S(1)}, u32[]{:S(2)}, u32[]{:S(2)}) collective-permute-start(f32[4,128,128]{2,1,0:T(8,128)S(1)} %get-tuple-element.10), channel_id=1, source_target_pairs={{0,4},{1,5},{2,6},{3,7},{4,8},{5,9},{6,10},{7,11},{8,12},{9,13},{1... | collective-permute-start | bytes 786440 | tf_op jit(solution)/shard_map/ppermute | solution.py:13
  48.8 1.3 %collective-permute-start.4 = (f32[4,128,128]{2,1,0:T(8,128)S(1)}, f32[4,128,128]{2,1,0:T(8,128)S(1)}, u32[]{:S(2)}, u32[]{:S(2)}) collective-permute-start(f32[4,128,128]{2,1,0:T(8,128)S(1)} %get-tuple-element.9), channel_id=1, source_target_pairs={{0,4},{1,5},{2,6},{3,7},{4,8},{5,9},{6,10},{7,11},{8,12},{9,13},{1... | collective-permute-start | bytes 786440 | tf_op jit(solution)/shard_map/ppermute | solution.py:13
  50.1 0.6 fusion.94
  50.7 7.7 %collective-permute-done.5 = f32[4,128,128]{2,1,0:T(8,128)S(1)} collective-permute-done((f32[4,128,128]{2,1,0:T(8,128)S(1)}, f32[4,128,128]{2,1,0:T(8,128)S(1)}, u32[]{:S(2)}, u32[]{:S(2)}) %collective-permute-start.5) | collective-permute-done | bytes 262176 | tf_op jit(solution)/shard_map/ppermute | solution.py:13
  58.4 0.4 convolution_add_fusion.6
  58.8 1.3 %collective-permute-start.6 = (f32[4,128,128]{2,1,0:T(8,128)S(1)}, f32[4,128,128]{2,1,0:T(8,128)S(1)}, u32[]{:S(2)}, u32[]{:S(2)}) collective-permute-start(f32[4,128,128]{2,1,0:T(8,128)S(1)} %convolution_add_fusion.6), channel_id=1, source_target_pairs={{0,8},{1,9},{2,10},{3,11},{4,12},{5,13},{6,14},{7,15},{16,24},{17,... | collective-permute-start | bytes 786440 | tf_op jit(solution)/shard_map/ppermute | solution.py:13
  60.1 1.1 collective-permute-done.4
  61.3 0.6 fusion.17
  61.9 6.7 %collective-permute-done.6 = f32[4,128,128]{2,1,0:T(8,128)S(1)} collective-permute-done((f32[4,128,128]{2,1,0:T(8,128)S(1)}, f32[4,128,128]{2,1,0:T(8,128)S(1)}, u32[]{:S(2)}, u32[]{:S(2)}) %collective-permute-start.6) | collective-permute-done | bytes 262176 | tf_op jit(solution)/shard_map/ppermute | solution.py:13
  68.6 0.4 convolution_add_fusion.8
  69.0 0.6 multiply_reduce_fusion.2
  69.6 0.6 copy-done.8
  70.7 32.5 %all_to_all.8 = bf16[1,32,4,512]{3,2,0,1:T(4,128)(2,1)S(1)} all-to-all(bf16[1,32,4,512]{3,2,0,1:T(4,128)(2,1)S(1)} %bitcast.116), channel_id=1, replica_groups=mesh['line'=32,'scan'=16] {'line'}, dimensions={1} | all-to-all | bytes 262144 | tf_op jit(solution)/shard_map/all_to_all | solution.py:191
  103.9 0.5 copy-done.9
  104.9 20.2 %all_to_all.9 = bf16[32,1,4,512]{3,2,1,0:T(4,128)(2,1)S(1)} all-to-all(bf16[32,1,4,512]{3,2,1,0:T(4,128)(2,1)S(1)} %copy.45), channel_id=1, replica_groups=mesh['line'=32,'scan'=16] {'line'}, dimensions={0} | all-to-all | bytes 262144 | tf_op jit(solution)/shard_map/all_to_all | solution.py:205
  125.0 0.7 reshape.266
  (70 shorter events, 3.4 us)
Async XLA Ops:
  1.2 0.7 copy-start.7
  2.2 0.7 copy-start.5
  8.4 0.9 copy-start.1
  11.3 8.2 %copy-start.2 = (bf16[32,1,4,512]{3,2,1,0:T(4,128)(2,1)S(1)}, bf16[32,1,4,512]{3,2,1,0:T(4,128)(2,1)}, u32[]{:S(2)}) copy-start(bf16[32,1,4,512]{3,2,1,0:T(4,128)(2,1)} %param.18) | copy-start | bytes 393220
  11.4 16.1 %collective-permute-start.1 = (f32[4,128,128]{2,1,0:T(8,128)S(1)}, f32[4,128,128]{2,1,0:T(8,128)S(1)}, u32[]{:S(2)}, u32[]{:S(2)}) collective-permute-start(f32[4,128,128]{2,1,0:T(8,128)S(1)} %get-tuple-element.13), channel_id=1, source_target_pairs={{0,1},{1,2},{2,3},{3,4},{4,5},{5,6},{6,7},{7,8},{8,9},{9,10},{10,1... | collective-permute-start | bytes 786440 | tf_op jit(solution)/shard_map/ppermute | solution.py:13
  14.9 14.2 %collective-permute-start = (f32[4,128,128]{2,1,0:T(8,128)S(1)}, f32[4,128,128]{2,1,0:T(8,128)S(1)}, u32[]{:S(2)}, u32[]{:S(2)}) collective-permute-start(f32[4,128,128]{2,1,0:T(8,128)S(1)} %get-tuple-element.14), channel_id=1, source_target_pairs={{0,1},{1,2},{2,3},{3,4},{4,5},{5,6},{6,7},{7,8},{8,9},{9,10},{10,1... | collective-permute-start | bytes 786440 | tf_op jit(solution)/shard_map/ppermute | solution.py:13
  18.5 0.7 copy-start.6
  19.9 0.7 copy-start.4
  22.1 0.9 copy-start
  23.0 0.9 copy-start.3
  29.7 13.5 %collective-permute-start.2 = (f32[4,128,128]{2,1,0:T(8,128)S(1)}, f32[4,128,128]{2,1,0:T(8,128)S(1)}, u32[]{:S(2)}, u32[]{:S(2)}) collective-permute-start(f32[4,128,128]{2,1,0:T(8,128)S(1)} %get-tuple-element.11), channel_id=1, source_target_pairs={{0,2},{1,3},{2,4},{3,5},{4,6},{5,7},{6,8},{7,9},{8,10},{9,11},{10,... | collective-permute-start | bytes 786440 | tf_op jit(solution)/shard_map/ppermute | solution.py:13
  33.1 13.7 %collective-permute-start.3 = (f32[4,128,128]{2,1,0:T(8,128)S(1)}, f32[4,128,128]{2,1,0:T(8,128)S(1)}, u32[]{:S(2)}, u32[]{:S(2)}) collective-permute-start(f32[4,128,128]{2,1,0:T(8,128)S(1)} %get-tuple-element.12), channel_id=1, source_target_pairs={{0,2},{1,3},{2,4},{3,5},{4,6},{5,7},{6,8},{7,9},{8,10},{9,11},{10,... | collective-permute-start | bytes 786440 | tf_op jit(solution)/shard_map/ppermute | solution.py:13
  47.5 11.0 %collective-permute-start.5 = (f32[4,128,128]{2,1,0:T(8,128)S(1)}, f32[4,128,128]{2,1,0:T(8,128)S(1)}, u32[]{:S(2)}, u32[]{:S(2)}) collective-permute-start(f32[4,128,128]{2,1,0:T(8,128)S(1)} %get-tuple-element.10), channel_id=1, source_target_pairs={{0,4},{1,5},{2,6},{3,7},{4,8},{5,9},{6,10},{7,11},{8,12},{9,13},{1... | collective-permute-start | bytes 786440 | tf_op jit(solution)/shard_map/ppermute | solution.py:13
  48.8 12.4 %collective-permute-start.4 = (f32[4,128,128]{2,1,0:T(8,128)S(1)}, f32[4,128,128]{2,1,0:T(8,128)S(1)}, u32[]{:S(2)}, u32[]{:S(2)}) collective-permute-start(f32[4,128,128]{2,1,0:T(8,128)S(1)} %get-tuple-element.9), channel_id=1, source_target_pairs={{0,4},{1,5},{2,6},{3,7},{4,8},{5,9},{6,10},{7,11},{8,12},{9,13},{1... | collective-permute-start | bytes 786440 | tf_op jit(solution)/shard_map/ppermute | solution.py:13
  58.8 9.8 %collective-permute-start.6 = (f32[4,128,128]{2,1,0:T(8,128)S(1)}, f32[4,128,128]{2,1,0:T(8,128)S(1)}, u32[]{:S(2)}, u32[]{:S(2)}) collective-permute-start(f32[4,128,128]{2,1,0:T(8,128)S(1)} %convolution_add_fusion.6), channel_id=1, source_target_pairs={{0,8},{1,9},{2,10},{3,11},{4,12},{5,13},{6,14},{7,15},{16,24},{17,... | collective-permute-start | bytes 786440 | tf_op jit(solution)/shard_map/ppermute | solution.py:13
  69.6 0.7 copy-start.8
  103.8 0.7 copy-start.9

commit v11 on v10

--- a/solution.py
+++ b/solution.py
@@ -115,7 +115,12 @@
     distance = 1
     while distance < scan_count:
         if 2 * distance < scan_count:
-            arrived = jnp.concatenate(from_behind((transfer, offset), "scan", distance), axis=-1)
+            if distance == 1:
+                arrived = from_behind(jnp.concatenate([transfer, offset], axis=-1), "scan", distance)
+            else:
+                arrived = jnp.concatenate(
+                    from_behind((transfer, offset), "scan", distance), axis=-1
+                )
             composed = matmul("bij,bjv->biv", transfer, arrived)
             if distance == 1:
                 ahead_transfer = arrived[:, :, :head_size]

time: 126 us -> 126 us (level)
  waiting for transfers between devices: 28.8 us -> 32.3 us
  starting transfers between devices: 15.9 us -> 12.5 us
    ppermute x7 -> x6, waiting for transfers between devices: 28.8 us -> 32.3 us  [from_behind(): return lax.ppermute(block, axis, route)]
    ppermute x7 -> x6, starting transfers between devices: 15.9 us -> 12.5 us  [from_behind(): return lax.ppermute(block, axis, route)]
  transfers between devices with their start and end apart: 7 -> 6, of which waited for: 6 -> 6; matrix products, arithmetic and copies ran while one was open for 6% -> 6% of each run, Pallas kernels for 0% -> 0%
where the time goes in v11:
time: 126 us
  blocking collectives  52.6 us (42%)
  waiting for transfers between devices  32.3 us (26%)
  matrix products  16.4 us (13%)
  starting transfers between devices  12.5 us (10%)
  local copies, waits for them, and re-layouts  8.49 us (7%)
  other arithmetic  2.71 us (2%)
    all_to_all x1, blocking collectives, shards(): lax.all_to_all(arranged, 'line', split_axis=1, concat_axis=0, tiled=True)  32.5 us
    ppermute x6, waiting for transfers between devices, from_behind(): return lax.ppermute(block, axis, route)  32.3 us
    all_to_all x1, blocking collectives, shards(): lax.all_to_all(normed, 'line', split_axis=0, concat_axis=1, tiled=True)  20.2 us
    dot_general x36, matrix products, matmul(): return jnp.einsum(spec, left, right, precision=HIGHEST)  16.4 us
    ppermute x6, starting transfers between devices, from_behind(): return lax.ppermute(block, axis, route)  12.5 us
    unnamed x23, local copies, waits for them, and re-layouts  5.76 us
  transfers between devices with their start and end apart: 6, of which 6 were waited for; matrix products, arithmetic and copies ran while one was open for 6% of the time, Pallas kernels for 0%

profile of v11, /device:TPU:6, one launch (start us, length us, event | category | flops | bytes accessed | tf_op | source)
XLA Modules:
  0.0 125.7 jit_solution(1595141215568692285)
XLA Ops:
  0.2 0.8 fusion.86
  1.2 0.7 copy-done.7
  1.9 0.3 reduce_window_sum.22
  2.2 0.7 copy-done.5
  2.8 0.8 fusion.4
  3.6 0.3 fusion.58
  3.9 0.4 fusion.35
  4.3 0.4 convolution_add_fusion.5
  4.7 0.4 fusion.88
  5.3 0.4 fusion.89
  5.6 0.4 convolution_add_fusion.4
  6.0 0.4 convolution_add_fusion.3
  6.4 0.4 fusion.29
  6.8 0.4 convolution_subtract_fusion.3
  7.2 0.4 fusion.27
  7.6 0.4 convolution_subtract_fusion.2
  8.1 0.4 fusion.25
  8.5 0.4 convolution_subtract_fusion.1
  8.9 0.4 copy-done.1
  9.6 0.3 broadcast_multiply_fusion
  9.9 0.6 fusion.7
  10.5 0.8 fusion.22
  11.4 3.7 %collective-permute-start = (f32[4,128,256]{2,1,0:T(8,128)S(1)}, f32[4,128,256]{2,1,0:T(8,128)S(1)}, u32[]{:S(2)}, u32[]{:S(2)}) collective-permute-start(f32[4,128,256]{2,1,0:T(8,128)S(1)} %pad_maximum_fusion), channel_id=1, source_target_pairs={{0,1},{1,2},{2,3},{3,4},{4,5},{5,6},{6,7},{7,8},{8,9},{9,10},{10,1... | collective-permute-start | bytes 1572872 | tf_op jit(solution)/shard_map/ppermute | solution.py:13
  15.2 0.6 copy-done.6
  16.5 0.7 copy-done.4
  17.2 0.7 fusion.6
  17.9 0.4 fusion.32
  18.3 0.4 convolution_add_fusion.2
  18.7 0.4 fusion.92
  19.1 0.5 copy-done
  19.6 0.9 copy-done.3
  20.6 0.4 convolution_multiply_fusion.2
  21.0 0.4 fusion.93
  21.4 0.4 convolution_add_fusion.1
  21.8 0.4 convolution_add_fusion
  22.2 0.4 fusion.19
  22.6 0.5 convolution_multiply_fusion.4
  23.1 0.4 convolution_subtract_fusion
  23.5 0.6 fusion.90
  24.1 5.0 %collective-permute-done = f32[4,128,256]{2,1,0:T(8,128)S(1)} collective-permute-done((f32[4,128,256]{2,1,0:T(8,128)S(1)}, f32[4,128,256]{2,1,0:T(8,128)S(1)}, u32[]{:S(2)}, u32[]{:S(2)}) %collective-permute-start) | collective-permute-done | bytes 524320 | tf_op jit(solution)/shard_map/ppermute | solution.py:13
  29.1 0.6 fusion.91
  29.7 3.0 %collective-permute-start.1 = (f32[4,128,128]{2,1,0:T(8,128)S(1)}, f32[4,128,128]{2,1,0:T(8,128)S(1)}, u32[]{:S(2)}, u32[]{:S(2)}) collective-permute-start(f32[4,128,128]{2,1,0:T(8,128)S(1)} %get-tuple-element.11), channel_id=1, source_target_pairs={{0,2},{1,3},{2,4},{3,5},{4,6},{5,7},{6,8},{7,9},{8,10},{9,11},{10,... | collective-permute-start | bytes 786440 | tf_op jit(solution)/shard_map/ppermute | solution.py:13
  32.7 0.4 convolution_multiply_fusion
  33.1 1.9 %collective-permute-start.2 = (f32[4,128,128]{2,1,0:T(8,128)S(1)}, f32[4,128,128]{2,1,0:T(8,128)S(1)}, u32[]{:S(2)}, u32[]{:S(2)}) collective-permute-start(f32[4,128,128]{2,1,0:T(8,128)S(1)} %get-tuple-element.12), channel_id=1, source_target_pairs={{0,2},{1,3},{2,4},{3,5},{4,6},{5,7},{6,8},{7,9},{8,10},{9,11},{10,... | collective-permute-start | bytes 786440 | tf_op jit(solution)/shard_map/ppermute | solution.py:13
  35.1 8.2 %collective-permute-done.1 = f32[4,128,128]{2,1,0:T(8,128)S(1)} collective-permute-done((f32[4,128,128]{2,1,0:T(8,128)S(1)}, f32[4,128,128]{2,1,0:T(8,128)S(1)}, u32[]{:S(2)}, u32[]{:S(2)}) %collective-permute-start.1) | collective-permute-done | bytes 262176 | tf_op jit(solution)/shard_map/ppermute | solution.py:13
  43.3 3.5 %collective-permute-done.2 = f32[4,128,128]{2,1,0:T(8,128)S(1)} collective-permute-done((f32[4,128,128]{2,1,0:T(8,128)S(1)}, f32[4,128,128]{2,1,0:T(8,128)S(1)}, u32[]{:S(2)}, u32[]{:S(2)}) %collective-permute-start.2) | collective-permute-done | bytes 262176 | tf_op jit(solution)/shard_map/ppermute | solution.py:13
  46.8 0.6 fusion.75
  47.5 1.3 %collective-permute-start.4 = (f32[4,128,128]{2,1,0:T(8,128)S(1)}, f32[4,128,128]{2,1,0:T(8,128)S(1)}, u32[]{:S(2)}, u32[]{:S(2)}) collective-permute-start(f32[4,128,128]{2,1,0:T(8,128)S(1)} %get-tuple-element.10), channel_id=1, source_target_pairs={{0,4},{1,5},{2,6},{3,7},{4,8},{5,9},{6,10},{7,11},{8,12},{9,13},{1... | collective-permute-start | bytes 786440 | tf_op jit(solution)/shard_map/ppermute | solution.py:13
  48.8 1.3 %collective-permute-start.3 = (f32[4,128,128]{2,1,0:T(8,128)S(1)}, f32[4,128,128]{2,1,0:T(8,128)S(1)}, u32[]{:S(2)}, u32[]{:S(2)}) collective-permute-start(f32[4,128,128]{2,1,0:T(8,128)S(1)} %get-tuple-element.9), channel_id=1, source_target_pairs={{0,4},{1,5},{2,6},{3,7},{4,8},{5,9},{6,10},{7,11},{8,12},{9,13},{1... | collective-permute-start | bytes 786440 | tf_op jit(solution)/shard_map/ppermute | solution.py:13
  50.1 0.6 fusion.15
  50.7 7.7 %collective-permute-done.4 = f32[4,128,128]{2,1,0:T(8,128)S(1)} collective-permute-done((f32[4,128,128]{2,1,0:T(8,128)S(1)}, f32[4,128,128]{2,1,0:T(8,128)S(1)}, u32[]{:S(2)}, u32[]{:S(2)}) %collective-permute-start.4) | collective-permute-done | bytes 262176 | tf_op jit(solution)/shard_map/ppermute | solution.py:13
  58.4 0.4 convolution_add_fusion.6
  58.9 1.3 %collective-permute-start.5 = (f32[4,128,128]{2,1,0:T(8,128)S(1)}, f32[4,128,128]{2,1,0:T(8,128)S(1)}, u32[]{:S(2)}, u32[]{:S(2)}) collective-permute-start(f32[4,128,128]{2,1,0:T(8,128)S(1)} %convolution_add_fusion.6), channel_id=1, source_target_pairs={{0,8},{1,9},{2,10},{3,11},{4,12},{5,13},{6,14},{7,15},{16,24},{17,... | collective-permute-start | bytes 786440 | tf_op jit(solution)/shard_map/ppermute | solution.py:13
  60.2 1.1 collective-permute-done.3
  61.3 0.6 fusion.13
  61.9 6.7 %collective-permute-done.5 = f32[4,128,128]{2,1,0:T(8,128)S(1)} collective-permute-done((f32[4,128,128]{2,1,0:T(8,128)S(1)}, f32[4,128,128]{2,1,0:T(8,128)S(1)}, u32[]{:S(2)}, u32[]{:S(2)}) %collective-permute-start.5) | collective-permute-done | bytes 262176 | tf_op jit(solution)/shard_map/ppermute | solution.py:13
  68.6 0.4 convolution_add_fusion.8
  69.0 0.6 multiply_reduce_fusion.2
  69.6 0.6 copy-done.8
  70.7 32.5 %all_to_all.8 = bf16[1,32,4,512]{3,2,0,1:T(4,128)(2,1)S(1)} all-to-all(bf16[1,32,4,512]{3,2,0,1:T(4,128)(2,1)S(1)} %bitcast.116), channel_id=1, replica_groups=mesh['line'=32,'scan'=16] {'line'}, dimensions={1} | all-to-all | bytes 262144 | tf_op jit(solution)/shard_map/all_to_all | solution.py:196
  103.4 0.2 fusion.94
  103.9 0.5 copy-done.9
  104.9 20.2 %all_to_all.9 = bf16[32,1,4,512]{3,2,1,0:T(4,128)(2,1)S(1)} all-to-all(bf16[32,1,4,512]{3,2,1,0:T(4,128)(2,1)S(1)} %copy.45), channel_id=1, replica_groups=mesh['line'=32,'scan'=16] {'line'}, dimensions={0} | all-to-all | bytes 262144 | tf_op jit(solution)/shard_map/all_to_all | solution.py:210
  125.0 0.7 reshape.266
  (69 shorter events, 3.2 us)
Async XLA Ops:
  1.2 0.7 copy-start.7
  2.2 0.7 copy-start.5
  8.4 0.9 copy-start.1
  11.4 4.7 %copy-start.2 = (bf16[32,1,4,512]{3,2,1,0:T(4,128)(2,1)S(1)}, bf16[32,1,4,512]{3,2,1,0:T(4,128)(2,1)}, u32[]{:S(2)}) copy-start(bf16[32,1,4,512]{3,2,1,0:T(4,128)(2,1)} %param.18) | copy-start | bytes 393220
  11.4 17.7 %collective-permute-start = (f32[4,128,256]{2,1,0:T(8,128)S(1)}, f32[4,128,256]{2,1,0:T(8,128)S(1)}, u32[]{:S(2)}, u32[]{:S(2)}) collective-permute-start(f32[4,128,256]{2,1,0:T(8,128)S(1)} %pad_maximum_fusion), channel_id=1, source_target_pairs={{0,1},{1,2},{2,3},{3,4},{4,5},{5,6},{6,7},{7,8},{8,9},{9,10},{10,1... | collective-permute-start | bytes 1572872 | tf_op jit(solution)/shard_map/ppermute | solution.py:13
  15.1 0.7 copy-start.6
  16.5 0.7 copy-start.4
  18.7 0.9 copy-start
  19.6 0.9 copy-start.3
  29.7 13.5 %collective-permute-start.1 = (f32[4,128,128]{2,1,0:T(8,128)S(1)}, f32[4,128,128]{2,1,0:T(8,128)S(1)}, u32[]{:S(2)}, u32[]{:S(2)}) collective-permute-start(f32[4,128,128]{2,1,0:T(8,128)S(1)} %get-tuple-element.11), channel_id=1, source_target_pairs={{0,2},{1,3},{2,4},{3,5},{4,6},{5,7},{6,8},{7,9},{8,10},{9,11},{10,... | collective-permute-start | bytes 786440 | tf_op jit(solution)/shard_map/ppermute | solution.py:13
  33.1 13.7 %collective-permute-start.2 = (f32[4,128,128]{2,1,0:T(8,128)S(1)}, f32[4,128,128]{2,1,0:T(8,128)S(1)}, u32[]{:S(2)}, u32[]{:S(2)}) collective-permute-start(f32[4,128,128]{2,1,0:T(8,128)S(1)} %get-tuple-element.12), channel_id=1, source_target_pairs={{0,2},{1,3},{2,4},{3,5},{4,6},{5,7},{6,8},{7,9},{8,10},{9,11},{10,... | collective-permute-start | bytes 786440 | tf_op jit(solution)/shard_map/ppermute | solution.py:13
  47.5 11.0 %collective-permute-start.4 = (f32[4,128,128]{2,1,0:T(8,128)S(1)}, f32[4,128,128]{2,1,0:T(8,128)S(1)}, u32[]{:S(2)}, u32[]{:S(2)}) collective-permute-start(f32[4,128,128]{2,1,0:T(8,128)S(1)} %get-tuple-element.10), channel_id=1, source_target_pairs={{0,4},{1,5},{2,6},{3,7},{4,8},{5,9},{6,10},{7,11},{8,12},{9,13},{1... | collective-permute-start | bytes 786440 | tf_op jit(solution)/shard_map/ppermute | solution.py:13
  48.8 12.4 %collective-permute-start.3 = (f32[4,128,128]{2,1,0:T(8,128)S(1)}, f32[4,128,128]{2,1,0:T(8,128)S(1)}, u32[]{:S(2)}, u32[]{:S(2)}) collective-permute-start(f32[4,128,128]{2,1,0:T(8,128)S(1)} %get-tuple-element.9), channel_id=1, source_target_pairs={{0,4},{1,5},{2,6},{3,7},{4,8},{5,9},{6,10},{7,11},{8,12},{9,13},{1... | collective-permute-start | bytes 786440 | tf_op jit(solution)/shard_map/ppermute | solution.py:13
  58.9 9.8 %collective-permute-start.5 = (f32[4,128,128]{2,1,0:T(8,128)S(1)}, f32[4,128,128]{2,1,0:T(8,128)S(1)}, u32[]{:S(2)}, u32[]{:S(2)}) collective-permute-start(f32[4,128,128]{2,1,0:T(8,128)S(1)} %convolution_add_fusion.6), channel_id=1, source_target_pairs={{0,8},{1,9},{2,10},{3,11},{4,12},{5,13},{6,14},{7,15},{16,24},{17,... | collective-permute-start | bytes 786440 | tf_op jit(solution)/shard_map/ppermute | solution.py:13
  69.6 0.7 copy-start.8
  103.8 0.7 copy-start.9
